TPU v7x, 32 devices: a whole 2x2x4 slice. The times are simulated.
32 devices in a mesh: mem: 8 (over z, y), head: 4 (over x, core).
Axes of the slice: x: 2, y: 2, z: 4, core: 2. Of those that a mesh axis runs over, the one named last changes fastest.
Arguments:
- queries: bfloat16 [4096, 2048], P('mem', 'head'), may hold values from -8 to 8
- local_keys: bfloat16 [4096, 2048], P('mem', 'head'), may hold values from -8 to 8
- local_values: bfloat16 [4096, 2048], P('mem', 'head'), may hold values from -8 to 8
- memory_keys: bfloat16 [128, 32, 2048], P('mem', None, 'head'), may hold values from -8 to 8
- memory_values: bfloat16 [128, 32, 2048], P('mem', None, 'head'), may hold values from -8 to 8
- retrieval: int32 [8, 32], replicated, may hold values from 0 to 127, as said below
- gate_logit: float32 [16], P('head'), may hold values from -4 to 4
- dropout_keep: int32 [4096, 2048], P('mem', 'head'), may hold values 0 or 1
- out_weight: bfloat16 [2048, 2048], P('head'), may hold values from -0.125 to 0.125
- cotangent: bfloat16 [4096, 2048], P('mem', 'head'), may hold values from -6 to 6
Outputs:
- layer_out: bfloat16 [4096, 2048], P('mem', 'head')
- grad_queries: bfloat16 [4096, 2048], P('mem', 'head')
- grad_keys: bfloat16 [4096, 2048], P('mem', 'head')
- grad_values: bfloat16 [4096, 2048], P('mem', 'head')
- grad_memory_keys: bfloat16 [128, 32, 2048], P('mem', None, 'head')
- grad_memory_values: bfloat16 [128, 32, 2048], P('mem', None, 'head')
Inputs may be any that keep to these rules, and one draw needn't show every extreme that they name: `retrieval`: block i lies on shard i // 16. Rows d * 1 to (d + 1) - 1 belong to index d of mem; together they name 32 distinct blocks, at most 8 of them on any one shard, and in every draw one shard receives exactly 8 from the rows of every index.
All inputs are finite; a program needn't handle non-finite values. No bound on the sum of `dropout_keep` on one device may be relied on, other than what follows from the above.
Results may differ from a plain program's by a relative error of at most 0.0079.
Values may be sent and summed in bfloat16 or wider, within the bound.
No kernel may reach another device: no remote copies, remote signals or barrier semaphores. Data moves between devices by JAX's collectives and lax.ppermute only.
A program may use at most 128 MiB of HBM per device.

v0:
```python
import jax
import jax.numpy as jnp
from jax import lax
from jax.sharding import PartitionSpec as P

QBLK = 512


keep_scale = 1.0 / 0.9


def contract_last(left, right):
    return lax.dot_general(
        left, right, (((1,), (1,)), ((), ())), preferred_element_type=jnp.float32
    )


def contract_first(left, right):
    return lax.dot_general(
        left, right, (((0,), (0,)), ((), ())), preferred_element_type=jnp.float32
    )


def branch_weights(query_rows, keyset, causal):
    score_scale = query_rows.shape[1] ** (-0.5)
    scores = contract_last(query_rows, keyset) * score_scale
    if causal:
        row_iota = lax.broadcasted_iota(jnp.int32, scores.shape, 0)
        col_iota = lax.broadcasted_iota(jnp.int32, scores.shape, 1)
        scores = jnp.where(col_iota <= row_iota, scores, -jnp.inf)
    return jnp.exp(scores - jnp.max(scores, axis=1, keepdims=True))


def branch_forward(query_rows, keyset, valueset, causal):
    weights = branch_weights(query_rows, keyset, causal)
    row_total = jnp.sum(weights, axis=1, keepdims=True)
    mixed_out = (
        jnp.dot(weights.astype(jnp.bfloat16), valueset, preferred_element_type=jnp.float32)
        / row_total
    )
    return (mixed_out, row_total)


def branch_backward(query_rows, keyset, valueset, row_total, mixed_out, grad_mixed, causal):
    weights = branch_weights(query_rows, keyset, causal)
    probabilities = weights / row_total
    delta_rows = jnp.sum(grad_mixed * mixed_out, axis=1, keepdims=True)
    grad_low = grad_mixed.astype(jnp.bfloat16)
    grad_probs = contract_last(grad_low, valueset)
    score_scale = query_rows.shape[1] ** (-0.5)
    grad_scores = (probabilities * (grad_probs - delta_rows) * score_scale).astype(jnp.bfloat16)
    grad_query = jnp.dot(grad_scores, keyset, preferred_element_type=jnp.float32)
    grad_keyset = contract_first(grad_scores, query_rows)
    grad_valueset = contract_first(probabilities.astype(jnp.bfloat16), grad_low)
    return (grad_query, grad_keyset, grad_valueset)


def per_device(
    queries,
    local_keys,
    local_values,
    memory_keys,
    memory_values,
    retrieval,
    gate_logit,
    dropout_keep,
    out_weight,
    cotangent,
):
    mem_count = lax.axis_size("mem")
    mem_index = lax.axis_index("mem")
    tok_rows, feature_cols = queries.shape
    heads_here = gate_logit.shape[0]
    head_dim = feature_cols // heads_here
    blocks_here = memory_keys.shape[0]
    block_len = memory_keys.shape[1]
    query_blocks = tok_rows // QBLK
    top_blocks = retrieval.shape[1]
    request_count = query_blocks * top_blocks
    capacity = 2 * request_count // mem_count
    slot_count = mem_count * capacity
    entries = block_len * feature_cols
    owner_ids = retrieval // blocks_here
    local_ids = retrieval % blocks_here
    earlier_mask = lax.broadcasted_iota(
        jnp.int32, (request_count, request_count), 0
    ) < lax.broadcasted_iota(jnp.int32, (request_count, request_count), 1)
    same_owner = owner_ids[:, :, None] == owner_ids[:, None, :]
    owner_rank = jnp.sum((same_owner & earlier_mask[None]).astype(jnp.int32), axis=1)
    request_owner = lax.dynamic_index_in_dim(owner_ids, mem_index, 0, keepdims=False)
    request_rank = lax.dynamic_index_in_dim(owner_rank, mem_index, 0, keepdims=False)
    request_slot = request_owner * capacity + request_rank
    slot_iota = lax.broadcasted_iota(jnp.int32, (request_count, slot_count), 1)
    pick_table = (request_slot[:, None] == slot_iota).astype(jnp.bfloat16)
    cap_iota = lax.broadcasted_iota(jnp.int32, (mem_count, request_count, capacity), 2)
    wanted = (owner_ids[:, :, None] == mem_index) & (owner_rank[:, :, None] == cap_iota)
    send_local = jnp.sum(wanted.astype(jnp.int32) * (local_ids[:, :, None] + 1), axis=1) - 1
    block_iota = lax.broadcasted_iota(jnp.int32, (slot_count, blocks_here), 1)
    serve_table = (send_local.reshape(slot_count, 1) == block_iota).astype(jnp.bfloat16)

    def outgoing(table):
        flat_rows = table.reshape(blocks_here, entries)
        served = jnp.dot(serve_table, flat_rows, preferred_element_type=jnp.float32)
        return served.astype(jnp.bfloat16).reshape(mem_count, capacity, block_len, feature_cols)

    def selected(blocks):
        flat_rows = blocks.reshape(slot_count, entries)
        chosen = jnp.dot(pick_table, flat_rows, preferred_element_type=jnp.float32)
        return chosen.astype(jnp.bfloat16).reshape(top_blocks * block_len, feature_cols)

    fetched = (
        lax.all_to_all(outgoing(memory_keys), "mem", split_axis=0, concat_axis=0, tiled=True),
        lax.all_to_all(outgoing(memory_values), "mem", split_axis=0, concat_axis=0, tiled=True),
    )
    gate_values = 1.0 / (1.0 + jnp.exp(-gate_logit))
    keep_mask = dropout_keep.astype(jnp.float32)
    saved_state = []
    block_index = 0
    row_start = block_index * QBLK
    row_stop = row_start + QBLK
    mem_keyset = selected(fetched[0])
    mem_valueset = selected(fetched[1])
    head_parts = []
    for head_index in range(heads_here):
        col_start = head_index * head_dim
        col_stop = col_start + head_dim
        query_rows = queries[row_start:row_stop, col_start:col_stop]
        mixed_loc, total_loc = branch_forward(
            query_rows,
            local_keys[row_start:row_stop, col_start:col_stop],
            local_values[row_start:row_stop, col_start:col_stop],
            True,
        )
        mixed_mem, total_mem = branch_forward(
            query_rows,
            mem_keyset[:, col_start:col_stop],
            mem_valueset[:, col_start:col_stop],
            False,
        )
        saved_state.append((mixed_loc, total_loc, mixed_mem, total_mem))
        head_parts.append(
            gate_values[head_index] * mixed_mem + (1.0 - gate_values[head_index]) * mixed_loc
        )
    attended_parts = jnp.concatenate(head_parts, axis=1)
    dropped = (attended_parts * keep_mask * keep_scale).astype(jnp.bfloat16)
    partial_out = jnp.dot(dropped, out_weight, preferred_element_type=jnp.float32)
    layer_out = lax.psum_scatter(partial_out, "head", scatter_dimension=1, tiled=True).astype(
        jnp.bfloat16
    )
    cotangent_full = lax.all_gather(cotangent, "head", axis=1, tiled=True)
    grad_attended = contract_last(cotangent_full, out_weight) * keep_mask * keep_scale
    query_grads, key_grads, value_grads, memkey_parts, memvalue_parts = ([], [], [], [], [])
    block_index = 0
    row_start = block_index * QBLK
    row_stop = row_start + QBLK
    mem_keyset = selected(fetched[0])
    mem_valueset = selected(fetched[1])
    head_query = []
    head_key = []
    head_value = []
    head_memkey = []
    head_memvalue = []
    for head_index in range(heads_here):
        col_start = head_index * head_dim
        col_stop = col_start + head_dim
        mixed_loc, total_loc, mixed_mem, total_mem = saved_state[
            block_index * heads_here + head_index
        ]
        query_rows = queries[row_start:row_stop, col_start:col_stop]
        grad_here = grad_attended[row_start:row_stop, col_start:col_stop]
        query_mem, keyset_mem, valueset_mem = branch_backward(
            query_rows,
            mem_keyset[:, col_start:col_stop],
            mem_valueset[:, col_start:col_stop],
            total_mem,
            mixed_mem,
            gate_values[head_index] * grad_here,
            False,
        )
        query_loc, keyset_loc, valueset_loc = branch_backward(
            query_rows,
            local_keys[row_start:row_stop, col_start:col_stop],
            local_values[row_start:row_stop, col_start:col_stop],
            total_loc,
            mixed_loc,
            (1.0 - gate_values[head_index]) * grad_here,
            True,
        )
        head_query.append((query_mem + query_loc).astype(jnp.bfloat16))
        head_key.append(keyset_loc.astype(jnp.bfloat16))
        head_value.append(valueset_loc.astype(jnp.bfloat16))
        head_memkey.append(keyset_mem.astype(jnp.bfloat16))
        head_memvalue.append(valueset_mem.astype(jnp.bfloat16))
    query_grads.append(jnp.concatenate(head_query, axis=1))
    key_grads.append(jnp.concatenate(head_key, axis=1))
    value_grads.append(jnp.concatenate(head_value, axis=1))
    memkey_parts.append(jnp.concatenate(head_memkey, axis=1).reshape(top_blocks, entries))
    memvalue_parts.append(jnp.concatenate(head_memvalue, axis=1).reshape(top_blocks, entries))
    send_keys = contract_first(pick_table, memkey_parts[0]).astype(jnp.bfloat16)
    send_values = contract_first(pick_table, memvalue_parts[0]).astype(jnp.bfloat16)
    returned = (
        lax.all_to_all(
            send_keys.reshape(mem_count, capacity, block_len, feature_cols),
            "mem",
            split_axis=0,
            concat_axis=0,
            tiled=True,
        ),
        lax.all_to_all(
            send_values.reshape(mem_count, capacity, block_len, feature_cols),
            "mem",
            split_axis=0,
            concat_axis=0,
            tiled=True,
        ),
    )
    grad_memory_keys = contract_first(serve_table, returned[0].reshape(slot_count, entries)).astype(
        jnp.bfloat16
    )
    grad_memory_values = contract_first(
        serve_table, returned[1].reshape(slot_count, entries)
    ).astype(jnp.bfloat16)
    return (
        layer_out,
        query_grads[0],
        key_grads[0],
        value_grads[0],
        grad_memory_keys.reshape(blocks_here, block_len, feature_cols),
        grad_memory_values.reshape(blocks_here, block_len, feature_cols),
    )


def solution(mesh):
    placed = (
        P("mem", "head"),
        P("mem", "head"),
        P("mem", "head"),
        P("mem", None, "head"),
        P("mem", None, "head"),
        P(),
        P("head"),
        P("mem", "head"),
        P("head", None),
        P("mem", "head"),
    )
    return jax.shard_map(
        per_device,
        mesh=mesh,
        in_specs=placed,
        out_specs=(
            P("mem", "head"),
            P("mem", "head"),
            P("mem", "head"),
            P("mem", "head"),
            P("mem", None, "head"),
            P("mem", None, "head"),
        ),
        check_vma=False,
    )
```

profile of v0, /device:TPU:0, one launch (start us, length us, event | category | flops | bytes accessed | tf_op | source)
XLA Modules:
  0.0 273.9 jit_solution(1934526136832263948)
XLA Ops:
  12.6 7.4 %all-to-all-start = ((bf16[8,8,32,512]{3,1,2,0:T(8,128)(2,1)}), bf16[8,8,32,512]{3,1,2,0:T(8,128)(2,1)}, u32[]{:S(2)}, u32[]{:S(2)}) async-start(bf16[8,8,32,512]{3,1,2,0:T(8,128)(2,1)} %bitcast.85), calls=%async_computation | async-start | bytes 4194304 | tf_op jit(solution)/shard_map/all_to_all | solution.py:112
  27.8 2.1 convolution_convert_fusion.2
  29.9 38.5 %all-to-all-done = bf16[8,8,32,512]{3,1,2,0:T(8,128)(2,1)} async-done(((bf16[8,8,32,512]{3,1,2,0:T(8,128)(2,1)}), bf16[8,8,32,512]{3,1,2,0:T(8,128)(2,1)}, u32[]{:S(2)}, u32[]{:S(2)}) %all-to-all-start) | async-done | bytes 2097184 | tf_op jit(solution)/shard_map/all_to_all | solution.py:112
  68.4 4.3 %all-to-all-start.1 = ((bf16[8,8,32,512]{3,1,2,0:T(8,128)(2,1)}), bf16[8,8,32,512]{3,1,2,0:T(8,128)(2,1)}, u32[]{:S(2)}, u32[]{:S(2)}) async-start(bf16[8,8,32,512]{3,1,2,0:T(8,128)(2,1)} %bitcast.84), calls=%async_computation.1 | async-start | bytes 4194304 | tf_op jit(solution)/shard_map/all_to_all | solution.py:113
  75.2 2.5 copy.42
  85.4 3.0 %fusion.8 = f32[512,512]{0,1:T(8,128)S(1)} fusion(bf16[512,2048]{1,0:T(8,128)(2,1)} %all-gather.2.cloned.1.call-done, bf16[512,2048]{1,0:T(8,128)(2,1)S(1)} %copy-done, s32[512,512]{0,1:T(8,128)S(1)} %copy-done.21), kind=kOutput, calls=%fused_computation.37 | convolution fusion | flops 1074528256 | bytes 6291456 | tf_op jit(solution)/shard_map/dot_general | solution.py:13
  89.4 3.1 %convolution_convert_fusion.5 = bf16[32,16384]{1,0:T(8,128)(2,1)} fusion(bf16[64,16384]{1,0:T(8,128)(2,1)} %bitcast.3, s32[32]{0:T(128)S(1)} %add_bitcast_fusion), kind=kOutput, calls=%fused_computation.5 | convolution fusion | flops 67635200 | bytes 3145856 | tf_op jit(solution)/shard_map/dot_general | solution.py:108
  94.0 2.7 multiply_reduce_fusion
  102.1 18.4 %all-to-all-done.1 = bf16[8,8,32,512]{3,1,2,0:T(8,128)(2,1)} async-done(((bf16[8,8,32,512]{3,1,2,0:T(8,128)(2,1)}), bf16[8,8,32,512]{3,1,2,0:T(8,128)(2,1)}, u32[]{:S(2)}, u32[]{:S(2)}) %all-to-all-start.1) | async-done | bytes 2097184 | tf_op jit(solution)/shard_map/all_to_all | solution.py:113
  120.5 3.1 %convolution_convert_fusion.4 = bf16[32,16384]{1,0:T(8,128)(2,1)} fusion(bf16[64,16384]{1,0:T(8,128)(2,1)} %bitcast.5, s32[32]{0:T(128)S(1)} %add_bitcast_fusion), kind=kOutput, calls=%fused_computation.4 | convolution fusion | flops 67635200 | bytes 3145856 | tf_op jit(solution)/shard_map/dot_general | solution.py:108
  123.6 2.3 reshape.130
  125.9 2.1 fusion.31
  132.0 3.3 %multiply_reduce_fusion.10 = (f32[512]{0:T(512)}, f32[512]{0:T(512)}, f32[512]{0:T(512)S(1)}, f32[512]{0:T(512)}, f32[512]{0:T(512)S(1)}, /*index=5*/f32[512]{0:...) fusion(f32[512,512]{0,1:T(8,128)S(1)} %copy-done.76, f32[]{:T(128)S(6)} %sub.91, ...), kind=kOutput, calls=%fused_computation.151 | convolution fusion | flops 69268480 | bytes 4342800 | tf_op jit(solution)/shard_map/dot_general | solution.py:38
  149.2 3.4 %fusion.71 = f32[512,2048]{1,0:T(8,128)} fusion(bf16[512,2048]{1,0:T(8,128)(2,1)S(1)} %copy-done, f32[512,128]{0,1:T(8,128)S(1)} %get-tuple-element.35, f32[512,128]{0,1:T(8,128)S(1)} %get-tuple-element.34, f32[512,128]{0,1:T(8,128)S(1)} %get-tuple-element.36, f32[512,128]{0,1:T(8,128)S(1)} %get-tuple-element.37, s32[512,512]{0,1:T(8,128)S(1)} %copy-done.22), kind=kOutput, calls=%fused_computation.132 | convolution fusion | flops 1075576832 | bytes 8388608 | tf_op jit(solution)/shard_map/dot_general | solution.py:146
  155.1 2.2 convolution_convert_fusion.1
  157.3 3.8 %all-to-all-start.2 = ((bf16[8,8,32,512]{3,1,2,0:T(8,128)(2,1)}), bf16[8,8,32,512]{3,1,2,0:T(8,128)(2,1)S(1)}, u32[]{:S(2)}, u32[]{:S(2)}) async-start(bf16[8,8,32,512]{3,1,2,0:T(8,128)(2,1)} %bitcast.83), calls=%async_computation.3 | async-start | bytes 4194304 | tf_op jit(solution)/shard_map/all_to_all | solution.py:202
  167.9 3.3 %convolution_convert_fusion.8 = bf16[1024,128]{0,1:T(8,128)(2,1)S(1)} fusion(f32[1024,512]{1,0:T(8,128)} %get-tuple-element.47, f32[512]{0:T(512)S(1)} %copy-done.68, f32[512]{0:T(512)S(1)} %copy-done.48, f32[512,512]{0,1:T(8,128)} %copy-done.75, f32[]{:T(128)} %bitcast.8), kind=kOutput, calls=%fused_computation.70 | convolution fusion | flops 136577024 | bytes 2626048 | tf_op jit(solution)/shard_map/dot_general | solution.py:19
  176.7 2.3 copy.52
  179.0 2.3 reshape.135
  184.6 2.3 fusion.33
  189.0 20.5 %all-to-all-done.2 = bf16[8,8,32,512]{3,1,2,0:T(8,128)(2,1)S(1)} async-done(((bf16[8,8,32,512]{3,1,2,0:T(8,128)(2,1)}), bf16[8,8,32,512]{3,1,2,0:T(8,128)(2,1)S(1)}, u32[]{:S(2)}, u32[]{:S(2)}) %all-to-all-start.2) | async-done | bytes 2097184 | tf_op jit(solution)/shard_map/all_to_all | solution.py:202
  209.5 4.5 %all-to-all-start.3 = ((bf16[8,8,32,512]{3,1,2,0:T(8,128)(2,1)}), bf16[8,8,32,512]{3,1,2,0:T(8,128)(2,1)}, u32[]{:S(2)}, u32[]{:S(2)}) async-start(bf16[8,8,32,512]{3,1,2,0:T(8,128)(2,1)} %bitcast.82), calls=%async_computation.4 | async-start | bytes 4194304 | tf_op jit(solution)/shard_map/all_to_all | solution.py:209
  230.7 31.1 %all-to-all-done.3 = bf16[8,8,32,512]{3,1,2,0:T(8,128)(2,1)} async-done(((bf16[8,8,32,512]{3,1,2,0:T(8,128)(2,1)}), bf16[8,8,32,512]{3,1,2,0:T(8,128)(2,1)}, u32[]{:S(2)}, u32[]{:S(2)}) %all-to-all-start.3) | async-done | bytes 2097184 | tf_op jit(solution)/shard_map/all_to_all | solution.py:209
  261.8 2.2 convolution_convert_fusion.6
  (258 shorter events, 85.4 us)
Async XLA Ops:
  7.2 78.2 %copy-start = (bf16[512,2048]{1,0:T(8,128)(2,1)S(1)}, bf16[512,2048]{1,0:T(8,128)(2,1)}, u32[]{:S(2)}) copy-start(bf16[512,2048]{1,0:T(8,128)(2,1)} %param.18) | copy-start | bytes 6291460
  12.6 9.5 %copy-start.74 = (f32[4]{0:T(128)S(1)}, f32[4]{0:T(128)}, u32[]{:S(2)}) copy-start(f32[4]{0:T(128)} %param.16) | copy-start | bytes 52
  12.6 10.2 %copy-start.9 = (bf16[512,512]{1,0:T(8,128)(2,1)S(1)}, bf16[512,512]{1,0:T(8,128)(2,1)}, u32[]{:S(2)}) copy-start(bf16[512,512]{1,0:T(8,128)(2,1)} %param.10) | copy-start | bytes 1572868
  12.6 55.8 %all-to-all-start = ((bf16[8,8,32,512]{3,1,2,0:T(8,128)(2,1)}), bf16[8,8,32,512]{3,1,2,0:T(8,128)(2,1)}, u32[]{:S(2)}, u32[]{:S(2)}) async-start(bf16[8,8,32,512]{3,1,2,0:T(8,128)(2,1)} %bitcast.85), calls=%async_computation | async-start | bytes 4194304 | tf_op jit(solution)/shard_map/all_to_all | solution.py:112
  20.0 65.4 %all-gather.2.cloned.1.call-start = ((), (), s32[]{:S(2)}) async-start(), calls=%async_computation.6 | async-start | bytes 2621440 | tf_op jit(solution)/shard_map/all_gather | solution.py:150
  24.0 64.3 %copy-start.49 = (f32[512]{0:T(512)}, f32[512]{0:T(512)S(1)}, u32[]{:S(2)}) copy-start(f32[512]{0:T(512)S(1)} %get-tuple-element.52) | copy-start | bytes 6148
  25.2 63.2 %copy-start.51 = (f32[512]{0:T(512)}, f32[512]{0:T(512)S(1)}, u32[]{:S(2)}) copy-start(f32[512]{0:T(512)S(1)} %fusion.59) | copy-start | bytes 6148
  26.5 104.4 %copy-start.55 = (f32[512]{0:T(512)}, f32[512]{0:T(512)S(1)}, u32[]{:S(2)}) copy-start(f32[512]{0:T(512)S(1)} %get-tuple-element.42) | copy-start | bytes 6148
  27.8 55.5 %copy-start.53 = (f32[512]{0:T(512)}, f32[512]{0:T(512)S(1)}, u32[]{:S(2)}) copy-start(f32[512]{0:T(512)S(1)} %get-tuple-element.44) | copy-start | bytes 6148
  68.4 52.2 %all-to-all-start.1 = ((bf16[8,8,32,512]{3,1,2,0:T(8,128)(2,1)}), bf16[8,8,32,512]{3,1,2,0:T(8,128)(2,1)}, u32[]{:S(2)}, u32[]{:S(2)}) async-start(bf16[8,8,32,512]{3,1,2,0:T(8,128)(2,1)} %bitcast.84), calls=%async_computation.1 | async-start | bytes 4194304 | tf_op jit(solution)/shard_map/all_to_all | solution.py:113
  72.7 192.3 %reduce-scatter.2.cloned.1.call-start = ((), (), s32[]{:S(2)}) async-start(), calls=%async_computation.5 | async-start | bytes 5242880 | tf_op jit(solution)/shard_map/reduce_scatter | solution.py:147
  77.7 4.5 %copy-start.30 = (f32[512,512]{0,1:T(8,128)S(1)}, f32[512,512]{0,1:T(8,128)}, u32[]{:S(2)}) copy-start(f32[512,512]{0,1:T(8,128)} %copy-done.29) | copy-start | bytes 3145732
  77.7 4.5 %copy-start.73 = (bf16[512,512]{1,0:T(8,128)(2,1)S(1)}, bf16[512,512]{1,0:T(8,128)(2,1)}, u32[]{:S(2)}) copy-start(bf16[512,512]{1,0:T(8,128)(2,1)} %param.12) | copy-start | bytes 1572868
  79.3 51.6 %copy-start.63 = (f32[512]{0:T(512)}, f32[512]{0:T(512)S(1)}, u32[]{:S(2)}) copy-start(f32[512]{0:T(512)S(1)} %fusion.56) | copy-start | bytes 6148
  96.7 39.9 %copy-start.47 = (f32[512]{0:T(512)}, f32[512]{0:T(512)S(1)}, u32[]{:S(2)}) copy-start(f32[512]{0:T(512)S(1)} %get-tuple-element.46) | copy-start | bytes 6148
  98.6 36.8 %copy-start.45 = (f32[512]{0:T(512)}, f32[512]{0:T(512)S(1)}, u32[]{:S(2)}) copy-start(f32[512]{0:T(512)S(1)} %get-tuple-element.50) | copy-start | bytes 6148
  128.2 8.5 %copy-start.67 = (f32[512]{0:T(512)}, f32[512]{0:T(512)S(1)}, u32[]{:S(2)}) copy-start(f32[512]{0:T(512)S(1)} %fusion.31) | copy-start | bytes 6148
  130.2 5.1 %copy-start.65 = (f32[512]{0:T(512)}, f32[512]{0:T(512)S(1)}, u32[]{:S(2)}) copy-start(f32[512]{0:T(512)S(1)} %fusion.28) | copy-start | bytes 6148
  157.3 3.9 %copy-start.64 = (f32[512]{0:T(512)S(1)}, f32[512]{0:T(512)}, u32[]{:S(2)}) copy-start(f32[512]{0:T(512)} %copy-done.63) | copy-start | bytes 6148
  157.3 52.2 %all-to-all-start.2 = ((bf16[8,8,32,512]{3,1,2,0:T(8,128)(2,1)}), bf16[8,8,32,512]{3,1,2,0:T(8,128)(2,1)S(1)}, u32[]{:S(2)}, u32[]{:S(2)}) async-start(bf16[8,8,32,512]{3,1,2,0:T(8,128)(2,1)} %bitcast.83), calls=%async_computation.3 | async-start | bytes 4194304 | tf_op jit(solution)/shard_map/all_to_all | solution.py:202
  176.7 4.6 %copy-start.85 = (f32[512]{0:T(512)S(1)}, f32[512]{0:T(512)}, u32[]{:S(2)}) copy-start(f32[512]{0:T(512)} %get-tuple-element.24) | copy-start | bytes 6148
  209.5 5.9 %copy-start.83 = (f32[512]{0:T(512)S(1)}, f32[512]{0:T(512)}, u32[]{:S(2)}) copy-start(f32[512]{0:T(512)} %get-tuple-element.27) | copy-start | bytes 6148
  209.5 52.3 %all-to-all-start.3 = ((bf16[8,8,32,512]{3,1,2,0:T(8,128)(2,1)}), bf16[8,8,32,512]{3,1,2,0:T(8,128)(2,1)}, u32[]{:S(2)}, u32[]{:S(2)}) async-start(bf16[8,8,32,512]{3,1,2,0:T(8,128)(2,1)} %bitcast.82), calls=%async_computation.4 | async-start | bytes 4194304 | tf_op jit(solution)/shard_map/all_to_all | solution.py:209
  261.8 5.3 %copy-start.1 = (bf16[512,2048]{1,0:T(8,128)(2,1)S(1)}, bf16[512,2048]{1,0:T(8,128)(2,1)}, u32[]{:S(2)}) copy-start(bf16[512,2048]{1,0:T(8,128)(2,1)} %param.18) | copy-start | bytes 6291460
  (68 other events, 145.5 us)
Sparse Core Ops, SparseCore 0:
  22.4 23.9 all-gather.1
  152.8 43.4 reduce-scatter.1
where the time goes:
time: 276 us; the launch traced here: 274 us
  waiting for transfers between devices  109 us (39%)
  matrix products  82.7 us (30%)
  local copies, waits for them, and re-layouts  30.8 us (11%)
  starting transfers between devices  20.2 us (7%)
  between operations  17.6 us (6%)
  other arithmetic  13.5 us (5%)
    all_to_all x1, waiting for transfers between devices, per_device(): lax.all_to_all(outgoing(memory_keys), 'mem', split_axis=0, concat_axis=0,...  38.5 us
    all_to_all x1, waiting for transfers between devices, per_device(): lax.all_to_all(send_values.reshape(mem_count, capacity, block_len, featur...  31.1 us
    dot_general x17, matrix products, contract_last(): lax.dot_general(left, right, (((1,), (1,)), ((), ())), preferred_element_...  28.6 us
    dot_general x20, matrix products, contract_first(): lax.dot_general(left, right, (((0,), (0,)), ((), ())), preferred_element_...  24.6 us
    all_to_all x1, waiting for transfers between devices, per_device(): lax.all_to_all(send_keys.reshape(mem_count, capacity, block_len, feature_...  20.5 us
    unnamed x180, local copies, waits for them, and re-layouts  20.2 us
    all_to_all x1, waiting for transfers between devices, per_device(): lax.all_to_all(outgoing(memory_values), 'mem', split_axis=0, concat_axis=...  18.4 us
    dot_general x8, matrix products, branch_forward(): jnp.dot(weights.astype(jnp.bfloat16), valueset, preferred_element_type=jn...  10.8 us
  transfers between devices with their start and end apart: 6, of which 4 were waited for; matrix products, arithmetic and copies ran while one was open for 30% of the time, Pallas kernels for 0%

commit v1 on v0

v1 whole, which is shorter than its diff:
```python
import jax
import jax.numpy as jnp
from jax import lax
from jax.sharding import PartitionSpec as P

QBLK = 512


keep_scale = 1.0 / 0.9


def mm(spec, left, right):
    return jnp.einsum(spec, left, right, preferred_element_type=jnp.float32)


def branch(query_rows, keyset, valueset, grad_mixed, causal, score_scale):
    scores = mm("thd,khd->htk", query_rows, keyset) * score_scale
    if causal:
        row_iota = lax.broadcasted_iota(jnp.int32, scores.shape, 1)
        col_iota = lax.broadcasted_iota(jnp.int32, scores.shape, 2)
        scores = jnp.where(col_iota <= row_iota, scores, -jnp.inf)
    weights = jnp.exp(scores - jnp.max(scores, axis=2, keepdims=True))
    row_total = jnp.sum(weights, axis=2, keepdims=True)
    mixed_out = mm("htk,khd->htd", weights.astype(jnp.bfloat16), valueset) / row_total
    return weights, row_total, mixed_out


def branch_grads(query_rows, keyset, valueset, weights, row_total, mixed_out, grad_mixed, score_scale):
    probabilities = weights / row_total
    delta_rows = jnp.sum(grad_mixed * mixed_out, axis=2, keepdims=True)
    grad_low = grad_mixed.astype(jnp.bfloat16)
    grad_probs = mm("htd,khd->htk", grad_low, valueset)
    grad_scores = (probabilities * (grad_probs - delta_rows) * score_scale).astype(jnp.bfloat16)
    grad_query = mm("htk,khd->thd", grad_scores, keyset)
    grad_keyset = mm("htk,thd->khd", grad_scores, query_rows)
    grad_valueset = mm("htk,htd->khd", probabilities.astype(jnp.bfloat16), grad_low)
    return grad_query, grad_keyset, grad_valueset


def per_device(
    queries,
    local_keys,
    local_values,
    memory_keys,
    memory_values,
    retrieval,
    gate_logit,
    dropout_keep,
    out_weight,
    cotangent,
):
    mem_count = lax.axis_size("mem")
    mem_index = lax.axis_index("mem")
    tok_rows, feature_cols = queries.shape
    heads_here = gate_logit.shape[0]
    head_dim = feature_cols // heads_here
    score_scale = head_dim ** (-0.5)
    blocks_here = memory_keys.shape[0]
    block_len = memory_keys.shape[1]
    query_blocks = tok_rows // QBLK
    top_blocks = retrieval.shape[1]
    request_count = query_blocks * top_blocks
    capacity = 2 * request_count // mem_count
    slot_count = mem_count * capacity
    owner_ids = retrieval // blocks_here
    local_ids = retrieval % blocks_here
    earlier_mask = lax.broadcasted_iota(
        jnp.int32, (request_count, request_count), 0
    ) < lax.broadcasted_iota(jnp.int32, (request_count, request_count), 1)
    same_owner = owner_ids[:, :, None] == owner_ids[:, None, :]
    owner_rank = jnp.sum((same_owner & earlier_mask[None]).astype(jnp.int32), axis=1)
    request_owner = lax.dynamic_index_in_dim(owner_ids, mem_index, 0, keepdims=False)
    request_rank = lax.dynamic_index_in_dim(owner_rank, mem_index, 0, keepdims=False)
    request_slot = request_owner * capacity + request_rank
    slot_iota = lax.broadcasted_iota(jnp.int32, (request_count, slot_count), 1)
    pick_table = (request_slot[:, None] == slot_iota).astype(jnp.bfloat16)
    cap_iota = lax.broadcasted_iota(jnp.int32, (mem_count, request_count, capacity), 2)
    wanted = (owner_ids[:, :, None] == mem_index) & (owner_rank[:, :, None] == cap_iota)
    send_local = jnp.sum(wanted.astype(jnp.int32) * (local_ids[:, :, None] + 1), axis=1) - 1
    block_iota = lax.broadcasted_iota(jnp.int32, (slot_count, blocks_here), 1)
    serve_table = (send_local.reshape(slot_count, 1) == block_iota).astype(jnp.bfloat16)

    both = jnp.concatenate([memory_keys, memory_values], axis=2)
    entries2 = block_len * 2 * feature_cols
    served = jnp.dot(
        serve_table, both.reshape(blocks_here, entries2), preferred_element_type=jnp.float32
    ).astype(jnp.bfloat16)
    fetched = lax.all_to_all(
        served.reshape(mem_count, capacity, block_len, 2 * feature_cols),
        "mem", split_axis=0, concat_axis=0, tiled=True,
    )
    chosen = jnp.dot(
        pick_table, fetched.reshape(slot_count, entries2), preferred_element_type=jnp.float32
    ).astype(jnp.bfloat16).reshape(top_blocks * block_len, 2 * feature_cols)
    mem_keyset = chosen[:, :feature_cols].reshape(-1, heads_here, head_dim)
    mem_valueset = chosen[:, feature_cols:].reshape(-1, heads_here, head_dim)

    gate_values = 1.0 / (1.0 + jnp.exp(-gate_logit))
    gate_col = gate_values[None, :, None]
    keep_mask = dropout_keep.astype(jnp.float32)

    query_rows = queries.reshape(tok_rows, heads_here, head_dim)
    key_rows = local_keys.reshape(tok_rows, heads_here, head_dim)
    value_rows = local_values.reshape(tok_rows, heads_here, head_dim)

    cotangent_full = lax.all_gather(cotangent, "head", axis=1, tiled=True)
    grad_attended = lax.dot_general(
        cotangent_full, out_weight, (((1,), (1,)), ((), ())), preferred_element_type=jnp.float32
    ) * keep_mask * keep_scale
    grad_heads = grad_attended.reshape(tok_rows, heads_here, head_dim)
    grad_mem = (gate_col * grad_heads).transpose(1, 0, 2)
    grad_loc = ((1.0 - gate_col) * grad_heads).transpose(1, 0, 2)

    w_loc, l_loc, o_loc = branch(query_rows, key_rows, value_rows, grad_loc, True, score_scale)
    q_loc, k_loc, v_loc = branch_grads(
        query_rows, key_rows, value_rows, w_loc, l_loc, o_loc, grad_loc, score_scale
    )
    w_mem, l_mem, o_mem = branch(query_rows, mem_keyset, mem_valueset, grad_mem, False, score_scale)
    q_mem, k_mem, v_mem = branch_grads(
        query_rows, mem_keyset, mem_valueset, w_mem, l_mem, o_mem, grad_mem, score_scale
    )

    attended = (gate_col * o_mem.transpose(1, 0, 2) + (1.0 - gate_col) * o_loc.transpose(1, 0, 2))
    dropped = (attended.reshape(tok_rows, feature_cols) * keep_mask * keep_scale).astype(jnp.bfloat16)
    partial_out = jnp.dot(dropped, out_weight, preferred_element_type=jnp.float32)
    layer_out = lax.psum_scatter(partial_out, "head", scatter_dimension=1, tiled=True).astype(
        jnp.bfloat16
    )

    grad_queries = (q_mem + q_loc).astype(jnp.bfloat16).reshape(tok_rows, feature_cols)
    grad_keys = k_loc.astype(jnp.bfloat16).reshape(tok_rows, feature_cols)
    grad_values = v_loc.astype(jnp.bfloat16).reshape(tok_rows, feature_cols)

    parts = jnp.concatenate(
        [
            k_mem.astype(jnp.bfloat16).reshape(top_blocks, block_len, feature_cols),
            v_mem.astype(jnp.bfloat16).reshape(top_blocks, block_len, feature_cols),
        ],
        axis=2,
    ).reshape(top_blocks, entries2)
    send = lax.dot_general(
        pick_table, parts, (((0,), (0,)), ((), ())), preferred_element_type=jnp.float32
    ).astype(jnp.bfloat16)
    returned = lax.all_to_all(
        send.reshape(mem_count, capacity, block_len, 2 * feature_cols),
        "mem", split_axis=0, concat_axis=0, tiled=True,
    )
    summed = lax.dot_general(
        serve_table, returned.reshape(slot_count, entries2), (((0,), (0,)), ((), ())),
        preferred_element_type=jnp.float32,
    ).astype(jnp.bfloat16).reshape(blocks_here, block_len, 2 * feature_cols)
    return (
        layer_out,
        grad_queries,
        grad_keys,
        grad_values,
        summed[:, :, :feature_cols],
        summed[:, :, feature_cols:],
    )


def solution(mesh):
    placed = (
        P("mem", "head"),
        P("mem", "head"),
        P("mem", "head"),
        P("mem", None, "head"),
        P("mem", None, "head"),
        P(),
        P("head"),
        P("mem", "head"),
        P("head", None),
        P("mem", "head"),
    )
    return jax.shard_map(
        per_device,
        mesh=mesh,
        in_specs=placed,
        out_specs=(
            P("mem", "head"),
            P("mem", "head"),
            P("mem", "head"),
            P("mem", "head"),
            P("mem", None, "head"),
            P("mem", None, "head"),
        ),
        check_vma=False,
    )
```

time: 276 us -> 285 us (1.033)
  waiting for transfers between devices: 109 us -> 156 us
  matrix products: 82.7 us -> 55.5 us
  starting transfers between devices: 20.2 us -> 12.1 us
  local copies, waits for them, and re-layouts: 30.8 us -> 35.4 us
  between operations: 17.6 us -> 14.3 us
  other arithmetic: 13.5 us -> 10.6 us
    all_to_all x4 -> x2, waiting for transfers between devices: 109 us -> 137 us  [the longest x1 74.2 us: per_device(): lax.all_to_all(send.reshape(mem_count, capacity, block_len, 2 * feature_c...]
    dot_general x57 -> x17, matrix products: 79.3 us -> 51.2 us  [the longest x12 33.6 us: mm(): return jnp.einsum(spec, left, right, preferred_element_type=jnp.float32)]
    all_gather x1, waiting for transfers between devices: 0.01 us -> 18.1 us  [per_device(): cotangent_full = lax.all_gather(cotangent, 'head', axis=1, tiled=True)]
    all_to_all x4 -> x2, starting transfers between devices: 20.1 us -> 12.1 us  [the longest x1 7.44 us: per_device(): lax.all_to_all(served.reshape(mem_count, capacity, block_len, 2 * feature...]
    slice x1 -> x3, local copies, waits for them, and re-layouts: 0.66 us -> 6.38 us  [the longest x1 3.02 us: per_device(): mem_keyset = chosen[:, :feature_cols].reshape(-1, heads_here, head_dim)]
    unnamed x180 -> x42, local copies, waits for them, and re-layouts: 20.2 us -> 15.1 us
    reduce_sum x8 -> x3, other arithmetic: 6.68 us -> 2.43 us  [the longest x2 1.95 us: branch(): row_total = jnp.sum(weights, axis=2, keepdims=True)]
    convert_element_type x0 -> x2, local copies, waits for them, and re-layouts: none -> 4.17 us  [the longest x1 2.39 us: per_device(): v_mem.astype(jnp.bfloat16).reshape(top_blocks, block_len, feature_cols)]
  transfers between devices with their start and end apart: 6 -> 4, of which waited for: 4 -> 3; matrix products, arithmetic and copies ran while one was open for 30% -> 14% of each run, Pallas kernels for 0% -> 0%
where the time goes in v1:
time: 285 us; the launch traced here: 284 us
  waiting for transfers between devices  156 us (55%)
  matrix products  55.5 us (19%)
  local copies, waits for them, and re-layouts  35.4 us (12%)
  between operations  14.3 us (5%)
  starting transfers between devices  12.1 us (4%)
  other arithmetic  10.6 us (4%)
    all_to_all x1, waiting for transfers between devices, per_device(): lax.all_to_all(send.reshape(mem_count, capacity, block_len, 2 * feature_c...  74.2 us
    all_to_all x1, waiting for transfers between devices, per_device(): lax.all_to_all(served.reshape(mem_count, capacity, block_len, 2 * feature...  63.1 us
    dot_general x12, matrix products, mm(): return jnp.einsum(spec, left, right, preferred_element_type=jnp.float32)  33.6 us
    all_gather x1, waiting for transfers between devices, per_device(): cotangent_full = lax.all_gather(cotangent, 'head', axis=1, tiled=True)  18.1 us
    unnamed x42, local copies, waits for them, and re-layouts  15.1 us
    all_to_all x1, starting transfers between devices, per_device(): lax.all_to_all(served.reshape(mem_count, capacity, block_len, 2 * feature...  7.44 us
  transfers between devices with their start and end apart: 4, of which 3 were waited for; matrix products, arithmetic and copies ran while one was open for 14% of the time, Pallas kernels for 0%

profile of v1, /device:TPU:0, one launch (start us, length us, event | category | flops | bytes accessed | tf_op | source)
XLA Modules:
  0.0 284.0 jit_solution(9445346572772178851)
XLA Ops:
  11.1 3.3 %convolution_convert_fusion.1 = bf16[64,32768]{1,0:T(8,128)(2,1)} fusion(bf16[16,32768]{1,0:T(8,128)(2,1)S(1)} %bitcast.165, s32[64]{0:T(128)S(1)} %sub.51), kind=kOutput, calls=%fused_computation.1 | convolution fusion | flops 69207040 | bytes 5243136 | tf_op jit(solution)/shard_map/dot_general | solution.py:85
  14.3 7.4 %all-to-all-start = ((bf16[8,8,32,1024]{3,1,2,0:T(8,128)(2,1)}), bf16[8,8,32,1024]{3,1,2,0:T(8,128)(2,1)}, u32[]{:S(2)}, u32[]{:S(2)}) async-start(bf16[8,8,32,1024]{3,1,2,0:T(8,128)(2,1)} %bitcast.154), calls=%async_computation | async-start | bytes 8388608 | tf_op jit(solution)/shard_map/all_to_all | solution.py:88
  25.2 2.3 fusion.10
  30.0 18.1 %all-gather.2.cloned.1.call-done = bf16[512,2048]{1,0:T(8,128)(2,1)} async-done(((bf16[512,512]{1,0:T(8,128)(2,1)}), bf16[512,2048]{1,0:T(8,128)(2,1)}) %all-gather.2.cloned.1.call-update) | async-done | bytes 2097168 | tf_op jit(solution)/shard_map/all_gather | solution.py:106
  48.2 3.8 %fusion.24 = f32[512,512]{0,1:T(8,128)} fusion(bf16[512,2048]{1,0:T(8,128)(2,1)} %all-gather.2.cloned.1.call-done, bf16[512,2048]{1,0:T(8,128)(2,1)S(1)} %copy-done, s32[512,512]{0,1:T(8,128)S(1)} %copy.80), kind=kOutput, calls=%fused_computation.35 | convolution fusion | flops 1074528256 | bytes 6291456 | tf_op jit(solution)/shard_map/dot_general | solution.py:107
  52.0 63.1 %all-to-all-done = bf16[8,8,32,1024]{3,1,2,0:T(8,128)(2,1)} async-done(((bf16[8,8,32,1024]{3,1,2,0:T(8,128)(2,1)}), bf16[8,8,32,1024]{3,1,2,0:T(8,128)(2,1)}, u32[]{:S(2)}, u32[]{:S(2)}) %all-to-all-start) | async-done | bytes 4194336 | tf_op jit(solution)/shard_map/all_to_all | solution.py:88
  115.1 4.3 %convolution_convert_fusion.2 = bf16[32,32768]{1,0:T(8,128)(2,1)} fusion(bf16[64,32768]{1,0:T(8,128)(2,1)} %bitcast.2, s32[32]{0:T(128)S(1)} %add_bitcast_fusion), kind=kOutput, calls=%fused_computation.2 | convolution fusion | flops 135268352 | bytes 6291584 | tf_op jit(solution)/shard_map/dot_general | solution.py:92
  119.3 4.2 %reshape.119 = bf16[1024,1024]{1,0:T(8,128)(2,1)} reshape(bf16[32,32768]{1,0:T(8,128)(2,1)} %convolution_convert_fusion.2) | data formatting | bytes 4194304 | tf_op jit(solution)/shard_map/reshape | solution.py:94
  123.5 3.0 %fusion.65 = (bf16[1024,512]{1,0:T(8,128)(2,1)}, bf16[1024,512]{1,0:T(8,128)(2,1)}) fusion(bf16[1024,1024]{1,0:T(8,128)(2,1)} %reshape.119), kind=kLoop, calls=%fused_computation.100 | loop fusion | bytes 4194304 | tf_op jit(solution)/shard_map/slice | solution.py:95
  130.3 2.3 bitcast_reduce_fusion
  134.7 2.5 fusion.4
  137.2 3.0 %fusion.20 = bf16[1024,4,128]{0,2,1:T(8,128)(2,1)} fusion(f32[4,512]{1,0:T(4,128)S(1)} %fusion.2, f32[4,512]{1,0:T(4,128)S(1)} %get-tuple-element.36, f32[4,1024,512]{2,1,0:T(8,128)S(1)} %get-tuple-element.37, f32[4]{0:T(128)S(1)} %get-tuple-element.27, f32[512,512]{0,1:T(8,128)S(1)} %copy-done.13), kind=kOutput, calls=%fused_computation.31 | convolution fusion | flops 546308096 | bytes 10502160 | tf_op jit(solution)/shard_map/htk,htd->khd/dot_general | solution.py:13
  140.2 2.4 copy.96
  142.6 2.3 reshape.131
  144.8 3.6 %fusion.34 = (f32[512,4,128]{0,2,1:T(8,128)S(1)}, f32[4,512,128]{1,2,0:T(8,128)S(1)}) fusion(f32[4,512,128]{1,2,0:T(8,128)} %fusion.4, f32[512,4]{0,1:T(4,128)S(1)} %bitcast.172, f32[4]{0:T(128)S(1)} %get-tuple-element.26, f32[512,4]{0,1:T(4,128)S(1)} %bitcast.173, f32[4]{0:T(128)S(1)} %get-tuple-element.27, f32[4,512]{1,0:T(4,128)S(1)} %get-tuple-element.34, ...), kind=kOutput, calls=%fused_computation.51 | convolution fusion | flops 274989056 | bytes 7888928 | tf_op jit(solution)/shard_map/htk,khd->htd/dot_general | solution.py:13
  150.1 5.3 %multiply_convert_fusion = bf16[4,512,1024]{1,2,0:T(8,128)(2,1)S(1)} fusion(f32[4,512]{1,0:T(4,128)S(1)} %get-tuple-element.24, bf16[1024,4,128]{0,2,1:T(8,128)(2,1)S(1)} %bitcast.161, f32[4,512]{1,0:T(4,128)S(1)} %fusion.2, f32[4,512]{1,0:T(4,128)S(1)} %get-tuple-element.36, f32[4,1024,512]{2,1,0:T(8,128)} %copy-done.1, f32[4]{0:T(128)S(1)} %get-tuple-element.27, ...), kind=kOutput, calls=%fused_computation.7 | convolution fusion | flops 552075264 | bytes 14704656 | tf_op jit(solution)/shard_map/htd,khd->htk/dot_general | solution.py:13
  162.7 4.3 %fusion.67 = f32[512,2048]{1,0:T(8,128)} fusion(bf16[512,512]{0,1:T(8,128)(2,1)} %fusion.32, bf16[512,2048]{1,0:T(8,128)(2,1)S(1)} %copy-done), kind=kOutput, calls=%fused_computation.102 | convolution fusion | flops 1073741824 | bytes 6815744 | tf_op jit(solution)/shard_map/dot_general | solution.py:125
  169.9 3.3 %convolution_convert_fusion = bf16[64,32768]{1,0:T(8,128)(2,1)} fusion(bf16[32,32768]{1,0:T(8,128)(2,1)S(1)} %bitcast.158, s32[32]{0:T(128)S(1)} %add_bitcast_fusion), kind=kOutput, calls=%fused_computation | convolution fusion | flops 136316928 | bytes 6291584 | tf_op jit(solution)/shard_map/dot_general | solution.py:141
  173.2 4.6 %all-to-all-start.1 = ((bf16[8,8,32,1024]{3,1,2,0:T(8,128)(2,1)}), bf16[8,8,32,1024]{3,1,2,0:T(8,128)(2,1)}, u32[]{:S(2)}, u32[]{:S(2)}) async-start(bf16[8,8,32,1024]{3,1,2,0:T(8,128)(2,1)} %bitcast.155), calls=%async_computation.2 | async-start | bytes 8388608 | tf_op jit(solution)/shard_map/all_to_all | solution.py:144
  177.9 4.2 %fusion.26 = bf16[4,128,512]{2,1,0:T(8,128)(2,1)} fusion(f32[4,512]{1,0:T(4,128)S(1)} %fusion.46, f32[4,512,512]{1,2,0:T(8,128)} %copy-done.8, f32[4,512]{1,0:T(4,128)S(1)} %get-tuple-element.34, f32[4]{0:T(128)S(1)} %get-tuple-element.26, f32[512,512]{0,1:T(8,128)} %fusion.24), kind=kOutput, calls=%fused_computation.38 | convolution fusion | flops 275513344 | bytes 5783568 | tf_op jit(solution)/shard_map/htk,htd->khd/dot_general | solution.py:13
  184.1 4.4 %multiply_convert_fusion.1 = bf16[4,512,512]{1,2,0:T(8,128)(2,1)S(1)} fusion(f32[4,512]{1,0:T(4,128)S(1)} %get-tuple-element.25, f32[4,512]{1,0:T(4,128)S(1)} %fusion.46, f32[4,512]{1,0:T(4,128)S(1)} %get-tuple-element.34, f32[4,512,512]{1,2,0:T(8,128)} %copy-done.8, f32[4]{0:T(128)S(1)} %get-tuple-element.26, f32[512,512]{0,1:T(8,128)} %fusion.24, ...), kind=kOutput, calls=%fused_computation.14 | convolution fusion | flops 278396928 | bytes 7888912 | tf_op jit(solution)/shard_map/htd,khd->htk/dot_general | solution.py:13
  192.7 2.5 convolution_convert_fusion.5
  196.2 74.2 %all-to-all-done.1 = bf16[8,8,32,1024]{3,1,2,0:T(8,128)(2,1)} async-done(((bf16[8,8,32,1024]{3,1,2,0:T(8,128)(2,1)}), bf16[8,8,32,1024]{3,1,2,0:T(8,128)(2,1)}, u32[]{:S(2)}, u32[]{:S(2)}) %all-to-all-start.1) | async-done | bytes 4194336 | tf_op jit(solution)/shard_map/all_to_all | solution.py:144
  270.4 3.0 %convolution_convert_fusion.3 = bf16[16,32768]{1,0:T(8,128)(2,1)S(1)} fusion(bf16[64,32768]{1,0:T(8,128)(2,1)} %bitcast.24, s32[64]{0:T(128)S(1)} %sub.51), kind=kOutput, calls=%fused_computation.3 | convolution fusion | flops 67634176 | bytes 5243136 | tf_op jit(solution)/shard_map/dot_general | solution.py:148
  (71 shorter events, 38.1 us)
Async XLA Ops:
  7.2 41.0 %copy-start = (bf16[512,2048]{1,0:T(8,128)(2,1)S(1)}, bf16[512,2048]{1,0:T(8,128)(2,1)}, u32[]{:S(2)}) copy-start(bf16[512,2048]{1,0:T(8,128)(2,1)} %param.18) | copy-start | bytes 6291460
  14.3 8.2 %copy-start.15 = (bf16[512,512]{1,0:T(8,128)(2,1)S(1)}, bf16[512,512]{1,0:T(8,128)(2,1)}, u32[]{:S(2)}) copy-start(bf16[512,512]{1,0:T(8,128)(2,1)} %param.11) | copy-start | bytes 1572868
  14.3 10.8 %copy-start.16 = (f32[4]{0:T(128)S(1)}, f32[4]{0:T(128)}, u32[]{:S(2)}) copy-start(f32[4]{0:T(128)} %param.16) | copy-start | bytes 52
  14.3 100.7 %all-to-all-start = ((bf16[8,8,32,1024]{3,1,2,0:T(8,128)(2,1)}), bf16[8,8,32,1024]{3,1,2,0:T(8,128)(2,1)}, u32[]{:S(2)}, u32[]{:S(2)}) async-start(bf16[8,8,32,1024]{3,1,2,0:T(8,128)(2,1)} %bitcast.154), calls=%async_computation | async-start | bytes 8388608 | tf_op jit(solution)/shard_map/all_to_all | solution.py:88
  21.8 26.4 %all-gather.2.cloned.1.call-start = ((), (), s32[]{:S(2)}) async-start(), calls=%async_computation.4 | async-start | bytes 2621440 | tf_op jit(solution)/shard_map/all_gather | solution.py:106
  22.5 252.6 %reduce-scatter.2.cloned.1.call-start = ((), (), s32[]{:S(2)}) async-start(), calls=%async_computation.3 | async-start | bytes 5242880 | tf_op jit(solution)/shard_map/reduce_scatter | solution.py:126
  25.1 23.0 %copy-start.9 = (s32[512,512]{0,1:T(8,128)}, s32[512,512]{0,1:T(8,128)S(1)}, u32[]{:S(2)}) copy-start(s32[512,512]{0,1:T(8,128)S(1)} %copy.80) | copy-start | bytes 3145732
  27.5 2.0 copy-start.8
  132.6 4.5 %copy-start.1 = (f32[4,1024,512]{2,1,0:T(8,128)}, f32[4,1024,512]{2,1,0:T(8,128)S(1)}, u32[]{:S(2)}) copy-start(f32[4,1024,512]{2,1,0:T(8,128)S(1)} %get-tuple-element.37) | copy-start | bytes 25165828
  132.7 2.0 copy-start.5
  134.7 2.5 copy-start.13
  144.8 3.7 %copy-start.10 = (s32[512,512]{0,1:T(8,128)S(1)}, s32[512,512]{0,1:T(8,128)}, u32[]{:S(2)}) copy-start(s32[512,512]{0,1:T(8,128)} %copy-done.9) | copy-start | bytes 3145732
  144.8 4.7 %copy-start.7 = (f32[4,512,128]{1,2,0:T(8,128)S(1)}, f32[4,512,128]{1,2,0:T(8,128)}, u32[]{:S(2)}) copy-start(f32[4,512,128]{1,2,0:T(8,128)} %fusion.4) | copy-start | bytes 3145732
  144.8 4.7 %copy-start.14 = (f32[512,512]{0,1:T(8,128)S(1)}, f32[512,512]{0,1:T(8,128)}, u32[]{:S(2)}) copy-start(f32[512,512]{0,1:T(8,128)} %fusion.24) | copy-start | bytes 3145732
  148.5 1.6 copy-start.6
  150.1 7.3 %copy-start.12 = (bf16[512,512]{1,0:T(8,128)(2,1)S(1)}, bf16[512,512]{1,0:T(8,128)(2,1)}, u32[]{:S(2)}) copy-start(bf16[512,512]{1,0:T(8,128)(2,1)} %param.10) | copy-start | bytes 1572868
  155.4 2.0 copy-start.2
  173.2 97.2 %all-to-all-start.1 = ((bf16[8,8,32,1024]{3,1,2,0:T(8,128)(2,1)}), bf16[8,8,32,1024]{3,1,2,0:T(8,128)(2,1)}, u32[]{:S(2)}, u32[]{:S(2)}) async-start(bf16[8,8,32,1024]{3,1,2,0:T(8,128)(2,1)} %bitcast.155), calls=%async_computation.2 | async-start | bytes 8388608 | tf_op jit(solution)/shard_map/all_to_all | solution.py:144
  184.1 4.4 %copy-start.11 = (bf16[512,512]{0,1:T(8,128)(2,1)S(1)}, bf16[512,512]{0,1:T(8,128)(2,1)}, u32[]{:S(2)}) copy-start(bf16[512,512]{0,1:T(8,128)(2,1)} %copy.114) | copy-start | bytes 1572868
  184.1 4.9 %copy-start.3 = (bf16[4,512,1024]{1,2,0:T(8,128)(2,1)S(1)}, bf16[4,512,1024]{1,2,0:T(8,128)(2,1)}, u32[]{:S(2)}) copy-start(bf16[4,512,1024]{1,2,0:T(8,128)(2,1)} %copy-done.2) | copy-start | bytes 12582916
  188.6 2.1 copy-start.4
Sparse Core Ops, SparseCore 0:
  24.2 23.9 all-gather.1
  167.1 43.4 reduce-scatter.1

commit v2 on v1

--- a/solution.py
+++ b/solution.py
@@ -4,6 +4,7 @@
 from jax.sharding import PartitionSpec as P
 
 QBLK = 512
+CHUNKS = 2
 
 
 keep_scale = 1.0 / 0.9
@@ -80,21 +81,6 @@
     block_iota = lax.broadcasted_iota(jnp.int32, (slot_count, blocks_here), 1)
     serve_table = (send_local.reshape(slot_count, 1) == block_iota).astype(jnp.bfloat16)
 
-    both = jnp.concatenate([memory_keys, memory_values], axis=2)
-    entries2 = block_len * 2 * feature_cols
-    served = jnp.dot(
-        serve_table, both.reshape(blocks_here, entries2), preferred_element_type=jnp.float32
-    ).astype(jnp.bfloat16)
-    fetched = lax.all_to_all(
-        served.reshape(mem_count, capacity, block_len, 2 * feature_cols),
-        "mem", split_axis=0, concat_axis=0, tiled=True,
-    )
-    chosen = jnp.dot(
-        pick_table, fetched.reshape(slot_count, entries2), preferred_element_type=jnp.float32
-    ).astype(jnp.bfloat16).reshape(top_blocks * block_len, 2 * feature_cols)
-    mem_keyset = chosen[:, :feature_cols].reshape(-1, heads_here, head_dim)
-    mem_valueset = chosen[:, feature_cols:].reshape(-1, heads_here, head_dim)
-
     gate_values = 1.0 / (1.0 + jnp.exp(-gate_logit))
     gate_col = gate_values[None, :, None]
     keep_mask = dropout_keep.astype(jnp.float32)
@@ -102,6 +88,24 @@
     query_rows = queries.reshape(tok_rows, heads_here, head_dim)
     key_rows = local_keys.reshape(tok_rows, heads_here, head_dim)
     value_rows = local_values.reshape(tok_rows, heads_here, head_dim)
+
+    chunk_heads = heads_here // CHUNKS if heads_here % CHUNKS == 0 else heads_here
+    chunk_count = heads_here // chunk_heads
+    chunk_cols = chunk_heads * head_dim
+    entries2 = block_len * 2 * chunk_cols
+
+    def fetch(chunk):
+        cols = slice(chunk * chunk_cols, (chunk + 1) * chunk_cols)
+        both = jnp.concatenate([memory_keys[:, :, cols], memory_values[:, :, cols]], axis=2)
+        served = jnp.dot(
+            serve_table, both.reshape(blocks_here, entries2), preferred_element_type=jnp.float32
+        ).astype(jnp.bfloat16)
+        return lax.all_to_all(
+            served.reshape(mem_count, capacity, block_len, 2 * chunk_cols),
+            "mem", split_axis=0, concat_axis=0, tiled=True,
+        )
+
+    fetched = [fetch(0)]
 
     cotangent_full = lax.all_gather(cotangent, "head", axis=1, tiled=True)
     grad_attended = lax.dot_general(
@@ -115,11 +119,51 @@
     q_loc, k_loc, v_loc = branch_grads(
         query_rows, key_rows, value_rows, w_loc, l_loc, o_loc, grad_loc, score_scale
     )
-    w_mem, l_mem, o_mem = branch(query_rows, mem_keyset, mem_valueset, grad_mem, False, score_scale)
-    q_mem, k_mem, v_mem = branch_grads(
-        query_rows, mem_keyset, mem_valueset, w_mem, l_mem, o_mem, grad_mem, score_scale
-    )
-
+
+    if chunk_count > 1:
+        memory_keys, memory_values, o_loc, q_loc, k_loc, v_loc, grad_mem = lax.optimization_barrier(
+            (memory_keys, memory_values, o_loc, q_loc, k_loc, v_loc, grad_mem)
+        )
+    o_mem_parts, q_mem_parts, summed_parts = [], [], []
+    for chunk in range(chunk_count):
+        if chunk + 1 < chunk_count:
+            fetched.append(fetch(chunk + 1))
+        heads = slice(chunk * chunk_heads, (chunk + 1) * chunk_heads)
+        chosen = jnp.dot(
+            pick_table, fetched[chunk].reshape(slot_count, entries2),
+            preferred_element_type=jnp.float32,
+        ).astype(jnp.bfloat16).reshape(top_blocks * block_len, 2 * chunk_cols)
+        mem_keyset = chosen[:, :chunk_cols].reshape(-1, chunk_heads, head_dim)
+        mem_valueset = chosen[:, chunk_cols:].reshape(-1, chunk_heads, head_dim)
+        q_chunk = query_rows[:, heads]
+        g_chunk = grad_mem[heads]
+        w_mem, l_mem, o_mem = branch(q_chunk, mem_keyset, mem_valueset, g_chunk, False, score_scale)
+        q_mem, k_mem, v_mem = branch_grads(
+            q_chunk, mem_keyset, mem_valueset, w_mem, l_mem, o_mem, g_chunk, score_scale
+        )
+        o_mem_parts.append(o_mem)
+        q_mem_parts.append(q_mem)
+        parts = jnp.concatenate(
+            [
+                k_mem.astype(jnp.bfloat16).reshape(top_blocks, block_len, chunk_cols),
+                v_mem.astype(jnp.bfloat16).reshape(top_blocks, block_len, chunk_cols),
+            ],
+            axis=2,
+        ).reshape(top_blocks, entries2)
+        send = lax.dot_general(
+            pick_table, parts, (((0,), (0,)), ((), ())), preferred_element_type=jnp.float32
+        ).astype(jnp.bfloat16)
+        returned = lax.all_to_all(
+            send.reshape(mem_count, capacity, block_len, 2 * chunk_cols),
+            "mem", split_axis=0, concat_axis=0, tiled=True,
+        )
+        summed_parts.append(lax.dot_general(
+            serve_table, returned.reshape(slot_count, entries2), (((0,), (0,)), ((), ())),
+            preferred_element_type=jnp.float32,
+        ).astype(jnp.bfloat16).reshape(blocks_here, block_len, 2 * chunk_cols))
+
+    o_mem = jnp.concatenate(o_mem_parts, axis=0)
+    q_mem = jnp.concatenate(q_mem_parts, axis=1)
     attended = (gate_col * o_mem.transpose(1, 0, 2) + (1.0 - gate_col) * o_loc.transpose(1, 0, 2))
     dropped = (attended.reshape(tok_rows, feature_cols) * keep_mask * keep_scale).astype(jnp.bfloat16)
     partial_out = jnp.dot(dropped, out_weight, preferred_element_type=jnp.float32)
@@ -130,32 +174,15 @@
     grad_queries = (q_mem + q_loc).astype(jnp.bfloat16).reshape(tok_rows, feature_cols)
     grad_keys = k_loc.astype(jnp.bfloat16).reshape(tok_rows, feature_cols)
     grad_values = v_loc.astype(jnp.bfloat16).reshape(tok_rows, feature_cols)
-
-    parts = jnp.concatenate(
-        [
-            k_mem.astype(jnp.bfloat16).reshape(top_blocks, block_len, feature_cols),
-            v_mem.astype(jnp.bfloat16).reshape(top_blocks, block_len, feature_cols),
-        ],
-        axis=2,
-    ).reshape(top_blocks, entries2)
-    send = lax.dot_general(
-        pick_table, parts, (((0,), (0,)), ((), ())), preferred_element_type=jnp.float32
-    ).astype(jnp.bfloat16)
-    returned = lax.all_to_all(
-        send.reshape(mem_count, capacity, block_len, 2 * feature_cols),
-        "mem", split_axis=0, concat_axis=0, tiled=True,
-    )
-    summed = lax.dot_general(
-        serve_table, returned.reshape(slot_count, entries2), (((0,), (0,)), ((), ())),
-        preferred_element_type=jnp.float32,
-    ).astype(jnp.bfloat16).reshape(blocks_here, block_len, 2 * feature_cols)
+    grad_memory_keys = jnp.concatenate([s[:, :, :chunk_cols] for s in summed_parts], axis=2)
+    grad_memory_values = jnp.concatenate([s[:, :, chunk_cols:] for s in summed_parts], axis=2)
     return (
         layer_out,
         grad_queries,
         grad_keys,
         grad_values,
-        summed[:, :, :feature_cols],
-        summed[:, :, feature_cols:],
+        grad_memory_keys,
+        grad_memory_values,
     )
 
 

time: 285 us -> 281 us (0.986)
  waiting for transfers between devices: 156 us -> 120 us
  local copies, waits for them, and re-layouts: 35.4 us -> 49.2 us
  starting transfers between devices: 12.1 us -> 21 us
  matrix products: 55.5 us -> 64 us
    all_to_all x2 -> x4, waiting for transfers between devices: 137 us -> 114 us  [the longest x2 59.6 us: per_device(): lax.all_to_all(send.reshape(mem_count, capacity, block_len, 2 * chunk_col...]
    all_gather x1, waiting for transfers between devices: 18.1 us -> 4.83 us  [per_device(): cotangent_full = lax.all_gather(cotangent, 'head', axis=1, tiled=True)]
    all_to_all x2 -> x4, starting transfers between devices: 12.1 us -> 20.8 us  [the longest x2 11.8 us: fetch(): lax.all_to_all(served.reshape(mem_count, capacity, block_len, 2 * chunk_c...]
    dot_general x12 -> x18, matrix products: 33.6 us -> 39 us  [mm(): return jnp.einsum(spec, left, right, preferred_element_type=jnp.float32)]
    convert_element_type x2 -> x6, local copies, waits for them, and re-layouts: 4.17 us -> 8.93 us  [the longest x2 4.01 us: per_device(): v_mem.astype(jnp.bfloat16).reshape(top_blocks, block_len, chunk_cols)]
    unnamed x42 -> x51, local copies, waits for them, and re-layouts: 15.1 us -> 19.3 us
    reshape x4 -> x6, local copies, waits for them, and re-layouts: 9.7 us -> 12.7 us  [the longest x2 4.45 us: per_device(): v_mem.astype(jnp.bfloat16).reshape(top_blocks, block_len, chunk_cols)]
    dot_general x2 -> x4, matrix products: 7.54 us -> 10.2 us  [the longest x2 6.11 us: per_device(): jnp.dot(pick_table, fetched[chunk].reshape(slot_count, entries2), preferr...]
  transfers between devices with their start and end apart: 4 -> 6, of which waited for: 3 -> 5; matrix products, arithmetic and copies ran while one was open for 14% -> 35% of each run, Pallas kernels for 0% -> 0%
where the time goes in v2:
time: 281 us; the launch traced here: 280 us
  waiting for transfers between devices  120 us (43%)
  matrix products  64 us (23%)
  local copies, waits for them, and re-layouts  49.2 us (18%)
  starting transfers between devices  21 us (7%)
  between operations  14.5 us (5%)
  other arithmetic  11.3 us (4%)
    all_to_all x2, waiting for transfers between devices, per_device(): lax.all_to_all(send.reshape(mem_count, capacity, block_len, 2 * chunk_col...  59.6 us
    all_to_all x2, waiting for transfers between devices, fetch(): lax.all_to_all(served.reshape(mem_count, capacity, block_len, 2 * chunk_c...  54.4 us
    dot_general x18, matrix products, mm(): return jnp.einsum(spec, left, right, preferred_element_type=jnp.float32)  39 us
    unnamed x51, local copies, waits for them, and re-layouts  19.3 us
    all_to_all x2, starting transfers between devices, fetch(): lax.all_to_all(served.reshape(mem_count, capacity, block_len, 2 * chunk_c...  11.8 us
    all_to_all x2, starting transfers between devices, per_device(): lax.all_to_all(send.reshape(mem_count, capacity, block_len, 2 * chunk_col...  8.98 us
    dot_general x2, matrix products, per_device(): jnp.dot(pick_table, fetched[chunk].reshape(slot_count, entries2), preferr...  6.11 us
  transfers between devices with their start and end apart: 6, of which 5 were waited for; matrix products, arithmetic and copies ran while one was open for 35% of the time, Pallas kernels for 0%

profile of v2, /device:TPU:0, one launch (start us, length us, event | category | flops | bytes accessed | tf_op | source)
XLA Modules:
  0.0 279.5 jit_solution(14870585356025470156)
XLA Ops:
  14.1 7.4 %all-to-all-start = ((bf16[8,8,32,512]{3,1,2,0:T(8,128)(2,1)}), bf16[8,8,32,512]{3,1,2,0:T(8,128)(2,1)}, u32[]{:S(2)}, u32[]{:S(2)}) async-start(bf16[8,8,32,512]{3,1,2,0:T(8,128)(2,1)} %bitcast.166), calls=%async_computation | async-start | bytes 4194304 | tf_op jit(solution)/shard_map/all_to_all | solution.py:103
  23.2 2.4 copy.90
  30.0 4.8 %all-gather.2.cloned.1.call-done = bf16[512,2048]{1,0:T(8,128)(2,1)} async-done(((bf16[512,512]{1,0:T(8,128)(2,1)}), bf16[512,2048]{1,0:T(8,128)(2,1)}) %all-gather.2.cloned.1.call-update) | async-done | bytes 2097168 | tf_op jit(solution)/shard_map/all_gather | solution.py:110
  34.9 3.0 %fusion.31 = f32[512,512]{0,1:T(8,128)S(1)} fusion(bf16[512,2048]{1,0:T(8,128)(2,1)} %all-gather.2.cloned.1.call-done, bf16[512,2048]{1,0:T(8,128)(2,1)S(1)} %copy-done, s32[512,512]{0,1:T(8,128)S(1)} %copy.99), kind=kOutput, calls=%fused_computation.47 | convolution fusion | flops 1074528256 | bytes 6291456 | tf_op jit(solution)/shard_map/dot_general | solution.py:111
  49.8 20.2 %all-to-all-done = bf16[8,8,32,512]{3,1,2,0:T(8,128)(2,1)} async-done(((bf16[8,8,32,512]{3,1,2,0:T(8,128)(2,1)}), bf16[8,8,32,512]{3,1,2,0:T(8,128)(2,1)}, u32[]{:S(2)}, u32[]{:S(2)}) %all-to-all-start) | async-done | bytes 2097184 | tf_op jit(solution)/shard_map/all_to_all | solution.py:103
  69.9 4.3 %all-to-all-start.1 = ((bf16[8,8,32,512]{3,1,2,0:T(8,128)(2,1)}), bf16[8,8,32,512]{3,1,2,0:T(8,128)(2,1)}, u32[]{:S(2)}, u32[]{:S(2)}) async-start(bf16[8,8,32,512]{3,1,2,0:T(8,128)(2,1)} %bitcast.167), calls=%async_computation.1 | async-start | bytes 4194304 | tf_op jit(solution)/shard_map/all_to_all | solution.py:103
  74.5 3.1 %convolution_convert_fusion.5 = bf16[32,16384]{1,0:T(8,128)(2,1)} fusion(bf16[64,16384]{1,0:T(8,128)(2,1)} %bitcast.2, s32[32]{0:T(128)S(1)} %add_bitcast_fusion), kind=kOutput, calls=%fused_computation.5 | convolution fusion | flops 67635200 | bytes 3145856 | tf_op jit(solution)/shard_map/dot_general | solution.py:132
  87.9 34.2 %all-to-all-done.1 = bf16[8,8,32,512]{3,1,2,0:T(8,128)(2,1)} async-done(((bf16[8,8,32,512]{3,1,2,0:T(8,128)(2,1)}), bf16[8,8,32,512]{3,1,2,0:T(8,128)(2,1)}, u32[]{:S(2)}, u32[]{:S(2)}) %all-to-all-start.1) | async-done | bytes 2097184 | tf_op jit(solution)/shard_map/all_to_all | solution.py:103
  122.1 3.0 %convolution_convert_fusion.4 = bf16[32,16384]{1,0:T(8,128)(2,1)} fusion(bf16[64,16384]{1,0:T(8,128)(2,1)} %bitcast.14, s32[32]{0:T(128)S(1)} %add_bitcast_fusion), kind=kOutput, calls=%fused_computation.4 | convolution fusion | flops 67635200 | bytes 3145856 | tf_op jit(solution)/shard_map/dot_general | solution.py:132
  125.1 2.3 reshape.168
  139.6 3.2 %fusion.99 = f32[512,2048]{1,0:T(8,128)} fusion(bf16[512,512]{0,1:T(8,128)(2,1)S(1)} %fusion.55, bf16[512,2048]{1,0:T(8,128)(2,1)S(1)} %copy-done), kind=kOutput, calls=%fused_computation.138 | convolution fusion | flops 1073741824 | bytes 6815744 | tf_op jit(solution)/shard_map/dot_general | solution.py:169
  142.9 5.3 %multiply_convert_fusion = bf16[2,512,1024]{1,2,0:T(8,128)(2,1)} fusion(bf16[1024,2,128]{0,2,1:T(8,128)(2,1)} %bitcast.198, f32[2,512]{1,0:T(2,128)S(1)} %get-tuple-element.39, f32[2,512]{1,0:T(2,128)S(1)} %fusion.7, f32[2,512]{1,0:T(2,128)S(1)} %get-tuple-element.56, f32[2,1024,512]{2,1,0:T(8,128)} %copy-done.3, f32[4,512,128]{1,2,0:T(8,128)} %multiply_bitcast_fusion), kind=kOutput, calls=%fused_computation.14 | convolution fusion | flops 275775488 | bytes 7090176 | tf_op jit(solution)/shard_map/htd,khd->htk/dot_general | solution.py:14
  150.2 2.3 reshape.182
  152.5 2.4 fusion.39
  162.4 4.4 %all-to-all-start.3 = ((bf16[8,8,32,512]{3,1,2,0:T(8,128)(2,1)}), bf16[8,8,32,512]{3,1,2,0:T(8,128)(2,1)}, u32[]{:S(2)}, u32[]{:S(2)}) async-start(bf16[8,8,32,512]{3,1,2,0:T(8,128)(2,1)} %bitcast.169), calls=%async_computation.4 | async-start | bytes 4194304 | tf_op jit(solution)/shard_map/all_to_all | solution.py:156
  166.8 4.2 %fusion.43 = bf16[1024,2,128]{0,2,1:T(8,128)(2,1)} fusion(f32[2,1024,512]{2,1,0:T(8,128)} %copy-done.1, f32[2,512]{1,0:T(2,128)S(1)} %fusion.4, f32[2,512]{1,0:T(2,128)S(1)} %get-tuple-element.58, f32[4,512,128]{1,2,0:T(8,128)} %multiply_bitcast_fusion), kind=kOutput, calls=%fused_computation.55 | convolution fusion | flops 272891904 | bytes 4988928 | tf_op jit(solution)/shard_map/htk,htd->khd/dot_general | solution.py:14
  172.9 2.2 reshape.176
  175.1 4.0 %multiply_convert_fusion.1 = bf16[2,512,1024]{1,2,0:T(8,128)(2,1)S(1)} fusion(bf16[1024,2,128]{0,2,1:T(8,128)(2,1)} %bitcast.196, f32[2,512]{1,0:T(2,128)S(1)} %get-tuple-element.38, f32[2,512]{1,0:T(2,128)S(1)} %fusion.4, f32[2,512]{1,0:T(2,128)S(1)} %get-tuple-element.58, f32[2,1024,512]{2,1,0:T(8,128)} %copy-done.1, f32[4,512,128]{1,2,0:T(8,128)} %multiply_bitcast_fusion), kind=kOutput, calls=%fused_computation.15 | convolution fusion | flops 275775488 | bytes 7090176 | tf_op jit(solution)/shard_map/htd,khd->htk/dot_general | solution.py:14
  181.8 2.2 reshape.175
  188.0 26.8 %all-to-all-done.3 = bf16[8,8,32,512]{3,1,2,0:T(8,128)(2,1)} async-done(((bf16[8,8,32,512]{3,1,2,0:T(8,128)(2,1)}), bf16[8,8,32,512]{3,1,2,0:T(8,128)(2,1)}, u32[]{:S(2)}, u32[]{:S(2)}) %all-to-all-start.3) | async-done | bytes 2097184 | tf_op jit(solution)/shard_map/all_to_all | solution.py:156
  214.9 4.6 %all-to-all-start.2 = ((bf16[8,8,32,512]{3,1,2,0:T(8,128)(2,1)}), bf16[8,8,32,512]{3,1,2,0:T(8,128)(2,1)}, u32[]{:S(2)}, u32[]{:S(2)}) async-start(bf16[8,8,32,512]{3,1,2,0:T(8,128)(2,1)} %bitcast.168), calls=%async_computation.3 | async-start | bytes 4194304 | tf_op jit(solution)/shard_map/all_to_all | solution.py:156
  225.6 2.6 convolution_bitcast_fusion.2
  228.2 2.5 convolution_bitcast_fusion.3
  234.4 32.8 %all-to-all-done.2 = bf16[8,8,32,512]{3,1,2,0:T(8,128)(2,1)} async-done(((bf16[8,8,32,512]{3,1,2,0:T(8,128)(2,1)}), bf16[8,8,32,512]{3,1,2,0:T(8,128)(2,1)}, u32[]{:S(2)}, u32[]{:S(2)}) %all-to-all-start.2) | async-done | bytes 2097184 | tf_op jit(solution)/shard_map/all_to_all | solution.py:156
  (115 shorter events, 80.7 us)
Async XLA Ops:
  7.2 27.7 %copy-start = (bf16[512,2048]{1,0:T(8,128)(2,1)S(1)}, bf16[512,2048]{1,0:T(8,128)(2,1)}, u32[]{:S(2)}) copy-start(bf16[512,2048]{1,0:T(8,128)(2,1)} %param.18) | copy-start | bytes 6291460
  7.2 27.7 %all-gather.2.cloned.1.call-start = ((), (), s32[]{:S(2)}) async-start(), calls=%async_computation.5 | async-start | bytes 2621440 | tf_op jit(solution)/shard_map/all_gather | solution.py:110
  14.1 11.4 %copy-start.18 = (f32[4]{0:T(128)S(1)}, f32[4]{0:T(128)}, u32[]{:S(2)}) copy-start(f32[4]{0:T(128)} %param.16) | copy-start | bytes 52
  14.1 55.8 %all-to-all-start = ((bf16[8,8,32,512]{3,1,2,0:T(8,128)(2,1)}), bf16[8,8,32,512]{3,1,2,0:T(8,128)(2,1)}, u32[]{:S(2)}, u32[]{:S(2)}) async-start(bf16[8,8,32,512]{3,1,2,0:T(8,128)(2,1)} %bitcast.166), calls=%async_computation | async-start | bytes 4194304 | tf_op jit(solution)/shard_map/all_to_all | solution.py:103
  23.1 11.7 %copy-start.7 = (s32[512,512]{0,1:T(8,128)}, s32[512,512]{0,1:T(8,128)S(1)}, u32[]{:S(2)}) copy-start(s32[512,512]{0,1:T(8,128)S(1)} %copy.99) | copy-start | bytes 3145732
  27.5 1.9 copy-start.5
  34.9 4.2 %copy-start.6 = (f32[4,512,512]{1,2,0:T(8,128)S(1)}, f32[4,512,512]{1,2,0:T(8,128)}, u32[]{:S(2)}) copy-start(f32[4,512,512]{1,2,0:T(8,128)} %copy-done.5) | copy-start | bytes 12582916
  34.9 4.2 %copy-start.17 = (bf16[512,512]{1,0:T(8,128)(2,1)S(1)}, bf16[512,512]{1,0:T(8,128)(2,1)}, u32[]{:S(2)}) copy-start(bf16[512,512]{1,0:T(8,128)(2,1)} %param.12) | copy-start | bytes 1572868
  40.9 2.8 %copy-start.14 = (bf16[512,512]{1,0:T(8,128)(2,1)S(1)}, bf16[512,512]{1,0:T(8,128)(2,1)}, u32[]{:S(2)}) copy-start(bf16[512,512]{1,0:T(8,128)(2,1)} %param.11) | copy-start | bytes 1572868
  45.7 1.7 slice-start
  45.7 1.7 slice-start.1
  69.9 52.2 %all-to-all-start.1 = ((bf16[8,8,32,512]{3,1,2,0:T(8,128)(2,1)}), bf16[8,8,32,512]{3,1,2,0:T(8,128)(2,1)}, u32[]{:S(2)}, u32[]{:S(2)}) async-start(bf16[8,8,32,512]{3,1,2,0:T(8,128)(2,1)} %bitcast.167), calls=%async_computation.1 | async-start | bytes 4194304 | tf_op jit(solution)/shard_map/all_to_all | solution.py:103
  74.3 196.3 %reduce-scatter.2.cloned.1.call-start = ((), (), s32[]{:S(2)}) async-start(), calls=%async_computation.6 | async-start | bytes 5242880 | tf_op jit(solution)/shard_map/reduce_scatter | solution.py:170
  85.2 2.0 copy-start.1
  131.8 2.5 copy-start.16
  133.6 2.0 copy-start.3
  133.6 2.0 copy-start.12
  135.6 2.4 copy-start.2
  135.6 2.5 copy-start.15
  137.4 1.6 copy-start.13
  162.4 52.5 %all-to-all-start.3 = ((bf16[8,8,32,512]{3,1,2,0:T(8,128)(2,1)}), bf16[8,8,32,512]{3,1,2,0:T(8,128)(2,1)}, u32[]{:S(2)}, u32[]{:S(2)}) async-start(bf16[8,8,32,512]{3,1,2,0:T(8,128)(2,1)} %bitcast.169), calls=%async_computation.4 | async-start | bytes 4194304 | tf_op jit(solution)/shard_map/all_to_all | solution.py:156
  175.1 4.0 %copy-start.10 = (bf16[512,512]{0,1:T(8,128)(2,1)S(1)}, bf16[512,512]{0,1:T(8,128)(2,1)}, u32[]{:S(2)}) copy-start(bf16[512,512]{0,1:T(8,128)(2,1)} %copy.90) | copy-start | bytes 1572868
  214.9 52.3 %all-to-all-start.2 = ((bf16[8,8,32,512]{3,1,2,0:T(8,128)(2,1)}), bf16[8,8,32,512]{3,1,2,0:T(8,128)(2,1)}, u32[]{:S(2)}, u32[]{:S(2)}) async-start(bf16[8,8,32,512]{3,1,2,0:T(8,128)(2,1)} %bitcast.168), calls=%async_computation.3 | async-start | bytes 4194304 | tf_op jit(solution)/shard_map/all_to_all | solution.py:156
  225.6 5.1 %copy-start.4 = (f32[512,4,128]{2,0,1:T(8,128)S(1)}, f32[512,4,128]{2,0,1:T(8,128)}, u32[]{:S(2)}) copy-start(f32[512,4,128]{2,0,1:T(8,128)} %convolution_bitcast_fusion.1) | copy-start | bytes 3145732
  (3 other events, 3.9 us)
Sparse Core Ops, SparseCore 0:
  9.5 25.2 all-gather.1
  143.0 43.4 reduce-scatter.1

commit v3 on v2

--- a/solution.py
+++ b/solution.py
@@ -1,6 +1,10 @@
+import functools
+
 import jax
 import jax.numpy as jnp
 from jax import lax
+from jax.experimental import pallas as pl
+from jax.experimental.pallas import tpu as pltpu
 from jax.sharding import PartitionSpec as P
 
 QBLK = 512
@@ -10,32 +14,68 @@
 keep_scale = 1.0 / 0.9
 
 
-def mm(spec, left, right):
-    return jnp.einsum(spec, left, right, preferred_element_type=jnp.float32)
-
-
-def branch(query_rows, keyset, valueset, grad_mixed, causal, score_scale):
-    scores = mm("thd,khd->htk", query_rows, keyset) * score_scale
+def _branch_kernel(q_ref, k_ref, v_ref, g_ref, o_ref, dq_ref, dk_ref, dv_ref, *, causal, score_scale):
+    q = q_ref[...]
+    k = k_ref[...]
+    v = v_ref[...]
+    g = g_ref[...]
+    scores = lax.dot_general(
+        q, k, (((1,), (1,)), ((), ())), preferred_element_type=jnp.float32
+    ) * score_scale
     if causal:
-        row_iota = lax.broadcasted_iota(jnp.int32, scores.shape, 1)
-        col_iota = lax.broadcasted_iota(jnp.int32, scores.shape, 2)
-        scores = jnp.where(col_iota <= row_iota, scores, -jnp.inf)
-    weights = jnp.exp(scores - jnp.max(scores, axis=2, keepdims=True))
-    row_total = jnp.sum(weights, axis=2, keepdims=True)
-    mixed_out = mm("htk,khd->htd", weights.astype(jnp.bfloat16), valueset) / row_total
-    return weights, row_total, mixed_out
-
-
-def branch_grads(query_rows, keyset, valueset, weights, row_total, mixed_out, grad_mixed, score_scale):
-    probabilities = weights / row_total
-    delta_rows = jnp.sum(grad_mixed * mixed_out, axis=2, keepdims=True)
-    grad_low = grad_mixed.astype(jnp.bfloat16)
-    grad_probs = mm("htd,khd->htk", grad_low, valueset)
-    grad_scores = (probabilities * (grad_probs - delta_rows) * score_scale).astype(jnp.bfloat16)
-    grad_query = mm("htk,khd->thd", grad_scores, keyset)
-    grad_keyset = mm("htk,thd->khd", grad_scores, query_rows)
-    grad_valueset = mm("htk,htd->khd", probabilities.astype(jnp.bfloat16), grad_low)
-    return grad_query, grad_keyset, grad_valueset
+        row = lax.broadcasted_iota(jnp.int32, scores.shape, 0)
+        col = lax.broadcasted_iota(jnp.int32, scores.shape, 1)
+        scores = jnp.where(col <= row, scores, -jnp.inf)
+    weights = jnp.exp(scores - jnp.max(scores, axis=1, keepdims=True))
+    total = jnp.sum(weights, axis=1, keepdims=True)
+    mixed = jnp.dot(weights.astype(jnp.bfloat16), v, preferred_element_type=jnp.float32) / total
+    o_ref[...] = mixed
+    probs = weights / total
+    delta = jnp.sum(g * mixed, axis=1, keepdims=True)
+    g_low = g.astype(jnp.bfloat16)
+    grad_probs = lax.dot_general(
+        g_low, v, (((1,), (1,)), ((), ())), preferred_element_type=jnp.float32
+    )
+    ds = (probs * (grad_probs - delta) * score_scale).astype(jnp.bfloat16)
+    dq_ref[...] = jnp.dot(ds, k, preferred_element_type=jnp.float32)
+    dk_ref[...] = lax.dot_general(
+        ds, q, (((0,), (0,)), ((), ())), preferred_element_type=jnp.float32
+    ).astype(dk_ref.dtype)
+    dv_ref[...] = lax.dot_general(
+        probs.astype(jnp.bfloat16), g_low, (((0,), (0,)), ((), ())),
+        preferred_element_type=jnp.float32,
+    ).astype(dv_ref.dtype)
+
+
+def attention_branch(q, g, k, v, heads, head_dim, causal, q_off=0, k_off=0, v_off=0):
+    rows = q.shape[0]
+    keys = k.shape[0]
+    cols = heads * head_dim
+    kernel = functools.partial(_branch_kernel, causal=causal, score_scale=head_dim ** (-0.5))
+
+    def spec(length, offset):
+        return pl.BlockSpec((length, head_dim), lambda h: (0, h + offset))
+
+    out_row = pl.BlockSpec((rows, head_dim), lambda h: (0, h))
+    out_key = pl.BlockSpec((keys, head_dim), lambda h: (0, h))
+    return pl.pallas_call(
+        kernel,
+        grid=(heads,),
+        in_specs=[spec(rows, q_off), spec(keys, k_off), spec(keys, v_off), spec(rows, q_off)],
+        out_specs=[out_row, out_row, out_key, out_key],
+        out_shape=[
+            jax.ShapeDtypeStruct((rows, cols), jnp.float32),
+            jax.ShapeDtypeStruct((rows, cols), jnp.float32),
+            jax.ShapeDtypeStruct((keys, cols), jnp.bfloat16),
+            jax.ShapeDtypeStruct((keys, cols), jnp.bfloat16),
+        ],
+        compiler_params=pltpu.CompilerParams(vmem_limit_bytes=48 * 1024 * 1024),
+        cost_estimate=pl.CostEstimate(
+            flops=12 * rows * keys * head_dim * heads,
+            transcendentals=rows * keys * heads,
+            bytes_accessed=rows * cols * 14 + keys * cols * 8,
+        ),
+    )(q, k, v, g)
 
 
 def per_device(
@@ -82,12 +122,8 @@
     serve_table = (send_local.reshape(slot_count, 1) == block_iota).astype(jnp.bfloat16)
 
     gate_values = 1.0 / (1.0 + jnp.exp(-gate_logit))
-    gate_col = gate_values[None, :, None]
+    gate_cols = jnp.repeat(gate_values, head_dim)[None, :]
     keep_mask = dropout_keep.astype(jnp.float32)
-
-    query_rows = queries.reshape(tok_rows, heads_here, head_dim)
-    key_rows = local_keys.reshape(tok_rows, heads_here, head_dim)
-    value_rows = local_values.reshape(tok_rows, heads_here, head_dim)
 
     chunk_heads = heads_here // CHUNKS if heads_here % CHUNKS == 0 else heads_here
     chunk_count = heads_here // chunk_heads
@@ -111,13 +147,11 @@
     grad_attended = lax.dot_general(
         cotangent_full, out_weight, (((1,), (1,)), ((), ())), preferred_element_type=jnp.float32
     ) * keep_mask * keep_scale
-    grad_heads = grad_attended.reshape(tok_rows, heads_here, head_dim)
-    grad_mem = (gate_col * grad_heads).transpose(1, 0, 2)
-    grad_loc = ((1.0 - gate_col) * grad_heads).transpose(1, 0, 2)
-
-    w_loc, l_loc, o_loc = branch(query_rows, key_rows, value_rows, grad_loc, True, score_scale)
-    q_loc, k_loc, v_loc = branch_grads(
-        query_rows, key_rows, value_rows, w_loc, l_loc, o_loc, grad_loc, score_scale
+    grad_mem = gate_cols * grad_attended
+    grad_loc = (1.0 - gate_cols) * grad_attended
+
+    o_loc, q_loc, k_loc, v_loc = attention_branch(
+        queries, grad_loc, local_keys, local_values, heads_here, head_dim, True
     )
 
     if chunk_count > 1:
@@ -128,28 +162,17 @@
     for chunk in range(chunk_count):
         if chunk + 1 < chunk_count:
             fetched.append(fetch(chunk + 1))
-        heads = slice(chunk * chunk_heads, (chunk + 1) * chunk_heads)
         chosen = jnp.dot(
             pick_table, fetched[chunk].reshape(slot_count, entries2),
             preferred_element_type=jnp.float32,
         ).astype(jnp.bfloat16).reshape(top_blocks * block_len, 2 * chunk_cols)
-        mem_keyset = chosen[:, :chunk_cols].reshape(-1, chunk_heads, head_dim)
-        mem_valueset = chosen[:, chunk_cols:].reshape(-1, chunk_heads, head_dim)
-        q_chunk = query_rows[:, heads]
-        g_chunk = grad_mem[heads]
-        w_mem, l_mem, o_mem = branch(q_chunk, mem_keyset, mem_valueset, g_chunk, False, score_scale)
-        q_mem, k_mem, v_mem = branch_grads(
-            q_chunk, mem_keyset, mem_valueset, w_mem, l_mem, o_mem, g_chunk, score_scale
+        o_mem, q_mem, k_mem, v_mem = attention_branch(
+            queries, grad_mem, chosen, chosen, chunk_heads, head_dim, False,
+            q_off=chunk * chunk_heads, k_off=0, v_off=chunk_heads,
         )
         o_mem_parts.append(o_mem)
         q_mem_parts.append(q_mem)
-        parts = jnp.concatenate(
-            [
-                k_mem.astype(jnp.bfloat16).reshape(top_blocks, block_len, chunk_cols),
-                v_mem.astype(jnp.bfloat16).reshape(top_blocks, block_len, chunk_cols),
-            ],
-            axis=2,
-        ).reshape(top_blocks, entries2)
+        parts = jnp.concatenate([k_mem, v_mem], axis=1).reshape(top_blocks, entries2)
         send = lax.dot_general(
             pick_table, parts, (((0,), (0,)), ((), ())), preferred_element_type=jnp.float32
         ).astype(jnp.bfloat16)
@@ -162,18 +185,18 @@
             preferred_element_type=jnp.float32,
         ).astype(jnp.bfloat16).reshape(blocks_here, block_len, 2 * chunk_cols))
 
-    o_mem = jnp.concatenate(o_mem_parts, axis=0)
+    o_mem = jnp.concatenate(o_mem_parts, axis=1)
     q_mem = jnp.concatenate(q_mem_parts, axis=1)
-    attended = (gate_col * o_mem.transpose(1, 0, 2) + (1.0 - gate_col) * o_loc.transpose(1, 0, 2))
-    dropped = (attended.reshape(tok_rows, feature_cols) * keep_mask * keep_scale).astype(jnp.bfloat16)
+    attended = gate_cols * o_mem + (1.0 - gate_cols) * o_loc
+    dropped = (attended * keep_mask * keep_scale).astype(jnp.bfloat16)
     partial_out = jnp.dot(dropped, out_weight, preferred_element_type=jnp.float32)
     layer_out = lax.psum_scatter(partial_out, "head", scatter_dimension=1, tiled=True).astype(
         jnp.bfloat16
     )
 
-    grad_queries = (q_mem + q_loc).astype(jnp.bfloat16).reshape(tok_rows, feature_cols)
-    grad_keys = k_loc.astype(jnp.bfloat16).reshape(tok_rows, feature_cols)
-    grad_values = v_loc.astype(jnp.bfloat16).reshape(tok_rows, feature_cols)
+    grad_queries = (q_mem + q_loc).astype(jnp.bfloat16)
+    grad_keys = k_loc
+    grad_values = v_loc
     grad_memory_keys = jnp.concatenate([s[:, :, :chunk_cols] for s in summed_parts], axis=2)
     grad_memory_values = jnp.concatenate([s[:, :, chunk_cols:] for s in summed_parts], axis=2)
     return (

time: 281 us -> 268 us (0.954)
  matrix products: 64 us -> 28.9 us
  waiting for transfers between devices: 120 us -> 147 us
  local copies, waits for them, and re-layouts: 49.2 us -> 26.2 us
  Pallas kernels: 0 us -> 18.4 us
    dot_general x18 -> x0, matrix products: 39 us -> none  [mm(): return jnp.einsum(spec, left, right, preferred_element_type=jnp.float32)]
    all_to_all x2, waiting for transfers between devices: 59.6 us -> 82.8 us  [per_device(): lax.all_to_all(send.reshape(mem_count, capacity, block_len, 2 * chunk_col...]
    pallas_call x0 -> x3, Pallas kernels: none -> 18.4 us  [attention_branch(): pl.pallas_call(kernel, grid=(heads,), in_specs=[spec(rows, q_off), spec(k...]
    convert_element_type x6 -> x0, local copies, waits for them, and re-layouts: 8.93 us -> none  [the longest x2 4.01 us: per_device(): v_mem.astype(jnp.bfloat16).reshape(top_blocks, block_len, chunk_cols)]
    all_gather x1, waiting for transfers between devices: 4.83 us -> 13.2 us  [per_device(): cotangent_full = lax.all_gather(cotangent, 'head', axis=1, tiled=True)]
    slice x4 -> x0, local copies, waits for them, and re-layouts: 6.14 us -> none  [the longest x2 3.09 us: per_device(): mem_keyset = chosen[:, :chunk_cols].reshape(-1, chunk_heads, head_dim)]
    unnamed x51 -> x50, local copies, waits for them, and re-layouts: 19.3 us -> 14.6 us
    all_to_all x2, waiting for transfers between devices: 54.4 us -> 50.1 us  [fetch(): lax.all_to_all(served.reshape(mem_count, capacity, block_len, 2 * chunk_c...]
  transfers between devices with their start and end apart: 6 -> 6, of which waited for: 5 -> 5; matrix products, arithmetic and copies ran while one was open for 35% -> 16% of each run, Pallas kernels for 0% -> 5%
where the time goes in v3:
time: 268 us; the launch traced here: 267 us
  waiting for transfers between devices  147 us (55%)
  matrix products  28.9 us (11%)
  local copies, waits for them, and re-layouts  26.2 us (10%)
  starting transfers between devices  20.8 us (8%)
  Pallas kernels  18.4 us (7%)
  between operations  14.3 us (5%)
  other arithmetic  11.7 us (4%)
    all_to_all x2, waiting for transfers between devices, per_device(): lax.all_to_all(send.reshape(mem_count, capacity, block_len, 2 * chunk_col...  82.8 us
    all_to_all x2, waiting for transfers between devices, fetch(): lax.all_to_all(served.reshape(mem_count, capacity, block_len, 2 * chunk_c...  50.1 us
    pallas_call x3, Pallas kernels, attention_branch(): pl.pallas_call(kernel, grid=(heads,), in_specs=[spec(rows, q_off), spec(k...  18.4 us
    unnamed x50, local copies, waits for them, and re-layouts  14.6 us
    all_gather x1, waiting for transfers between devices, per_device(): cotangent_full = lax.all_gather(cotangent, 'head', axis=1, tiled=True)  13.2 us
    all_to_all x2, starting transfers between devices, fetch(): lax.all_to_all(served.reshape(mem_count, capacity, block_len, 2 * chunk_c...  11.8 us
    all_to_all x2, starting transfers between devices, per_device(): lax.all_to_all(send.reshape(mem_count, capacity, block_len, 2 * chunk_col...  8.72 us
    dot_general x2, matrix products, per_device(): lax.dot_general(pick_table, parts, (((0,), (0,)), ((), ())), preferred_el...  7.2 us
  transfers between devices with their start and end apart: 6, of which 5 were waited for; matrix products, arithmetic and copies ran while one was open for 16% of the time, Pallas kernels for 5%

profile of v3, /device:TPU:0, one launch (start us, length us, event | category | flops | bytes accessed | tf_op | source)
XLA Modules:
  0.0 267.0 jit_solution(1236622551477152947)
XLA Ops:
  14.2 7.4 %all-to-all-start = ((bf16[8,8,32,512]{3,1,2,0:T(8,128)(2,1)}), bf16[8,8,32,512]{3,1,2,0:T(8,128)(2,1)}, u32[]{:S(2)}, u32[]{:S(2)}) async-start(bf16[8,8,32,512]{3,1,2,0:T(8,128)(2,1)} %bitcast.35), calls=%async_computation | async-start | bytes 4194304 | tf_op jit(solution)/shard_map/all_to_all | solution.py:139
  21.7 13.2 %all-gather.2.cloned.1.call-done = bf16[512,2048]{1,0:T(8,128)(2,1)} async-done(((bf16[512,512]{1,0:T(8,128)(2,1)}), bf16[512,2048]{1,0:T(8,128)(2,1)}) %all-gather.2.cloned.1.call-update) | async-done | bytes 2097168 | tf_op jit(solution)/shard_map/all_gather | solution.py:146
  34.9 4.0 %broadcast_multiply_fusion = (f32[512,512]{1,0:T(8,128)}, f32[512,512]{1,0:T(8,128)S(1)}) fusion(f32[512]{0:T(512)S(1)} %get-tuple-element.54, f32[512]{0:T(512)S(1)} %get-tuple-element.53, s32[512,512]{1,0:T(8,128)S(1)} %copy-done.20, bf16[512,2048]{1,0:T(8,128)(2,1)} %all-gather.2.cloned.1.call-done, bf16[512,2048]{1,0:T(8,128)(2,1)S(1)} %copy-done), kind=kOutput, calls=%fused_computation.25 | convolution fusion | flops 1074790400 | bytes 7344128 | tf_op jit(solution)/shard_map/dot_general | solution.py:147
  38.9 7.3 %shard_map.145 = (f32[512,512]{1,0:T(8,128)S(1)}, f32[512,512]{1,0:T(8,128)S(1)}, bf16[512,512]{1,0:T(8,128)(2,1)}, bf16[512,512]{1,0:T(8,128)(2,1)}) custom-call(bf16[512,512]{1,0:T(8,128)(2,1)S(1)} %copy-done.15, bf16[512,512]{1,0:T(8,128)(2,1)S(1)} %copy-done.13, bf16[512,512]{1,0:T(8,128)(2,1)S(1)} %copy-done.14, f32[512,512]{1,0:T(8,128)S(1)} %get-tuple-element.47.g_ref), custom_call_target="tpu_custom_call" | custom-call | flops 1610612736 | bytes 5767168 | tf_op jit(solution)/shard_map/pallas_call | solution.py:61
  49.7 20.2 %all-to-all-done = bf16[8,8,32,512]{3,1,2,0:T(8,128)(2,1)} async-done(((bf16[8,8,32,512]{3,1,2,0:T(8,128)(2,1)}), bf16[8,8,32,512]{3,1,2,0:T(8,128)(2,1)}, u32[]{:S(2)}, u32[]{:S(2)}) %all-to-all-start) | async-done | bytes 2097184 | tf_op jit(solution)/shard_map/all_to_all | solution.py:139
  69.9 4.4 %all-to-all-start.1 = ((bf16[8,8,32,512]{3,1,2,0:T(8,128)(2,1)}), bf16[8,8,32,512]{3,1,2,0:T(8,128)(2,1)}, u32[]{:S(2)}, u32[]{:S(2)}) async-start(bf16[8,8,32,512]{3,1,2,0:T(8,128)(2,1)} %bitcast.36), calls=%async_computation.1 | async-start | bytes 4194304 | tf_op jit(solution)/shard_map/all_to_all | solution.py:139
  74.6 3.1 %convolution_convert_fusion.5 = bf16[32,16384]{1,0:T(8,128)(2,1)} fusion(bf16[64,16384]{1,0:T(8,128)(2,1)} %bitcast.3, s32[32]{0:T(128)S(1)} %add_bitcast_fusion), kind=kOutput, calls=%fused_computation.5 | convolution fusion | flops 67635200 | bytes 3145856 | tf_op jit(solution)/shard_map/dot_general | solution.py:165
  77.7 2.4 reshape.106.k_ref.v_ref
  83.5 5.6 %shard_map.146 = (f32[512,256]{1,0:T(8,128)S(1)}, f32[512,256]{1,0:T(8,128)S(1)}, bf16[1024,256]{1,0:T(8,128)(2,1)S(1)}, bf16[1024,256]{1,0:T(8,128)(2,1)S(1)}) custom-call(bf16[512,512]{1,0:T(8,128)(2,1)S(1)} %copy-done.16, bf16[1024,512]{1,0:T(8,128)(2,1)S(1)} %copy-done.2, bf16[1024,512]{1,0:T(8,128)(2,1)S(1)} %copy-done.2, f32[512,512]{1,0:T(8,128)S(1)} %copy-done.18), custom_call_target="tpu_custom_call" | custom-call | flops 1610612736 | bytes 3932160 | tf_op jit(solution)/shard_map/pallas_call | solution.py:61
  92.3 29.8 %all-to-all-done.1 = bf16[8,8,32,512]{3,1,2,0:T(8,128)(2,1)} async-done(((bf16[8,8,32,512]{3,1,2,0:T(8,128)(2,1)}), bf16[8,8,32,512]{3,1,2,0:T(8,128)(2,1)}, u32[]{:S(2)}, u32[]{:S(2)}) %all-to-all-start.1) | async-done | bytes 2097184 | tf_op jit(solution)/shard_map/all_to_all | solution.py:139
  122.1 3.1 %convolution_convert_fusion.4 = bf16[32,16384]{1,0:T(8,128)(2,1)} fusion(bf16[64,16384]{1,0:T(8,128)(2,1)} %bitcast.5, s32[32]{0:T(128)S(1)} %add_bitcast_fusion), kind=kOutput, calls=%fused_computation.4 | convolution fusion | flops 67635200 | bytes 3145856 | tf_op jit(solution)/shard_map/dot_general | solution.py:165
  125.2 2.4 reshape.110.k_ref.v_ref
  131.0 5.5 %shard_map.147 = (f32[512,256]{1,0:T(8,128)S(1)}, f32[512,256]{1,0:T(8,128)S(1)}, bf16[1024,256]{1,0:T(8,128)(2,1)S(1)}, bf16[1024,256]{1,0:T(8,128)(2,1)S(1)}) custom-call(bf16[512,512]{1,0:T(8,128)(2,1)S(1)} %copy-done.17, bf16[1024,512]{1,0:T(8,128)(2,1)S(1)} %copy-done.1, bf16[1024,512]{1,0:T(8,128)(2,1)S(1)} %copy-done.1, f32[512,512]{1,0:T(8,128)S(1)} %copy-done.19), custom_call_target="tpu_custom_call" | custom-call | flops 1610612736 | bytes 3932160 | tf_op jit(solution)/shard_map/pallas_call | solution.py:61
  139.0 3.2 %fusion.5 = f32[512,2048]{1,0:T(8,128)} fusion(bf16[512,2048]{1,0:T(8,128)(2,1)S(1)} %copy-done, f32[512,256]{1,0:T(8,128)S(1)} %get-tuple-element.33, f32[512,256]{1,0:T(8,128)S(1)} %copy-done.12, f32[512,512]{1,0:T(8,128)S(1)} %copy-done.4, s32[512,512]{1,0:T(8,128)S(1)} %copy-done.21, f32[512]{0:T(512)S(1)} %get-tuple-element.52, ...), kind=kOutput, calls=%fused_computation.18 | convolution fusion | flops 1075838976 | bytes 9441280 | tf_op jit(solution)/shard_map/dot_general | solution.py:192
  142.2 2.3 pad_maximum_fusion
  144.5 2.4 reshape.111
  146.9 3.5 %convolution_convert_fusion.1 = bf16[64,16384]{1,0:T(8,128)(2,1)} fusion(bf16[32,16384]{1,0:T(8,128)(2,1)} %reshape.111, s32[32]{0:T(128)S(1)} %add_bitcast_fusion), kind=kOutput, calls=%fused_computation.1 | convolution fusion | flops 68159488 | bytes 3145856 | tf_op jit(solution)/shard_map/dot_general | solution.py:176
  150.4 4.4 %all-to-all-start.2 = ((bf16[8,8,32,512]{3,1,2,0:T(8,128)(2,1)}), bf16[8,8,32,512]{3,1,2,0:T(8,128)(2,1)}, u32[]{:S(2)}, u32[]{:S(2)}) async-start(bf16[8,8,32,512]{3,1,2,0:T(8,128)(2,1)} %bitcast.38), calls=%async_computation.3 | async-start | bytes 4194304 | tf_op jit(solution)/shard_map/all_to_all | solution.py:179
  154.8 2.3 pad_maximum_fusion.1
  157.0 2.4 reshape.115
  159.4 3.7 %convolution_convert_fusion = bf16[64,16384]{1,0:T(8,128)(2,1)} fusion(bf16[32,16384]{1,0:T(8,128)(2,1)} %reshape.115, s32[32]{0:T(128)S(1)} %add_bitcast_fusion), kind=kOutput, calls=%fused_computation | convolution fusion | flops 68159488 | bytes 3145856 | tf_op jit(solution)/shard_map/dot_general | solution.py:176
  163.1 39.4 %all-to-all-done.2 = bf16[8,8,32,512]{3,1,2,0:T(8,128)(2,1)} async-done(((bf16[8,8,32,512]{3,1,2,0:T(8,128)(2,1)}), bf16[8,8,32,512]{3,1,2,0:T(8,128)(2,1)}, u32[]{:S(2)}, u32[]{:S(2)}) %all-to-all-start.2) | async-done | bytes 2097184 | tf_op jit(solution)/shard_map/all_to_all | solution.py:179
  202.5 4.4 %all-to-all-start.3 = ((bf16[8,8,32,512]{3,1,2,0:T(8,128)(2,1)}), bf16[8,8,32,512]{3,1,2,0:T(8,128)(2,1)}, u32[]{:S(2)}, u32[]{:S(2)}) async-start(bf16[8,8,32,512]{3,1,2,0:T(8,128)(2,1)} %bitcast.37), calls=%async_computation.4 | async-start | bytes 4194304 | tf_op jit(solution)/shard_map/all_to_all | solution.py:179
  211.4 43.3 %all-to-all-done.3 = bf16[8,8,32,512]{3,1,2,0:T(8,128)(2,1)} async-done(((bf16[8,8,32,512]{3,1,2,0:T(8,128)(2,1)}), bf16[8,8,32,512]{3,1,2,0:T(8,128)(2,1)}, u32[]{:S(2)}, u32[]{:S(2)}) %all-to-all-start.3) | async-done | bytes 2097184 | tf_op jit(solution)/shard_map/all_to_all | solution.py:179
  (83 shorter events, 33.3 us)
Async XLA Ops:
  7.2 27.7 %copy-start = (bf16[512,2048]{1,0:T(8,128)(2,1)S(1)}, bf16[512,2048]{1,0:T(8,128)(2,1)}, u32[]{:S(2)}) copy-start(bf16[512,2048]{1,0:T(8,128)(2,1)} %param.18) | copy-start | bytes 6291460
  7.2 27.7 %all-gather.2.cloned.1.call-start = ((), (), s32[]{:S(2)}) async-start(), calls=%async_computation.5 | async-start | bytes 2621440 | tf_op jit(solution)/shard_map/all_gather | solution.py:146
  14.1 7.4 %copy-start.22 = (f32[4]{0:T(128)S(1)}, f32[4]{0:T(128)}, u32[]{:S(2)}) copy-start(f32[4]{0:T(128)} %param.16) | copy-start | bytes 52
  14.1 20.7 %copy-start.20 = (s32[512,512]{1,0:T(8,128)S(1)}, s32[512,512]{1,0:T(8,128)}, u32[]{:S(2)}) copy-start(s32[512,512]{1,0:T(8,128)} %param.17) | copy-start | bytes 3145732
  14.2 55.8 %all-to-all-start = ((bf16[8,8,32,512]{3,1,2,0:T(8,128)(2,1)}), bf16[8,8,32,512]{3,1,2,0:T(8,128)(2,1)}, u32[]{:S(2)}, u32[]{:S(2)}) async-start(bf16[8,8,32,512]{3,1,2,0:T(8,128)(2,1)} %bitcast.35), calls=%async_computation | async-start | bytes 4194304 | tf_op jit(solution)/shard_map/all_to_all | solution.py:139
  34.9 4.0 %copy-start.13 = (bf16[512,512]{1,0:T(8,128)(2,1)S(1)}, bf16[512,512]{1,0:T(8,128)(2,1)}, u32[]{:S(2)}) copy-start(bf16[512,512]{1,0:T(8,128)(2,1)} %k_ref.1) | copy-start | bytes 1572868
  34.9 4.0 %copy-start.14 = (bf16[512,512]{1,0:T(8,128)(2,1)S(1)}, bf16[512,512]{1,0:T(8,128)(2,1)}, u32[]{:S(2)}) copy-start(bf16[512,512]{1,0:T(8,128)(2,1)} %v_ref.1) | copy-start | bytes 1572868
  34.9 4.0 %copy-start.15 = (bf16[512,512]{1,0:T(8,128)(2,1)S(1)}, bf16[512,512]{1,0:T(8,128)(2,1)}, u32[]{:S(2)}) copy-start(bf16[512,512]{1,0:T(8,128)(2,1)} %q_ref.5) | copy-start | bytes 1572868
  38.9 8.4 %slice-start = ((bf16[16,32,512]{2,1,0:T(8,128)(2,1)}), bf16[16,32,256]{2,1,0:T(8,128)(2,1)S(1)}, s32[]{:S(2)}) async-start(bf16[16,32,512]{2,1,0:T(8,128)(2,1)} %param.13), calls=%async_computation.7 | async-start | bytes 524288 | tf_op jit(solution)/shard_map/slice | solution.py:135
  38.9 8.4 %slice-start.1 = ((bf16[16,32,512]{2,1,0:T(8,128)(2,1)}), bf16[16,32,256]{2,1,0:T(8,128)(2,1)S(1)}, s32[]{:S(2)}) async-start(bf16[16,32,512]{2,1,0:T(8,128)(2,1)} %param.14), calls=%async_computation.8 | async-start | bytes 524288 | tf_op jit(solution)/shard_map/slice | solution.py:135
  46.2 1.1 copy-start.3
  69.9 52.2 %all-to-all-start.1 = ((bf16[8,8,32,512]{3,1,2,0:T(8,128)(2,1)}), bf16[8,8,32,512]{3,1,2,0:T(8,128)(2,1)}, u32[]{:S(2)}, u32[]{:S(2)}) async-start(bf16[8,8,32,512]{3,1,2,0:T(8,128)(2,1)} %bitcast.36), calls=%async_computation.1 | async-start | bytes 4194304 | tf_op jit(solution)/shard_map/all_to_all | solution.py:139
  74.3 183.8 %reduce-scatter.2.cloned.1.call-start = ((), (), s32[]{:S(2)}) async-start(), calls=%async_computation.6 | async-start | bytes 5242880 | tf_op jit(solution)/shard_map/reduce_scatter | solution.py:193
  80.0 1.2 copy-start.2
  81.3 1.0 copy-start.16
  82.3 1.2 copy-start.18
  127.5 1.2 copy-start.1
  128.8 1.0 copy-start.17
  129.8 1.2 copy-start.19
  131.0 7.9 %copy-start.4 = (f32[512,512]{1,0:T(8,128)S(1)}, f32[512,512]{1,0:T(8,128)}, u32[]{:S(2)}) copy-start(f32[512,512]{1,0:T(8,128)} %copy-done.3) | copy-start | bytes 3145732
  131.0 7.9 %copy-start.12 = (f32[512,256]{1,0:T(8,128)S(1)}, f32[512,256]{1,0:T(8,128)}, u32[]{:S(2)}) copy-start(f32[512,256]{1,0:T(8,128)} %copy-done.11) | copy-start | bytes 1572868
  131.0 7.9 %copy-start.21 = (s32[512,512]{1,0:T(8,128)S(1)}, s32[512,512]{1,0:T(8,128)}, u32[]{:S(2)}) copy-start(s32[512,512]{1,0:T(8,128)} %param.17) | copy-start | bytes 3145732
  150.4 52.1 %all-to-all-start.2 = ((bf16[8,8,32,512]{3,1,2,0:T(8,128)(2,1)}), bf16[8,8,32,512]{3,1,2,0:T(8,128)(2,1)}, u32[]{:S(2)}, u32[]{:S(2)}) async-start(bf16[8,8,32,512]{3,1,2,0:T(8,128)(2,1)} %bitcast.38), calls=%async_computation.3 | async-start | bytes 4194304 | tf_op jit(solution)/shard_map/all_to_all | solution.py:179
  202.5 52.2 %all-to-all-start.3 = ((bf16[8,8,32,512]{3,1,2,0:T(8,128)(2,1)}), bf16[8,8,32,512]{3,1,2,0:T(8,128)(2,1)}, u32[]{:S(2)}, u32[]{:S(2)}) async-start(bf16[8,8,32,512]{3,1,2,0:T(8,128)(2,1)} %bitcast.37), calls=%async_computation.4 | async-start | bytes 4194304 | tf_op jit(solution)/shard_map/all_to_all | solution.py:179
  (7 other events, 5.6 us)
Sparse Core Ops, SparseCore 0:
  9.5 25.2 all-gather.1
  142.4 43.4 reduce-scatter.1

commit v4 on v3

--- a/solution.py
+++ b/solution.py
@@ -6,6 +6,7 @@
 from jax.experimental import pallas as pl
 from jax.experimental.pallas import tpu as pltpu
 from jax.sharding import PartitionSpec as P
+
 
 QBLK = 512
 CHUNKS = 2
@@ -95,7 +96,6 @@
     tok_rows, feature_cols = queries.shape
     heads_here = gate_logit.shape[0]
     head_dim = feature_cols // heads_here
-    score_scale = head_dim ** (-0.5)
     blocks_here = memory_keys.shape[0]
     block_len = memory_keys.shape[1]
     query_blocks = tok_rows // QBLK
@@ -112,12 +112,13 @@
     owner_rank = jnp.sum((same_owner & earlier_mask[None]).astype(jnp.int32), axis=1)
     request_owner = lax.dynamic_index_in_dim(owner_ids, mem_index, 0, keepdims=False)
     request_rank = lax.dynamic_index_in_dim(owner_rank, mem_index, 0, keepdims=False)
-    request_slot = request_owner * capacity + request_rank
+    request_slot = ((mem_index - request_owner) % mem_count) * capacity + request_rank
     slot_iota = lax.broadcasted_iota(jnp.int32, (request_count, slot_count), 1)
     pick_table = (request_slot[:, None] == slot_iota).astype(jnp.bfloat16)
     cap_iota = lax.broadcasted_iota(jnp.int32, (mem_count, request_count, capacity), 2)
     wanted = (owner_ids[:, :, None] == mem_index) & (owner_rank[:, :, None] == cap_iota)
     send_local = jnp.sum(wanted.astype(jnp.int32) * (local_ids[:, :, None] + 1), axis=1) - 1
+    send_local = jnp.roll(send_local, -mem_index, axis=0)
     block_iota = lax.broadcasted_iota(jnp.int32, (slot_count, blocks_here), 1)
     serve_table = (send_local.reshape(slot_count, 1) == block_iota).astype(jnp.bfloat16)
 
@@ -129,6 +130,13 @@
     chunk_count = heads_here // chunk_heads
     chunk_cols = chunk_heads * head_dim
     entries2 = block_len * 2 * chunk_cols
+
+    def exchange(buffer, sign):
+        pieces = [buffer[0]]
+        for shift in range(1, mem_count):
+            pairs = [(i, (i + sign * shift) % mem_count) for i in range(mem_count)]
+            pieces.append(lax.ppermute(buffer[shift], "mem", pairs))
+        return jnp.stack(pieces)
 
     def fetch(chunk):
         cols = slice(chunk * chunk_cols, (chunk + 1) * chunk_cols)
@@ -136,10 +144,7 @@
         served = jnp.dot(
             serve_table, both.reshape(blocks_here, entries2), preferred_element_type=jnp.float32
         ).astype(jnp.bfloat16)
-        return lax.all_to_all(
-            served.reshape(mem_count, capacity, block_len, 2 * chunk_cols),
-            "mem", split_axis=0, concat_axis=0, tiled=True,
-        )
+        return exchange(served.reshape(mem_count, capacity, block_len, 2 * chunk_cols), 1)
 
     fetched = [fetch(0)]
 
@@ -176,10 +181,9 @@
         send = lax.dot_general(
             pick_table, parts, (((0,), (0,)), ((), ())), preferred_element_type=jnp.float32
         ).astype(jnp.bfloat16)
-        returned = lax.all_to_all(
-            send.reshape(mem_count, capacity, block_len, 2 * chunk_cols),
-            "mem", split_axis=0, concat_axis=0, tiled=True,
-        )
+        if chunk + 1 < chunk_count:
+            send, fetched[chunk + 1] = lax.optimization_barrier((send, fetched[chunk + 1]))
+        returned = exchange(send.reshape(mem_count, capacity, block_len, 2 * chunk_cols), -1)
         summed_parts.append(lax.dot_general(
             serve_table, returned.reshape(slot_count, entries2), (((0,), (0,)), ((), ())),
             preferred_element_type=jnp.float32,

time: 268 us -> 274 us (1.022)
  starting transfers between devices: 20.8 us -> 96 us
  waiting for transfers between devices: 147 us -> 91.2 us
  matrix products: 28.9 us -> 15.2 us
    all_to_all x4 -> x0, waiting for transfers between devices: 133 us -> none  [the longest x2 82.8 us: per_device(): lax.all_to_all(send.reshape(mem_count, capacity, block_len, 2 * chunk_col...]
    ppermute x0 -> x28, starting transfers between devices: none -> 95.9 us  [exchange(): pieces.append(lax.ppermute(buffer[shift], 'mem', pairs))]
    ppermute x0 -> x28, waiting for transfers between devices: none -> 90.5 us  [exchange(): pieces.append(lax.ppermute(buffer[shift], 'mem', pairs))]
    all_to_all x4 -> x0, starting transfers between devices: 20.5 us -> none  [the longest x2 11.8 us: fetch(): lax.all_to_all(served.reshape(mem_count, capacity, block_len, 2 * chunk_c...]
    all_gather x1, waiting for transfers between devices: 13.2 us -> 0.01 us  [per_device(): cotangent_full = lax.all_gather(cotangent, 'head', axis=1, tiled=True)]
    dot_general x2, matrix products: 6.12 us -> 1.96 us  [per_device(): jnp.dot(pick_table, fetched[chunk].reshape(slot_count, entries2), preferr...]
    dot_general x2, matrix products: 4.2 us -> 1.02 us  [per_device(): lax.dot_general(serve_table, returned.reshape(slot_count, entries2), (((0...]
    dot_general x2, matrix products: 7.2 us -> 4.22 us  [per_device(): lax.dot_general(pick_table, parts, (((0,), (0,)), ((), ())), preferred_el...]
  transfers between devices with their start and end apart: 6 -> 30, of which waited for: 5 -> 12; matrix products, arithmetic and copies ran while one was open for 16% -> 9% of each run, Pallas kernels for 5% -> 0%
where the time goes in v4:
time: 274 us; the launch traced here: 273 us
  starting transfers between devices  96 us (35%)
  waiting for transfers between devices  91.2 us (33%)
  local copies, waits for them, and re-layouts  28.3 us (10%)
  Pallas kernels  18.4 us (7%)
  matrix products  15.2 us (6%)
  between operations  14.7 us (5%)
  other arithmetic  9.41 us (3%)
    ppermute x28, starting transfers between devices, exchange(): pieces.append(lax.ppermute(buffer[shift], 'mem', pairs))  95.9 us
    ppermute x28, waiting for transfers between devices, exchange(): pieces.append(lax.ppermute(buffer[shift], 'mem', pairs))  90.5 us
    pallas_call x3, Pallas kernels, attention_branch(): pl.pallas_call(kernel, grid=(heads,), in_specs=[spec(rows, q_off), spec(k...  18.4 us
    unnamed x78, local copies, waits for them, and re-layouts  15.3 us
  transfers between devices with their start and end apart: 30, of which 12 were waited for; matrix products, arithmetic and copies ran while one was open for 9% of the time, Pallas kernels for 0%

profile of v4, /device:TPU:0, one launch (start us, length us, event | category | flops | bytes accessed | tf_op | source)
XLA Modules:
  0.0 273.2 jit_solution(1231129212130382345)
XLA Ops:
  13.8 3.0 %collective-permute-start = (bf16[8,32,512]{2,0,1:T(8,128)(2,1)}, bf16[8,32,512]{2,0,1:T(8,128)(2,1)}, u32[]{:S(2)}, u32[]{:S(2)}) collective-permute-start(bf16[8,32,512]{2,0,1:T(8,128)(2,1)} %bitcast.4), channel_id=1, source_target_pairs={{0,4},{4,8},{8,12},{12,16},{16,20},{20,24},{24,28},{28,0},{1,5},{5... | collective-permute-start | bytes 786440 | tf_op jit(solution)/shard_map/ppermute | solution.py:138
  18.4 2.5 collective-permute-start.2
  22.2 2.6 collective-permute-start.4
  30.3 3.9 %collective-permute-start.6 = (bf16[8,32,512]{2,0,1:T(8,128)(2,1)S(1)}, bf16[8,32,512]{2,0,1:T(8,128)(2,1)S(1)}, u32[]{:S(2)}, u32[]{:S(2)}) collective-permute-start(bf16[8,32,512]{2,0,1:T(8,128)(2,1)S(1)} %bitcast.150), channel_id=1, source_target_pairs={{0,28},{4,0},{8,4},{12,8},{16,12},{20,16},{24,20},{28,24},{1,29},{... | collective-permute-start | bytes 786440 | tf_op jit(solution)/shard_map/ppermute | solution.py:138
  35.1 14.0 %collective-permute-done.2 = bf16[8,32,512]{2,0,1:T(8,128)(2,1)} collective-permute-done((bf16[8,32,512]{2,0,1:T(8,128)(2,1)}, bf16[8,32,512]{2,0,1:T(8,128)(2,1)}, u32[]{:S(2)}, u32[]{:S(2)}) %collective-permute-start.2) | collective-permute-done | bytes 262176 | tf_op jit(solution)/shard_map/ppermute | solution.py:138
  53.9 3.3 %broadcast_multiply_fusion = (f32[512,512]{1,0:T(8,128)S(1)}, f32[512,512]{1,0:T(8,128)S(1)}) fusion(f32[512]{0:T(512)S(1)} %get-tuple-element.90, f32[512]{0:T(512)S(1)} %get-tuple-element.89, s32[512,512]{1,0:T(8,128)} %param.17, bf16[512,2048]{1,0:T(8,128)(2,1)} %all-gather.2.cloned.1.call-done, bf16[512,2048]{1,0:T(8,128)(2,1)S(1)} %copy-done), kind=kOutput, calls=%fused_computation.25 | convolution fusion | flops 1074790400 | bytes 7344128 | tf_op jit(solution)/shard_map/dot_general | solution.py:152
  57.3 7.3 %shard_map.145 = (f32[512,512]{1,0:T(8,128)S(1)}, f32[512,512]{1,0:T(8,128)S(1)}, bf16[512,512]{1,0:T(8,128)(2,1)}, bf16[512,512]{1,0:T(8,128)(2,1)}) custom-call(bf16[512,512]{1,0:T(8,128)(2,1)S(1)} %copy-done.15, bf16[512,512]{1,0:T(8,128)(2,1)S(1)} %copy-done.13, bf16[512,512]{1,0:T(8,128)(2,1)S(1)} %copy-done.14, f32[512,512]{1,0:T(8,128)S(1)} %get-tuple-element.83.g_ref), custom_call_target="tpu_custom_call" | custom-call | flops 1610612736 | bytes 5767168 | tf_op jit(solution)/shard_map/pallas_call | solution.py:62
  65.6 5.6 %shard_map.146 = (f32[512,256]{1,0:T(8,128)S(1)}, f32[512,256]{1,0:T(8,128)S(1)}, bf16[1024,256]{1,0:T(8,128)(2,1)S(1)}, bf16[1024,256]{1,0:T(8,128)(2,1)S(1)}) custom-call(bf16[512,512]{1,0:T(8,128)(2,1)S(1)} %copy-done.15, bf16[1024,512]{1,0:T(8,128)(2,1)S(1)} %copy-done.1, bf16[1024,512]{1,0:T(8,128)(2,1)S(1)} %copy-done.1, ...), custom_call_target="tpu_custom_call" | custom-call | flops 1610612736 | bytes 3932160 | tf_op jit(solution)/shard_map/pallas_call | solution.py:62
  78.4 5.5 %collective-permute-start.7 = (bf16[8,32,512]{2,0,1:T(8,128)(2,1)S(1)}, bf16[8,32,512]{2,0,1:T(8,128)(2,1)S(1)}, u32[]{:S(2)}, u32[]{:S(2)}) collective-permute-start(bf16[8,32,512]{2,0,1:T(8,128)(2,1)S(1)} %bitcast.165), channel_id=1, source_target_pairs={{0,4},{4,8},{8,12},{12,16},{16,20},{20,24},{24,28},{28,0},{1,5},{5... | collective-permute-start | bytes 786440 | tf_op jit(solution)/shard_map/ppermute | solution.py:138
  86.1 10.6 %collective-permute-start.8 = (bf16[8,32,512]{2,0,1:T(8,128)(2,1)S(1)}, bf16[8,32,512]{2,0,1:T(8,128)(2,1)S(1)}, u32[]{:S(2)}, u32[]{:S(2)}) collective-permute-start(bf16[8,32,512]{2,0,1:T(8,128)(2,1)S(1)} %bitcast.164), channel_id=1, source_target_pairs={{0,8},{4,12},{8,16},{12,20},{16,24},{20,28},{24,0},{28,4},{1,9},{5... | collective-permute-start | bytes 786440 | tf_op jit(solution)/shard_map/ppermute | solution.py:138
  97.2 2.7 collective-permute-start.10
  99.9 3.4 %collective-permute-start.11 = (bf16[8,32,512]{2,0,1:T(8,128)(2,1)S(1)}, bf16[8,32,512]{2,0,1:T(8,128)(2,1)S(1)}, u32[]{:S(2)}, u32[]{:S(2)}) collective-permute-start(bf16[8,32,512]{2,0,1:T(8,128)(2,1)S(1)} %bitcast.159), channel_id=1, source_target_pairs={{0,20},{4,24},{8,28},{12,0},{16,4},{20,8},{24,12},{28,16},{1,21},{... | collective-permute-start | bytes 786440 | tf_op jit(solution)/shard_map/ppermute | solution.py:138
  103.4 2.7 collective-permute-done.8
  108.5 15.4 %collective-permute-done.9 = bf16[8,32,512]{2,0,1:T(8,128)(2,1)S(1)} collective-permute-done((bf16[8,32,512]{2,0,1:T(8,128)(2,1)S(1)}, bf16[8,32,512]{2,0,1:T(8,128)(2,1)S(1)}, u32[]{:S(2)}, u32[]{:S(2)}) %collective-permute-start.9) | collective-permute-done | bytes 262176 | tf_op jit(solution)/shard_map/ppermute | solution.py:138
  126.4 3.8 %collective-permute-done.13 = bf16[8,32,512]{2,0,1:T(8,128)(2,1)S(1)} collective-permute-done((bf16[8,32,512]{2,0,1:T(8,128)(2,1)S(1)}, bf16[8,32,512]{2,0,1:T(8,128)(2,1)S(1)}, u32[]{:S(2)}, u32[]{:S(2)}) %collective-permute-start.13) | collective-permute-done | bytes 262176 | tf_op jit(solution)/shard_map/ppermute | solution.py:138
  137.6 5.6 %shard_map.147 = (f32[512,256]{1,0:T(8,128)S(1)}, f32[512,256]{1,0:T(8,128)S(1)}, bf16[1024,256]{1,0:T(8,128)(2,1)S(1)}, bf16[1024,256]{1,0:T(8,128)(2,1)S(1)}) custom-call(bf16[512,512]{1,0:T(8,128)(2,1)S(1)} %copy-done.16, bf16[1024,512]{1,0:T(8,128)(2,1)S(1)} %copy-done.2, bf16[1024,512]{1,0:T(8,128)(2,1)S(1)} %copy-done.2, f32[512,512]{1,0:T(8,128)S(1)} %copy-done.18), custom_call_target="tpu_custom_call" | custom-call | flops 1610612736 | bytes 3932160 | tf_op jit(solution)/shard_map/pallas_call | solution.py:62
  145.6 3.3 %fusion.5 = f32[512,2048]{1,0:T(8,128)} fusion(bf16[512,2048]{1,0:T(8,128)(2,1)S(1)} %copy-done, f32[512,256]{1,0:T(8,128)S(1)} %get-tuple-element.38, f32[512,256]{1,0:T(8,128)S(1)} %copy-done.12, f32[512,512]{1,0:T(8,128)S(1)} %copy-done.4, s32[512,512]{1,0:T(8,128)S(1)} %copy-done.21, f32[512]{0:T(512)S(1)} %get-tuple-element.88, ...), kind=kOutput, calls=%fused_computation.18 | convolution fusion | flops 1075838976 | bytes 9441280 | tf_op jit(solution)/shard_map/dot_general | solution.py:196
  155.7 15.3 %collective-permute-start.21 = (bf16[8,32,512]{2,0,1:T(8,128)(2,1)S(1)}, bf16[8,32,512]{2,0,1:T(8,128)(2,1)S(1)}, u32[]{:S(2)}, u32[]{:S(2)}) collective-permute-start(bf16[8,32,512]{2,0,1:T(8,128)(2,1)S(1)} %bitcast.163), channel_id=1, source_target_pairs={{0,28},{4,0},{8,4},{12,8},{16,12},{20,16},{24,20},{28,24},{1,29},{... | collective-permute-start | bytes 786440 | tf_op jit(solution)/shard_map/ppermute | solution.py:138
  178.7 4.7 %collective-permute-done.22 = bf16[8,32,512]{2,0,1:T(8,128)(2,1)S(1)} collective-permute-done((bf16[8,32,512]{2,0,1:T(8,128)(2,1)S(1)}, bf16[8,32,512]{2,0,1:T(8,128)(2,1)S(1)}, u32[]{:S(2)}, u32[]{:S(2)}) %collective-permute-start.22) | collective-permute-done | bytes 262176 | tf_op jit(solution)/shard_map/ppermute | solution.py:138
  183.5 5.6 %collective-permute-done.23 = bf16[8,32,512]{2,0,1:T(8,128)(2,1)S(1)} collective-permute-done((bf16[8,32,512]{2,0,1:T(8,128)(2,1)S(1)}, bf16[8,32,512]{2,0,1:T(8,128)(2,1)S(1)}, u32[]{:S(2)}, u32[]{:S(2)}) %collective-permute-start.23) | collective-permute-done | bytes 262176 | tf_op jit(solution)/shard_map/ppermute | solution.py:138
  189.0 14.7 %collective-permute-start.14 = (bf16[8,32,512]{2,0,1:T(8,128)(2,1)S(1)}, bf16[8,32,512]{2,0,1:T(8,128)(2,1)S(1)}, u32[]{:S(2)}, u32[]{:S(2)}) collective-permute-start(bf16[8,32,512]{2,0,1:T(8,128)(2,1)S(1)} %bitcast.149), channel_id=1, source_target_pairs={{0,28},{4,0},{8,4},{12,8},{16,12},{20,16},{24,20},{28,24},{1,29},{... | collective-permute-start | bytes 786440 | tf_op jit(solution)/shard_map/ppermute | solution.py:138
  203.7 14.4 %collective-permute-done.24 = bf16[8,32,512]{2,0,1:T(8,128)(2,1)S(1)} collective-permute-done((bf16[8,32,512]{2,0,1:T(8,128)(2,1)S(1)}, bf16[8,32,512]{2,0,1:T(8,128)(2,1)S(1)}, u32[]{:S(2)}, u32[]{:S(2)}) %collective-permute-start.24) | collective-permute-done | bytes 262176 | tf_op jit(solution)/shard_map/ppermute | solution.py:138
  219.7 15.9 %collective-permute-start.17 = (bf16[8,32,512]{2,0,1:T(8,128)(2,1)S(1)}, bf16[8,32,512]{2,0,1:T(8,128)(2,1)S(1)}, u32[]{:S(2)}, u32[]{:S(2)}) collective-permute-start(bf16[8,32,512]{2,0,1:T(8,128)(2,1)S(1)} %bitcast.144), channel_id=1, source_target_pairs={{0,16},{4,20},{8,24},{12,28},{16,0},{20,4},{24,8},{28,12},{1,17},{... | collective-permute-start | bytes 786440 | tf_op jit(solution)/shard_map/ppermute | solution.py:138
  238.9 23.2 %collective-permute-done.17 = bf16[8,32,512]{2,0,1:T(8,128)(2,1)S(1)} collective-permute-done((bf16[8,32,512]{2,0,1:T(8,128)(2,1)S(1)}, bf16[8,32,512]{2,0,1:T(8,128)(2,1)S(1)}, u32[]{:S(2)}, u32[]{:S(2)}) %collective-permute-start.17) | collective-permute-done | bytes 262176 | tf_op jit(solution)/shard_map/ppermute | solution.py:138
  (167 shorter events, 69.7 us)
Async XLA Ops:
  7.2 46.7 %all-gather.2.cloned.1.call-start = ((), (), s32[]{:S(2)}) async-start(), calls=%async_computation.1 | async-start | bytes 2621440 | tf_op jit(solution)/shard_map/all_gather | solution.py:151
  7.9 256.3 %reduce-scatter.2.cloned.1.call-start = ((), (), s32[]{:S(2)}) async-start(), calls=%async_computation.2 | async-start | bytes 5242880 | tf_op jit(solution)/shard_map/reduce_scatter | solution.py:197
  18.4 30.7 %collective-permute-start.2 = (bf16[8,32,512]{2,0,1:T(8,128)(2,1)}, bf16[8,32,512]{2,0,1:T(8,128)(2,1)}, u32[]{:S(2)}, u32[]{:S(2)}) collective-permute-start(bf16[8,32,512]{2,0,1:T(8,128)(2,1)} %bitcast.8), channel_id=1, source_target_pairs={{0,12},{4,16},{8,20},{12,24},{16,28},{20,0},{24,4},{28,8},{1,13},{... | collective-permute-start | bytes 786440 | tf_op jit(solution)/shard_map/ppermute | solution.py:138
  20.9 29.1 %collective-permute-start.3 = (bf16[8,32,512]{2,0,1:T(8,128)(2,1)S(1)}, bf16[8,32,512]{2,0,1:T(8,128)(2,1)}, u32[]{:S(2)}, u32[]{:S(2)}) collective-permute-start(bf16[8,32,512]{2,0,1:T(8,128)(2,1)S(1)} %bitcast.156), channel_id=1, source_target_pairs={{0,16},{4,20},{8,24},{12,28},{16,0},{20,4},{24,8},{28,12},{1,17},{... | collective-permute-start | bytes 786440 | tf_op jit(solution)/shard_map/ppermute | solution.py:138
  22.2 28.9 %collective-permute-start.4 = (bf16[8,32,512]{2,0,1:T(8,128)(2,1)S(1)}, bf16[8,32,512]{2,0,1:T(8,128)(2,1)}, u32[]{:S(2)}, u32[]{:S(2)}) collective-permute-start(bf16[8,32,512]{2,0,1:T(8,128)(2,1)S(1)} %bitcast.153), channel_id=1, source_target_pairs={{0,20},{4,24},{8,28},{12,0},{16,4},{20,8},{24,12},{28,16},{1,21},{... | collective-permute-start | bytes 786440 | tf_op jit(solution)/shard_map/ppermute | solution.py:138
  27.5 24.5 %collective-permute-start.5 = (bf16[8,32,512]{2,0,1:T(8,128)(2,1)S(1)}, bf16[8,32,512]{2,0,1:T(8,128)(2,1)S(1)}, u32[]{:S(2)}, u32[]{:S(2)}) collective-permute-start(bf16[8,32,512]{2,0,1:T(8,128)(2,1)S(1)} %bitcast.152), channel_id=1, source_target_pairs={{0,24},{4,28},{8,0},{12,4},{16,8},{20,12},{24,16},{28,20},{1,25},{... | collective-permute-start | bytes 786440 | tf_op jit(solution)/shard_map/ppermute | solution.py:138
  30.3 21.8 %collective-permute-start.6 = (bf16[8,32,512]{2,0,1:T(8,128)(2,1)S(1)}, bf16[8,32,512]{2,0,1:T(8,128)(2,1)S(1)}, u32[]{:S(2)}, u32[]{:S(2)}) collective-permute-start(bf16[8,32,512]{2,0,1:T(8,128)(2,1)S(1)} %bitcast.150), channel_id=1, source_target_pairs={{0,28},{4,0},{8,4},{12,8},{16,12},{20,16},{24,20},{28,24},{1,29},{... | collective-permute-start | bytes 786440 | tf_op jit(solution)/shard_map/ppermute | solution.py:138
  78.4 25.0 %collective-permute-start.7 = (bf16[8,32,512]{2,0,1:T(8,128)(2,1)S(1)}, bf16[8,32,512]{2,0,1:T(8,128)(2,1)S(1)}, u32[]{:S(2)}, u32[]{:S(2)}) collective-permute-start(bf16[8,32,512]{2,0,1:T(8,128)(2,1)S(1)} %bitcast.165), channel_id=1, source_target_pairs={{0,4},{4,8},{8,12},{12,16},{16,20},{20,24},{24,28},{28,0},{1,5},{5... | collective-permute-start | bytes 786440 | tf_op jit(solution)/shard_map/ppermute | solution.py:138
  96.7 27.2 %collective-permute-start.9 = (bf16[8,32,512]{2,0,1:T(8,128)(2,1)S(1)}, bf16[8,32,512]{2,0,1:T(8,128)(2,1)S(1)}, u32[]{:S(2)}, u32[]{:S(2)}) collective-permute-start(bf16[8,32,512]{2,0,1:T(8,128)(2,1)S(1)} %bitcast.162), channel_id=1, source_target_pairs={{0,12},{4,16},{8,20},{12,24},{16,28},{20,0},{24,4},{28,8},{1,13},{... | collective-permute-start | bytes 786440 | tf_op jit(solution)/shard_map/ppermute | solution.py:138
  97.2 29.1 %collective-permute-start.10 = (bf16[8,32,512]{2,0,1:T(8,128)(2,1)S(1)}, bf16[8,32,512]{2,0,1:T(8,128)(2,1)S(1)}, u32[]{:S(2)}, u32[]{:S(2)}) collective-permute-start(bf16[8,32,512]{2,0,1:T(8,128)(2,1)S(1)} %bitcast.160), channel_id=1, source_target_pairs={{0,16},{4,20},{8,24},{12,28},{16,0},{20,4},{24,8},{28,12},{1,17},{... | collective-permute-start | bytes 786440 | tf_op jit(solution)/shard_map/ppermute | solution.py:138
  99.9 26.5 %collective-permute-start.11 = (bf16[8,32,512]{2,0,1:T(8,128)(2,1)S(1)}, bf16[8,32,512]{2,0,1:T(8,128)(2,1)S(1)}, u32[]{:S(2)}, u32[]{:S(2)}) collective-permute-start(bf16[8,32,512]{2,0,1:T(8,128)(2,1)S(1)} %bitcast.159), channel_id=1, source_target_pairs={{0,20},{4,24},{8,28},{12,0},{16,4},{20,8},{24,12},{28,16},{1,21},{... | collective-permute-start | bytes 786440 | tf_op jit(solution)/shard_map/ppermute | solution.py:138
  103.4 23.0 %collective-permute-start.12 = (bf16[8,32,512]{2,0,1:T(8,128)(2,1)S(1)}, bf16[8,32,512]{2,0,1:T(8,128)(2,1)S(1)}, u32[]{:S(2)}, u32[]{:S(2)}) collective-permute-start(bf16[8,32,512]{2,0,1:T(8,128)(2,1)S(1)} %bitcast.157), channel_id=1, source_target_pairs={{0,24},{4,28},{8,0},{12,4},{16,8},{20,12},{24,16},{28,20},{1,25},{... | collective-permute-start | bytes 786440 | tf_op jit(solution)/shard_map/ppermute | solution.py:138
  106.2 24.1 %collective-permute-start.13 = (bf16[8,32,512]{2,0,1:T(8,128)(2,1)S(1)}, bf16[8,32,512]{2,0,1:T(8,128)(2,1)S(1)}, u32[]{:S(2)}, u32[]{:S(2)}) collective-permute-start(bf16[8,32,512]{2,0,1:T(8,128)(2,1)S(1)} %bitcast.155), channel_id=1, source_target_pairs={{0,28},{4,0},{8,4},{12,8},{16,12},{20,16},{24,20},{28,24},{1,29},{... | collective-permute-start | bytes 786440 | tf_op jit(solution)/shard_map/ppermute | solution.py:138
  155.7 22.1 %collective-permute-start.21 = (bf16[8,32,512]{2,0,1:T(8,128)(2,1)S(1)}, bf16[8,32,512]{2,0,1:T(8,128)(2,1)S(1)}, u32[]{:S(2)}, u32[]{:S(2)}) collective-permute-start(bf16[8,32,512]{2,0,1:T(8,128)(2,1)S(1)} %bitcast.163), channel_id=1, source_target_pairs={{0,28},{4,0},{8,4},{12,8},{16,12},{20,16},{24,20},{28,24},{1,29},{... | collective-permute-start | bytes 786440 | tf_op jit(solution)/shard_map/ppermute | solution.py:138
  171.7 46.5 %collective-permute-start.24 = (bf16[8,32,512]{2,0,1:T(8,128)(2,1)S(1)}, bf16[8,32,512]{2,0,1:T(8,128)(2,1)S(1)}, u32[]{:S(2)}, u32[]{:S(2)}) collective-permute-start(bf16[8,32,512]{2,0,1:T(8,128)(2,1)S(1)} %bitcast.154), channel_id=1, source_target_pairs={{0,16},{4,20},{8,24},{12,28},{16,0},{20,4},{24,8},{28,12},{1,17},{... | collective-permute-start | bytes 786440 | tf_op jit(solution)/shard_map/ppermute | solution.py:138
  174.0 44.1 %collective-permute-start.25 = (bf16[8,32,512]{2,0,1:T(8,128)(2,1)S(1)}, bf16[8,32,512]{2,0,1:T(8,128)(2,1)S(1)}, u32[]{:S(2)}, u32[]{:S(2)}) collective-permute-start(bf16[8,32,512]{2,0,1:T(8,128)(2,1)S(1)} %bitcast.151), channel_id=1, source_target_pairs={{0,12},{4,16},{8,20},{12,24},{16,28},{20,0},{24,4},{28,8},{1,13},{... | collective-permute-start | bytes 786440 | tf_op jit(solution)/shard_map/ppermute | solution.py:138
  177.8 41.9 %collective-permute-start.26 = (bf16[8,32,512]{2,0,1:T(8,128)(2,1)S(1)}, bf16[8,32,512]{2,0,1:T(8,128)(2,1)S(1)}, u32[]{:S(2)}, u32[]{:S(2)}) collective-permute-start(bf16[8,32,512]{2,0,1:T(8,128)(2,1)S(1)} %bitcast.148), channel_id=1, source_target_pairs={{0,8},{4,12},{8,16},{12,20},{16,24},{20,28},{24,0},{28,4},{1,9},{5... | collective-permute-start | bytes 786440 | tf_op jit(solution)/shard_map/ppermute | solution.py:138
  183.4 52.2 %collective-permute-start.27 = (bf16[8,32,512]{2,0,1:T(8,128)(2,1)S(1)}, bf16[8,32,512]{2,0,1:T(8,128)(2,1)S(1)}, u32[]{:S(2)}, u32[]{:S(2)}) collective-permute-start(bf16[8,32,512]{2,0,1:T(8,128)(2,1)S(1)} %bitcast.146), channel_id=1, source_target_pairs={{0,4},{4,8},{8,12},{12,16},{16,20},{20,24},{24,28},{28,0},{1,5},{5... | collective-permute-start | bytes 786440 | tf_op jit(solution)/shard_map/ppermute | solution.py:138
  189.0 47.2 %collective-permute-start.14 = (bf16[8,32,512]{2,0,1:T(8,128)(2,1)S(1)}, bf16[8,32,512]{2,0,1:T(8,128)(2,1)S(1)}, u32[]{:S(2)}, u32[]{:S(2)}) collective-permute-start(bf16[8,32,512]{2,0,1:T(8,128)(2,1)S(1)} %bitcast.149), channel_id=1, source_target_pairs={{0,28},{4,0},{8,4},{12,8},{16,12},{20,16},{24,20},{28,24},{1,29},{... | collective-permute-start | bytes 786440 | tf_op jit(solution)/shard_map/ppermute | solution.py:138
  218.2 20.7 %collective-permute-start.16 = (bf16[8,32,512]{2,0,1:T(8,128)(2,1)S(1)}, bf16[8,32,512]{2,0,1:T(8,128)(2,1)S(1)}, u32[]{:S(2)}, u32[]{:S(2)}) collective-permute-start(bf16[8,32,512]{2,0,1:T(8,128)(2,1)S(1)} %bitcast.145), channel_id=1, source_target_pairs={{0,20},{4,24},{8,28},{12,0},{16,4},{20,8},{24,12},{28,16},{1,21},{... | collective-permute-start | bytes 786440 | tf_op jit(solution)/shard_map/ppermute | solution.py:138
  219.7 42.4 %collective-permute-start.17 = (bf16[8,32,512]{2,0,1:T(8,128)(2,1)S(1)}, bf16[8,32,512]{2,0,1:T(8,128)(2,1)S(1)}, u32[]{:S(2)}, u32[]{:S(2)}) collective-permute-start(bf16[8,32,512]{2,0,1:T(8,128)(2,1)S(1)} %bitcast.144), channel_id=1, source_target_pairs={{0,16},{4,20},{8,24},{12,28},{16,0},{20,4},{24,8},{28,12},{1,17},{... | collective-permute-start | bytes 786440 | tf_op jit(solution)/shard_map/ppermute | solution.py:138
  235.6 26.5 %collective-permute-start.18 = (bf16[8,32,512]{2,0,1:T(8,128)(2,1)S(1)}, bf16[8,32,512]{2,0,1:T(8,128)(2,1)S(1)}, u32[]{:S(2)}, u32[]{:S(2)}) collective-permute-start(bf16[8,32,512]{2,0,1:T(8,128)(2,1)S(1)} %bitcast.143), channel_id=1, source_target_pairs={{0,12},{4,16},{8,20},{12,24},{16,28},{20,0},{24,4},{28,8},{1,13},{... | collective-permute-start | bytes 786440 | tf_op jit(solution)/shard_map/ppermute | solution.py:138
  236.3 26.0 %collective-permute-start.19 = (bf16[8,32,512]{2,0,1:T(8,128)(2,1)S(1)}, bf16[8,32,512]{2,0,1:T(8,128)(2,1)S(1)}, u32[]{:S(2)}, u32[]{:S(2)}) collective-permute-start(bf16[8,32,512]{2,0,1:T(8,128)(2,1)S(1)} %bitcast.142), channel_id=1, source_target_pairs={{0,8},{4,12},{8,16},{12,20},{16,24},{20,28},{24,0},{28,4},{1,9},{5... | collective-permute-start | bytes 786440 | tf_op jit(solution)/shard_map/ppermute | solution.py:138
  236.4 26.0 %collective-permute-start.20 = (bf16[8,32,512]{2,0,1:T(8,128)(2,1)S(1)}, bf16[8,32,512]{2,0,1:T(8,128)(2,1)S(1)}, u32[]{:S(2)}, u32[]{:S(2)}) collective-permute-start(bf16[8,32,512]{2,0,1:T(8,128)(2,1)S(1)} %bitcast.141), channel_id=1, source_target_pairs={{0,4},{4,8},{8,12},{12,16},{16,20},{20,24},{24,28},{28,0},{1,5},{5... | collective-permute-start | bytes 786440 | tf_op jit(solution)/shard_map/ppermute | solution.py:138
  (30 other events, 243.7 us)
Sparse Core Ops, SparseCore 0:
  9.5 25.2 all-gather.1
  149.0 56.3 reduce-scatter.1

commit v5 on v4

--- a/solution.py
+++ b/solution.py
@@ -136,7 +136,17 @@
         for shift in range(1, mem_count):
             pairs = [(i, (i + sign * shift) % mem_count) for i in range(mem_count)]
             pieces.append(lax.ppermute(buffer[shift], "mem", pairs))
-        return jnp.stack(pieces)
+        return pieces
+
+    def gather_slots(table, pieces):
+        total = None
+        for shift, piece in enumerate(pieces):
+            part = lax.dot_general(
+                table[shift * capacity:(shift + 1) * capacity], piece.reshape(capacity, entries2),
+                (((0,), (0,)), ((), ())), preferred_element_type=jnp.float32,
+            )
+            total = part if total is None else total + part
+        return total.astype(jnp.bfloat16)
 
     def fetch(chunk):
         cols = slice(chunk * chunk_cols, (chunk + 1) * chunk_cols)
@@ -148,10 +158,25 @@
 
     fetched = [fetch(0)]
 
-    cotangent_full = lax.all_gather(cotangent, "head", axis=1, tiled=True)
-    grad_attended = lax.dot_general(
-        cotangent_full, out_weight, (((1,), (1,)), ((), ())), preferred_element_type=jnp.float32
-    ) * keep_mask * keep_scale
+    head_count = lax.axis_size("head")
+    head_index = lax.axis_index("head")
+
+    def weight_cols(owner):
+        return lax.dynamic_slice_in_dim(out_weight, owner * feature_cols, feature_cols, axis=1)
+
+    grad_proj = None
+    for shift in range(head_count):
+        if shift == 0:
+            piece = cotangent
+        else:
+            pairs = [(i, (i + shift) % head_count) for i in range(head_count)]
+            piece = lax.ppermute(cotangent, "head", pairs)
+        owner = (head_index - shift) % head_count
+        part = lax.dot_general(
+            piece, weight_cols(owner), (((1,), (1,)), ((), ())), preferred_element_type=jnp.float32
+        )
+        grad_proj = part if grad_proj is None else grad_proj + part
+    grad_attended = grad_proj * keep_mask * keep_scale
     grad_mem = gate_cols * grad_attended
     grad_loc = (1.0 - gate_cols) * grad_attended
 
@@ -167,10 +192,9 @@
     for chunk in range(chunk_count):
         if chunk + 1 < chunk_count:
             fetched.append(fetch(chunk + 1))
-        chosen = jnp.dot(
-            pick_table, fetched[chunk].reshape(slot_count, entries2),
-            preferred_element_type=jnp.float32,
-        ).astype(jnp.bfloat16).reshape(top_blocks * block_len, 2 * chunk_cols)
+        chosen = gather_slots(pick_table.T, fetched[chunk]).reshape(
+            top_blocks * block_len, 2 * chunk_cols
+        )
         o_mem, q_mem, k_mem, v_mem = attention_branch(
             queries, grad_mem, chosen, chosen, chunk_heads, head_dim, False,
             q_off=chunk * chunk_heads, k_off=0, v_off=chunk_heads,
@@ -184,19 +208,23 @@
         if chunk + 1 < chunk_count:
             send, fetched[chunk + 1] = lax.optimization_barrier((send, fetched[chunk + 1]))
         returned = exchange(send.reshape(mem_count, capacity, block_len, 2 * chunk_cols), -1)
-        summed_parts.append(lax.dot_general(
-            serve_table, returned.reshape(slot_count, entries2), (((0,), (0,)), ((), ())),
-            preferred_element_type=jnp.float32,
-        ).astype(jnp.bfloat16).reshape(blocks_here, block_len, 2 * chunk_cols))
+        summed_parts.append(
+            gather_slots(serve_table, returned).reshape(blocks_here, block_len, 2 * chunk_cols)
+        )
 
     o_mem = jnp.concatenate(o_mem_parts, axis=1)
     q_mem = jnp.concatenate(q_mem_parts, axis=1)
     attended = gate_cols * o_mem + (1.0 - gate_cols) * o_loc
     dropped = (attended * keep_mask * keep_scale).astype(jnp.bfloat16)
-    partial_out = jnp.dot(dropped, out_weight, preferred_element_type=jnp.float32)
-    layer_out = lax.psum_scatter(partial_out, "head", scatter_dimension=1, tiled=True).astype(
-        jnp.bfloat16
-    )
+    out_sum = None
+    for shift in range(head_count):
+        target = (head_index + shift) % head_count
+        part = jnp.dot(dropped, weight_cols(target), preferred_element_type=jnp.float32)
+        if shift:
+            pairs = [(i, (i + shift) % head_count) for i in range(head_count)]
+            part = lax.ppermute(part, "head", pairs)
+        out_sum = part if out_sum is None else out_sum + part
+    layer_out = out_sum.astype(jnp.bfloat16)
 
     grad_queries = (q_mem + q_loc).astype(jnp.bfloat16)
     grad_keys = k_loc

time: 274 us -> 288 us (1.051); the launches traced: 273 us -> 283 us
  waiting for transfers between devices: 91.2 us -> 141 us
  starting transfers between devices: 96 us -> 50.7 us
  matrix products: 15.2 us -> 42.8 us
  between operations: 14.7 us -> 1.4 us
  local copies, waits for them, and re-layouts: 28.3 us -> 22.1 us
  other arithmetic: 9.41 us -> 6.49 us
    ppermute x28, waiting for transfers between devices: 90.5 us -> 141 us  [exchange(): pieces.append(lax.ppermute(buffer[shift], 'mem', pairs))]
    ppermute x28, starting transfers between devices: 95.9 us -> 46.6 us  [exchange(): pieces.append(lax.ppermute(buffer[shift], 'mem', pairs))]
    dot_general x6 -> x40, matrix products: 9.51 us -> 35.9 us  [the longest x32 21.9 us: gather_slots(): lax.dot_general(table[shift * capacity:(shift + 1) * capacity], piece.res...]
    unnamed x78 -> x60, local copies, waits for them, and re-layouts: 15.3 us -> 8 us
    ppermute x0 -> x6, starting transfers between devices: none -> 4.05 us  [the longest x3 3.53 us: per_device(): piece = lax.ppermute(cotangent, 'head', pairs)]
  transfers between devices with their start and end apart: 30 -> 34, of which waited for: 12 -> 20; matrix products, arithmetic and copies ran while one was open for 9% -> 16% of each run, Pallas kernels for 0% -> 2%
where the time goes in v5:
time: 288 us; the launch traced here: 283 us
  waiting for transfers between devices  141 us (49%)
  starting transfers between devices  50.7 us (18%)
  matrix products  42.8 us (15%)
  local copies, waits for them, and re-layouts  22.1 us (8%)
  Pallas kernels  18.4 us (6%)
  other arithmetic  6.49 us (2%)
    ppermute x28, waiting for transfers between devices, exchange(): pieces.append(lax.ppermute(buffer[shift], 'mem', pairs))  141 us
    ppermute x28, starting transfers between devices, exchange(): pieces.append(lax.ppermute(buffer[shift], 'mem', pairs))  46.6 us
    dot_general x32, matrix products, gather_slots(): lax.dot_general(table[shift * capacity:(shift + 1) * capacity], piece.res...  21.9 us
    pallas_call x3, Pallas kernels, attention_branch(): pl.pallas_call(kernel, grid=(heads,), in_specs=[spec(rows, q_off), spec(k...  18.4 us
    unnamed x60, local copies, waits for them, and re-layouts  8 us
    dot_general x4, matrix products, per_device(): jnp.dot(dropped, weight_cols(target), preferred_element_type=jnp.float32)  7.52 us
    dot_general x4, matrix products, per_device(): lax.dot_general(piece, weight_cols(owner), (((1,), (1,)), ((), ())), pref...  6.49 us
  transfers between devices with their start and end apart: 34, of which 20 were waited for; matrix products, arithmetic and copies ran while one was open for 16% of the time, Pallas kernels for 2%

profile of v5, /device:TPU:0, one launch (start us, length us, event | category | flops | bytes accessed | tf_op | source)
XLA Modules:
  0.0 282.9 jit_solution(15043558318483492954)
XLA Ops:
  11.6 4.6 %collective-permute-start.6 = (bf16[8,32,512]{2,0,1:T(8,128)(2,1)}, bf16[8,32,512]{2,0,1:T(8,128)(2,1)}, u32[]{:S(2)}, u32[]{:S(2)}) collective-permute-start(bf16[8,32,512]{2,0,1:T(8,128)(2,1)} %bitcast.15), channel_id=1, source_target_pairs={{0,28},{4,0},{8,4},{12,8},{16,12},{20,16},{24,20},{28,24},{1,29},{... | collective-permute-start | bytes 786440 | tf_op jit(solution)/shard_map/ppermute | solution.py:138
  20.8 7.0 %collective-permute-done = bf16[8,32,512]{2,0,1:T(8,128)(2,1)} collective-permute-done((bf16[8,32,512]{2,0,1:T(8,128)(2,1)}, bf16[8,32,512]{2,0,1:T(8,128)(2,1)}, u32[]{:S(2)}, u32[]{:S(2)}) %collective-permute-start) | collective-permute-done | bytes 262176 | tf_op jit(solution)/shard_map/ppermute | solution.py:138
  38.1 5.2 %collective-permute-done.4 = bf16[8,32,512]{2,0,1:T(8,128)(2,1)S(1)} collective-permute-done((bf16[8,32,512]{2,0,1:T(8,128)(2,1)S(1)}, bf16[8,32,512]{2,0,1:T(8,128)(2,1)S(1)}, u32[]{:S(2)}, u32[]{:S(2)}) %collective-permute-start.4) | collective-permute-done | bytes 262176 | tf_op jit(solution)/shard_map/ppermute | solution.py:138
  44.7 18.6 %collective-permute-done.3 = bf16[8,32,512]{2,0,1:T(8,128)(2,1)S(1)} collective-permute-done((bf16[8,32,512]{2,0,1:T(8,128)(2,1)S(1)}, bf16[8,32,512]{2,0,1:T(8,128)(2,1)S(1)}, u32[]{:S(2)}, u32[]{:S(2)}) %collective-permute-start.3) | collective-permute-done | bytes 262176 | tf_op jit(solution)/shard_map/ppermute | solution.py:138
  63.8 6.7 %collective-permute-done.2 = bf16[8,32,512]{2,0,1:T(8,128)(2,1)S(1)} collective-permute-done((bf16[8,32,512]{2,0,1:T(8,128)(2,1)S(1)}, bf16[8,32,512]{2,0,1:T(8,128)(2,1)S(1)}, u32[]{:S(2)}, u32[]{:S(2)}) %collective-permute-start.2) | collective-permute-done | bytes 262176 | tf_op jit(solution)/shard_map/ppermute | solution.py:138
  81.7 7.3 %shard_map.145 = (f32[512,512]{1,0:T(8,128)S(1)}, f32[512,512]{1,0:T(8,128)S(1)}, bf16[512,512]{1,0:T(8,128)(2,1)}, bf16[512,512]{1,0:T(8,128)(2,1)}) custom-call(bf16[512,512]{1,0:T(8,128)(2,1)S(1)} %copy-done.15, bf16[512,512]{1,0:T(8,128)(2,1)S(1)} %copy-done.13, bf16[512,512]{1,0:T(8,128)(2,1)S(1)} %copy-done.14, f32[512,512]{1,0:T(8,128)S(1)} %get-tuple-element.94.g_ref), custom_call_target="tpu_custom_call" | custom-call | flops 1610612736 | bytes 5767168 | tf_op jit(solution)/shard_map/pallas_call | solution.py:62
  92.0 5.6 %shard_map.146 = (f32[512,256]{1,0:T(8,128)S(1)}, f32[512,256]{1,0:T(8,128)S(1)}, bf16[1024,256]{1,0:T(8,128)(2,1)S(1)}, bf16[1024,256]{1,0:T(8,128)(2,1)S(1)}) custom-call(bf16[512,512]{1,0:T(8,128)(2,1)S(1)} %copy-done.15, bf16[1024,512]{1,0:T(8,128)(2,1)S(1)} %copy-done.1, bf16[1024,512]{1,0:T(8,128)(2,1)S(1)} %copy-done.1, ...), custom_call_target="tpu_custom_call" | custom-call | flops 1610612736 | bytes 3932160 | tf_op jit(solution)/shard_map/pallas_call | solution.py:62
  111.7 3.4 %convolution_convert_fusion.2 = bf16[64,16384]{1,0:T(8,128)(2,1)} fusion(bf16[32,16384]{1,0:T(8,128)(2,1)} %reshape.248, s32[32]{0:T(128)S(1)} %fusion.115), kind=kOutput, calls=%fused_computation.2 | convolution fusion | flops 68159488 | bytes 3145856 | tf_op jit(solution)/shard_map/dot_general | solution.py:205
  115.0 10.0 %collective-permute-done.12 = bf16[8,32,512]{2,0,1:T(8,128)(2,1)S(1)} collective-permute-done((bf16[8,32,512]{2,0,1:T(8,128)(2,1)}, bf16[8,32,512]{2,0,1:T(8,128)(2,1)S(1)}, u32[]{:S(2)}, u32[]{:S(2)}) %collective-permute-start.12) | collective-permute-done | bytes 262176 | tf_op jit(solution)/shard_map/ppermute | solution.py:138
  125.0 4.5 %collective-permute-done.13 = bf16[8,32,512]{2,0,1:T(8,128)(2,1)S(1)} collective-permute-done((bf16[8,32,512]{2,0,1:T(8,128)(2,1)}, bf16[8,32,512]{2,0,1:T(8,128)(2,1)S(1)}, u32[]{:S(2)}, u32[]{:S(2)}) %collective-permute-start.13) | collective-permute-done | bytes 262176 | tf_op jit(solution)/shard_map/ppermute | solution.py:138
  144.9 5.6 %shard_map.147 = (f32[512,256]{1,0:T(8,128)S(1)}, f32[512,256]{1,0:T(8,128)S(1)}, bf16[1024,256]{1,0:T(8,128)(2,1)S(1)}, bf16[1024,256]{1,0:T(8,128)(2,1)S(1)}) custom-call(bf16[512,512]{1,0:T(8,128)(2,1)S(1)} %copy-done.16, bf16[1024,512]{1,0:T(8,128)(2,1)S(1)} %copy-done.2, bf16[1024,512]{1,0:T(8,128)(2,1)S(1)} %copy-done.2, f32[512,512]{1,0:T(8,128)S(1)} %copy-done.4), custom_call_target="tpu_custom_call" | custom-call | flops 1610612736 | bytes 3932160 | tf_op jit(solution)/shard_map/pallas_call | solution.py:62
  161.3 5.4 %collective-permute-start.33 = (bf16[8,32,512]{2,0,1:T(8,128)(2,1)S(1)}, bf16[8,32,512]{2,0,1:T(8,128)(2,1)S(1)}, u32[]{:S(2)}, u32[]{:S(2)}) collective-permute-start(bf16[8,32,512]{2,0,1:T(8,128)(2,1)S(1)} %bitcast.150), channel_id=1, source_target_pairs={{0,4},{4,8},{8,12},{12,16},{16,20},{20,24},{24,28},{28,0},{1,5},{5... | collective-permute-start | bytes 786440 | tf_op jit(solution)/shard_map/ppermute | solution.py:138
  167.0 12.0 %collective-permute-start.27 = (bf16[8,32,512]{2,0,1:T(8,128)(2,1)S(1)}, bf16[8,32,512]{2,0,1:T(8,128)(2,1)S(1)}, u32[]{:S(2)}, u32[]{:S(2)}) collective-permute-start(bf16[8,32,512]{2,0,1:T(8,128)(2,1)S(1)} %bitcast.151), channel_id=1, source_target_pairs={{0,28},{4,0},{8,4},{12,8},{16,12},{20,16},{24,20},{28,24},{1,29},{... | collective-permute-start | bytes 786440 | tf_op jit(solution)/shard_map/ppermute | solution.py:138
  180.1 9.3 %collective-permute-done.27 = bf16[8,32,512]{2,0,1:T(8,128)(2,1)S(1)} collective-permute-done((bf16[8,32,512]{2,0,1:T(8,128)(2,1)S(1)}, bf16[8,32,512]{2,0,1:T(8,128)(2,1)S(1)}, u32[]{:S(2)}, u32[]{:S(2)}) %collective-permute-start.27) | collective-permute-done | bytes 262176 | tf_op jit(solution)/shard_map/ppermute | solution.py:138
  192.6 7.9 %collective-permute-done.32 = bf16[8,32,512]{2,0,1:T(8,128)(2,1)S(1)} collective-permute-done((bf16[8,32,512]{2,0,1:T(8,128)(2,1)S(1)}, bf16[8,32,512]{2,0,1:T(8,128)(2,1)S(1)}, u32[]{:S(2)}, u32[]{:S(2)}) %collective-permute-start.32) | collective-permute-done | bytes 262176 | tf_op jit(solution)/shard_map/ppermute | solution.py:138
  200.8 14.9 %collective-permute-done.31 = bf16[8,32,512]{2,0,1:T(8,128)(2,1)S(1)} collective-permute-done((bf16[8,32,512]{2,0,1:T(8,128)(2,1)S(1)}, bf16[8,32,512]{2,0,1:T(8,128)(2,1)S(1)}, u32[]{:S(2)}, u32[]{:S(2)}) %collective-permute-start.31) | collective-permute-done | bytes 262176 | tf_op jit(solution)/shard_map/ppermute | solution.py:138
  216.1 6.4 %collective-permute-done.30 = bf16[8,32,512]{2,0,1:T(8,128)(2,1)S(1)} collective-permute-done((bf16[8,32,512]{2,0,1:T(8,128)(2,1)S(1)}, bf16[8,32,512]{2,0,1:T(8,128)(2,1)S(1)}, u32[]{:S(2)}, u32[]{:S(2)}) %collective-permute-start.30) | collective-permute-done | bytes 262176 | tf_op jit(solution)/shard_map/ppermute | solution.py:138
  222.4 4.2 %collective-permute-start.20 = (bf16[8,32,512]{2,0,1:T(8,128)(2,1)S(1)}, bf16[8,32,512]{2,0,1:T(8,128)(2,1)S(1)}, u32[]{:S(2)}, u32[]{:S(2)}) collective-permute-start(bf16[8,32,512]{2,0,1:T(8,128)(2,1)S(1)} %bitcast.146), channel_id=1, source_target_pairs={{0,28},{4,0},{8,4},{12,8},{16,12},{20,16},{24,20},{28,24},{1,29},{... | collective-permute-start | bytes 786440 | tf_op jit(solution)/shard_map/ppermute | solution.py:138
  227.4 5.9 %collective-permute-done.20 = bf16[8,32,512]{2,0,1:T(8,128)(2,1)S(1)} collective-permute-done((bf16[8,32,512]{2,0,1:T(8,128)(2,1)S(1)}, bf16[8,32,512]{2,0,1:T(8,128)(2,1)S(1)}, u32[]{:S(2)}, u32[]{:S(2)}) %collective-permute-start.20) | collective-permute-done | bytes 262176 | tf_op jit(solution)/shard_map/ppermute | solution.py:138
  235.5 3.7 %collective-permute-done.28 = bf16[8,32,512]{2,0,1:T(8,128)(2,1)S(1)} collective-permute-done((bf16[8,32,512]{2,0,1:T(8,128)(2,1)S(1)}, bf16[8,32,512]{2,0,1:T(8,128)(2,1)S(1)}, u32[]{:S(2)}, u32[]{:S(2)}) %collective-permute-start.28) | collective-permute-done | bytes 262176 | tf_op jit(solution)/shard_map/ppermute | solution.py:138
  240.7 5.0 %collective-permute-done.26 = bf16[8,32,512]{2,0,1:T(8,128)(2,1)S(1)} collective-permute-done((bf16[8,32,512]{2,0,1:T(8,128)(2,1)S(1)}, bf16[8,32,512]{2,0,1:T(8,128)(2,1)S(1)}, u32[]{:S(2)}, u32[]{:S(2)}) %collective-permute-start.26) | collective-permute-done | bytes 262176 | tf_op jit(solution)/shard_map/ppermute | solution.py:138
  246.1 4.1 %collective-permute-done.25 = bf16[8,32,512]{2,0,1:T(8,128)(2,1)S(1)} collective-permute-done((bf16[8,32,512]{2,0,1:T(8,128)(2,1)S(1)}, bf16[8,32,512]{2,0,1:T(8,128)(2,1)S(1)}, u32[]{:S(2)}, u32[]{:S(2)}) %collective-permute-start.25) | collective-permute-done | bytes 262176 | tf_op jit(solution)/shard_map/ppermute | solution.py:138
  250.5 15.4 %collective-permute-done.24 = bf16[8,32,512]{2,0,1:T(8,128)(2,1)S(1)} collective-permute-done((bf16[8,32,512]{2,0,1:T(8,128)(2,1)S(1)}, bf16[8,32,512]{2,0,1:T(8,128)(2,1)S(1)}, u32[]{:S(2)}, u32[]{:S(2)}) %collective-permute-start.24) | collective-permute-done | bytes 262176 | tf_op jit(solution)/shard_map/ppermute | solution.py:138
  268.2 9.0 %collective-permute-done.22 = bf16[8,32,512]{2,0,1:T(8,128)(2,1)S(1)} collective-permute-done((bf16[8,32,512]{2,0,1:T(8,128)(2,1)S(1)}, bf16[8,32,512]{2,0,1:T(8,128)(2,1)S(1)}, u32[]{:S(2)}, u32[]{:S(2)}) %collective-permute-start.22) | collective-permute-done | bytes 262176 | tf_op jit(solution)/shard_map/ppermute | solution.py:138
  (188 shorter events, 99.9 us)
Async XLA Ops:
  0.6 76.1 %collective-permute-start.9 = (bf16[512,512]{1,0:T(8,128)(2,1)}, bf16[512,512]{1,0:T(8,128)(2,1)}, u32[]{:S(2)}, u32[]{:S(2)}) collective-permute-start(bf16[512,512]{1,0:T(8,128)(2,1)} %param.19), channel_id=1, source_target_pairs={{0,3},{1,0},{2,1},{3,2},{4,7},{5,4},{6,5},{7,6},{8,11},{9,8},{10,9... | collective-permute-start | bytes 1572872 | tf_op jit(solution)/shard_map/ppermute | solution.py:173
  3.1 75.2 %collective-permute-start.7 = (bf16[512,512]{1,0:T(8,128)(2,1)}, bf16[512,512]{1,0:T(8,128)(2,1)}, u32[]{:S(2)}, u32[]{:S(2)}) collective-permute-start(bf16[512,512]{1,0:T(8,128)(2,1)} %param.19), channel_id=1, source_target_pairs={{0,1},{1,2},{2,3},{3,0},{4,5},{5,6},{6,7},{7,4},{8,9},{9,10},{10,1... | collective-permute-start | bytes 1572872 | tf_op jit(solution)/shard_map/ppermute | solution.py:173
  3.1 76.8 %collective-permute-start.8 = (bf16[512,512]{1,0:T(8,128)(2,1)}, bf16[512,512]{1,0:T(8,128)(2,1)}, u32[]{:S(2)}, u32[]{:S(2)}) collective-permute-start(bf16[512,512]{1,0:T(8,128)(2,1)} %param.19), channel_id=1, source_target_pairs={{0,2},{1,3},{2,0},{3,1},{4,6},{5,7},{6,4},{7,5},{8,10},{9,11},{10,... | collective-permute-start | bytes 1572872 | tf_op jit(solution)/shard_map/ppermute | solution.py:173
  11.6 19.3 %collective-permute-start.6 = (bf16[8,32,512]{2,0,1:T(8,128)(2,1)}, bf16[8,32,512]{2,0,1:T(8,128)(2,1)}, u32[]{:S(2)}, u32[]{:S(2)}) collective-permute-start(bf16[8,32,512]{2,0,1:T(8,128)(2,1)} %bitcast.15), channel_id=1, source_target_pairs={{0,28},{4,0},{8,4},{12,8},{16,12},{20,16},{24,20},{28,24},{1,29},{... | collective-permute-start | bytes 786440 | tf_op jit(solution)/shard_map/ppermute | solution.py:138
  30.9 12.4 %collective-permute-start.4 = (bf16[8,32,512]{2,0,1:T(8,128)(2,1)S(1)}, bf16[8,32,512]{2,0,1:T(8,128)(2,1)S(1)}, u32[]{:S(2)}, u32[]{:S(2)}) collective-permute-start(bf16[8,32,512]{2,0,1:T(8,128)(2,1)S(1)} %bitcast.136), channel_id=1, source_target_pairs={{0,20},{4,24},{8,28},{12,0},{16,4},{20,8},{24,12},{28,16},{1,21},{... | collective-permute-start | bytes 786440 | tf_op jit(solution)/shard_map/ppermute | solution.py:138
  36.4 26.9 %collective-permute-start.3 = (bf16[8,32,512]{2,0,1:T(8,128)(2,1)S(1)}, bf16[8,32,512]{2,0,1:T(8,128)(2,1)S(1)}, u32[]{:S(2)}, u32[]{:S(2)}) collective-permute-start(bf16[8,32,512]{2,0,1:T(8,128)(2,1)S(1)} %bitcast.135), channel_id=1, source_target_pairs={{0,16},{4,20},{8,24},{12,28},{16,0},{20,4},{24,8},{28,12},{1,17},{... | collective-permute-start | bytes 786440 | tf_op jit(solution)/shard_map/ppermute | solution.py:138
  43.3 27.2 %collective-permute-start.2 = (bf16[8,32,512]{2,0,1:T(8,128)(2,1)S(1)}, bf16[8,32,512]{2,0,1:T(8,128)(2,1)S(1)}, u32[]{:S(2)}, u32[]{:S(2)}) collective-permute-start(bf16[8,32,512]{2,0,1:T(8,128)(2,1)S(1)} %bitcast.134), channel_id=1, source_target_pairs={{0,12},{4,16},{8,20},{12,24},{16,28},{20,0},{24,4},{28,8},{1,13},{... | collective-permute-start | bytes 786440 | tf_op jit(solution)/shard_map/ppermute | solution.py:138
  91.4 17.8 %collective-permute-start.10 = (bf16[8,32,512]{2,0,1:T(8,128)(2,1)}, bf16[8,32,512]{2,0,1:T(8,128)(2,1)}, u32[]{:S(2)}, u32[]{:S(2)}) collective-permute-start(bf16[8,32,512]{2,0,1:T(8,128)(2,1)} %bitcast.19), channel_id=1, source_target_pairs={{0,4},{4,8},{8,12},{12,16},{16,20},{20,24},{24,28},{28,0},{1,5},{5... | collective-permute-start | bytes 786440 | tf_op jit(solution)/shard_map/ppermute | solution.py:138
  91.4 19.3 %collective-permute-start.11 = (bf16[8,32,512]{2,0,1:T(8,128)(2,1)}, bf16[8,32,512]{2,0,1:T(8,128)(2,1)}, u32[]{:S(2)}, u32[]{:S(2)}) collective-permute-start(bf16[8,32,512]{2,0,1:T(8,128)(2,1)} %bitcast.20), channel_id=1, source_target_pairs={{0,8},{4,12},{8,16},{12,20},{16,24},{20,28},{24,0},{28,4},{1,9},{5... | collective-permute-start | bytes 786440 | tf_op jit(solution)/shard_map/ppermute | solution.py:138
  102.6 22.4 %collective-permute-start.12 = (bf16[8,32,512]{2,0,1:T(8,128)(2,1)}, bf16[8,32,512]{2,0,1:T(8,128)(2,1)S(1)}, u32[]{:S(2)}, u32[]{:S(2)}) collective-permute-start(bf16[8,32,512]{2,0,1:T(8,128)(2,1)} %bitcast.156), channel_id=1, source_target_pairs={{0,12},{4,16},{8,20},{12,24},{16,28},{20,0},{24,4},{28,8},{1,13},{... | collective-permute-start | bytes 786440 | tf_op jit(solution)/shard_map/ppermute | solution.py:138
  104.3 25.2 %collective-permute-start.13 = (bf16[8,32,512]{2,0,1:T(8,128)(2,1)}, bf16[8,32,512]{2,0,1:T(8,128)(2,1)S(1)}, u32[]{:S(2)}, u32[]{:S(2)}) collective-permute-start(bf16[8,32,512]{2,0,1:T(8,128)(2,1)} %bitcast.155), channel_id=1, source_target_pairs={{0,16},{4,20},{8,24},{12,28},{16,0},{20,4},{24,8},{28,12},{1,17},{... | collective-permute-start | bytes 786440 | tf_op jit(solution)/shard_map/ppermute | solution.py:138
  107.3 22.2 %collective-permute-start.14 = (bf16[8,32,512]{2,0,1:T(8,128)(2,1)}, bf16[8,32,512]{2,0,1:T(8,128)(2,1)S(1)}, u32[]{:S(2)}, u32[]{:S(2)}) collective-permute-start(bf16[8,32,512]{2,0,1:T(8,128)(2,1)} %bitcast.154), channel_id=1, source_target_pairs={{0,20},{4,24},{8,28},{12,0},{16,4},{20,8},{24,12},{28,16},{1,21},{... | collective-permute-start | bytes 786440 | tf_op jit(solution)/shard_map/ppermute | solution.py:138
  109.2 20.4 %collective-permute-start.15 = (bf16[8,32,512]{2,0,1:T(8,128)(2,1)}, bf16[8,32,512]{2,0,1:T(8,128)(2,1)S(1)}, u32[]{:S(2)}, u32[]{:S(2)}) collective-permute-start(bf16[8,32,512]{2,0,1:T(8,128)(2,1)} %bitcast.153), channel_id=1, source_target_pairs={{0,24},{4,28},{8,0},{12,4},{16,8},{20,12},{24,16},{28,20},{1,25},{... | collective-permute-start | bytes 786440 | tf_op jit(solution)/shard_map/ppermute | solution.py:138
  110.7 21.6 %collective-permute-start.16 = (bf16[8,32,512]{2,0,1:T(8,128)(2,1)}, bf16[8,32,512]{2,0,1:T(8,128)(2,1)S(1)}, u32[]{:S(2)}, u32[]{:S(2)}) collective-permute-start(bf16[8,32,512]{2,0,1:T(8,128)(2,1)} %bitcast.152), channel_id=1, source_target_pairs={{0,28},{4,0},{8,4},{12,8},{16,12},{20,16},{24,20},{28,24},{1,29},{... | collective-permute-start | bytes 786440 | tf_op jit(solution)/shard_map/ppermute | solution.py:138
  152.3 127.4 %collective-permute-start.19 = (f32[512,512]{1,0:T(8,128)}, f32[512,512]{1,0:T(8,128)}, u32[]{:S(2)}, u32[]{:S(2)}) collective-permute-start(f32[512,512]{1,0:T(8,128)} %fusion.30), channel_id=1, source_target_pairs={{0,3},{1,0},{2,1},{3,2},{4,7},{5,4},{6,5},{7,6},{8,11},{9,8},{10,9... | collective-permute-start | bytes 3145736 | tf_op jit(solution)/shard_map/ppermute | solution.py:225
  153.8 126.0 %collective-permute-start.18 = (f32[512,512]{1,0:T(8,128)}, f32[512,512]{1,0:T(8,128)}, u32[]{:S(2)}, u32[]{:S(2)}) collective-permute-start(f32[512,512]{1,0:T(8,128)} %fusion.32), channel_id=1, source_target_pairs={{0,2},{1,3},{2,0},{3,1},{4,6},{5,7},{6,4},{7,5},{8,10},{9,11},{10,... | collective-permute-start | bytes 3145736 | tf_op jit(solution)/shard_map/ppermute | solution.py:225
  155.6 124.2 %collective-permute-start.17 = (f32[512,512]{1,0:T(8,128)}, f32[512,512]{1,0:T(8,128)}, u32[]{:S(2)}, u32[]{:S(2)}) collective-permute-start(f32[512,512]{1,0:T(8,128)} %fusion.34), channel_id=1, source_target_pairs={{0,1},{1,2},{2,3},{3,0},{4,5},{5,6},{6,7},{7,4},{8,9},{9,10},{10,1... | collective-permute-start | bytes 3145736 | tf_op jit(solution)/shard_map/ppermute | solution.py:225
  161.3 29.7 %collective-permute-start.33 = (bf16[8,32,512]{2,0,1:T(8,128)(2,1)S(1)}, bf16[8,32,512]{2,0,1:T(8,128)(2,1)S(1)}, u32[]{:S(2)}, u32[]{:S(2)}) collective-permute-start(bf16[8,32,512]{2,0,1:T(8,128)(2,1)S(1)} %bitcast.150), channel_id=1, source_target_pairs={{0,4},{4,8},{8,12},{12,16},{16,20},{20,24},{24,28},{28,0},{1,5},{5... | collective-permute-start | bytes 786440 | tf_op jit(solution)/shard_map/ppermute | solution.py:138
  167.0 22.4 %collective-permute-start.27 = (bf16[8,32,512]{2,0,1:T(8,128)(2,1)S(1)}, bf16[8,32,512]{2,0,1:T(8,128)(2,1)S(1)}, u32[]{:S(2)}, u32[]{:S(2)}) collective-permute-start(bf16[8,32,512]{2,0,1:T(8,128)(2,1)S(1)} %bitcast.151), channel_id=1, source_target_pairs={{0,28},{4,0},{8,4},{12,8},{16,12},{20,16},{24,20},{28,24},{1,29},{... | collective-permute-start | bytes 786440 | tf_op jit(solution)/shard_map/ppermute | solution.py:138
  191.0 24.7 %collective-permute-start.31 = (bf16[8,32,512]{2,0,1:T(8,128)(2,1)S(1)}, bf16[8,32,512]{2,0,1:T(8,128)(2,1)S(1)}, u32[]{:S(2)}, u32[]{:S(2)}) collective-permute-start(bf16[8,32,512]{2,0,1:T(8,128)(2,1)S(1)} %bitcast.148), channel_id=1, source_target_pairs={{0,12},{4,16},{8,20},{12,24},{16,28},{20,0},{24,4},{28,8},{1,13},{... | collective-permute-start | bytes 786440 | tf_op jit(solution)/shard_map/ppermute | solution.py:138
  200.4 22.0 %collective-permute-start.30 = (bf16[8,32,512]{2,0,1:T(8,128)(2,1)S(1)}, bf16[8,32,512]{2,0,1:T(8,128)(2,1)S(1)}, u32[]{:S(2)}, u32[]{:S(2)}) collective-permute-start(bf16[8,32,512]{2,0,1:T(8,128)(2,1)S(1)} %bitcast.147), channel_id=1, source_target_pairs={{0,16},{4,20},{8,24},{12,28},{16,0},{20,4},{24,8},{28,12},{1,17},{... | collective-permute-start | bytes 786440 | tf_op jit(solution)/shard_map/ppermute | solution.py:138
  233.4 12.3 %collective-permute-start.26 = (bf16[8,32,512]{2,0,1:T(8,128)(2,1)S(1)}, bf16[8,32,512]{2,0,1:T(8,128)(2,1)S(1)}, u32[]{:S(2)}, u32[]{:S(2)}) collective-permute-start(bf16[8,32,512]{2,0,1:T(8,128)(2,1)S(1)} %bitcast.143), channel_id=1, source_target_pairs={{0,4},{4,8},{8,12},{12,16},{16,20},{20,24},{24,28},{28,0},{1,5},{5... | collective-permute-start | bytes 786440 | tf_op jit(solution)/shard_map/ppermute | solution.py:138
  245.7 20.2 %collective-permute-start.24 = (bf16[8,32,512]{2,0,1:T(8,128)(2,1)S(1)}, bf16[8,32,512]{2,0,1:T(8,128)(2,1)S(1)}, u32[]{:S(2)}, u32[]{:S(2)}) collective-permute-start(bf16[8,32,512]{2,0,1:T(8,128)(2,1)S(1)} %bitcast.141), channel_id=1, source_target_pairs={{0,12},{4,16},{8,20},{12,24},{16,28},{20,0},{24,4},{28,8},{1,13},{... | collective-permute-start | bytes 786440 | tf_op jit(solution)/shard_map/ppermute | solution.py:138
  250.2 16.1 %collective-permute-start.23 = (bf16[8,32,512]{2,0,1:T(8,128)(2,1)S(1)}, bf16[8,32,512]{2,0,1:T(8,128)(2,1)S(1)}, u32[]{:S(2)}, u32[]{:S(2)}) collective-permute-start(bf16[8,32,512]{2,0,1:T(8,128)(2,1)S(1)} %bitcast.140), channel_id=1, source_target_pairs={{0,16},{4,20},{8,24},{12,28},{16,0},{20,4},{24,8},{28,12},{1,17},{... | collective-permute-start | bytes 786440 | tf_op jit(solution)/shard_map/ppermute | solution.py:138
  (40 other events, 267.3 us)

commit v6 on v5

--- a/solution.py
+++ b/solution.py
@@ -184,10 +184,6 @@
         queries, grad_loc, local_keys, local_values, heads_here, head_dim, True
     )
 
-    if chunk_count > 1:
-        memory_keys, memory_values, o_loc, q_loc, k_loc, v_loc, grad_mem = lax.optimization_barrier(
-            (memory_keys, memory_values, o_loc, q_loc, k_loc, v_loc, grad_mem)
-        )
     o_mem_parts, q_mem_parts, summed_parts = [], [], []
     for chunk in range(chunk_count):
         if chunk + 1 < chunk_count:
@@ -205,8 +201,6 @@
         send = lax.dot_general(
             pick_table, parts, (((0,), (0,)), ((), ())), preferred_element_type=jnp.float32
         ).astype(jnp.bfloat16)
-        if chunk + 1 < chunk_count:
-            send, fetched[chunk + 1] = lax.optimization_barrier((send, fetched[chunk + 1]))
         returned = exchange(send.reshape(mem_count, capacity, block_len, 2 * chunk_cols), -1)
         summed_parts.append(
             gather_slots(serve_table, returned).reshape(blocks_here, block_len, 2 * chunk_cols)

time: 288 us -> 285 us (0.990)
  the two profiles are of different devices: /device:TPU:0 before, /device:TPU:23 now
where the time goes in v6:
time: 285 us; the launch traced here: 284 us
  waiting for transfers between devices  104 us (36%)
  starting transfers between devices  98.5 us (35%)
  matrix products  37.1 us (13%)
  local copies, waits for them, and re-layouts  18.6 us (7%)
  Pallas kernels  18.4 us (6%)
  other arithmetic  6.09 us (2%)
    ppermute x28, starting transfers between devices, exchange(): pieces.append(lax.ppermute(buffer[shift], 'mem', pairs))  78.4 us
    ppermute x28, waiting for transfers between devices, exchange(): pieces.append(lax.ppermute(buffer[shift], 'mem', pairs))  62.5 us
    ppermute x3, waiting for transfers between devices, per_device(): part = lax.ppermute(part, 'head', pairs)  41.7 us
    dot_general x32, matrix products, gather_slots(): lax.dot_general(table[shift * capacity:(shift + 1) * capacity], piece.res...  21.5 us
    pallas_call x3, Pallas kernels, attention_branch(): pl.pallas_call(kernel, grid=(heads,), in_specs=[spec(rows, q_off), spec(k...  18.4 us
    ppermute x3, starting transfers between devices, per_device(): part = lax.ppermute(part, 'head', pairs)  18.1 us
    dot_general x4, matrix products, per_device(): lax.dot_general(piece, weight_cols(owner), (((1,), (1,)), ((), ())), pref...  7.4 us
    unnamed x86, local copies, waits for them, and re-layouts  6.14 us
  transfers between devices with their start and end apart: 34, of which 14 were waited for; matrix products, arithmetic and copies ran while one was open for 14% of the time, Pallas kernels for 3%

profile of v6, /device:TPU:23, one launch (start us, length us, event | category | flops | bytes accessed | tf_op | source)
XLA Modules:
  0.0 284.3 jit_solution(9954756865414773334)
XLA Ops:
  11.7 2.8 fusion.54
  20.2 2.9 %collective-permute-done = bf16[8,32,512]{2,0,1:T(8,128)(2,1)} collective-permute-done((bf16[8,32,512]{2,0,1:T(8,128)(2,1)}, bf16[8,32,512]{2,0,1:T(8,128)(2,1)}, u32[]{:S(2)}, u32[]{:S(2)}) %collective-permute-start) | collective-permute-done | bytes 262176 | tf_op jit(solution)/shard_map/ppermute | solution.py:138
  27.4 12.8 %collective-permute-done.3 = bf16[8,32,512]{2,0,1:T(8,128)(2,1)S(1)} collective-permute-done((bf16[8,32,512]{2,0,1:T(8,128)(2,1)}, bf16[8,32,512]{2,0,1:T(8,128)(2,1)S(1)}, u32[]{:S(2)}, u32[]{:S(2)}) %collective-permute-start.3) | collective-permute-done | bytes 262176 | tf_op jit(solution)/shard_map/ppermute | solution.py:138
  41.7 4.0 %collective-permute-done.2 = bf16[8,32,512]{2,0,1:T(8,128)(2,1)S(1)} collective-permute-done((bf16[8,32,512]{2,0,1:T(8,128)(2,1)S(1)}, bf16[8,32,512]{2,0,1:T(8,128)(2,1)S(1)}, u32[]{:S(2)}, u32[]{:S(2)}) %collective-permute-start.2) | collective-permute-done | bytes 262176 | tf_op jit(solution)/shard_map/ppermute | solution.py:138
  51.8 6.0 %collective-permute-start.10 = (bf16[8,32,512]{2,0,1:T(8,128)(2,1)S(1)}, bf16[8,32,512]{2,0,1:T(8,128)(2,1)S(1)}, u32[]{:S(2)}, u32[]{:S(2)}) collective-permute-start(bf16[8,32,512]{2,0,1:T(8,128)(2,1)S(1)} %bitcast.141), channel_id=1, source_target_pairs={{0,4},{4,8},{8,12},{12,16},{16,20},{20,24},{24,28},{28,0},{1,5},{5... | collective-permute-start | bytes 786440 | tf_op jit(solution)/shard_map/ppermute | solution.py:138
  58.3 5.1 %collective-permute-start.13 = (bf16[8,32,512]{2,0,1:T(8,128)(2,1)S(1)}, bf16[8,32,512]{2,0,1:T(8,128)(2,1)S(1)}, u32[]{:S(2)}, u32[]{:S(2)}) collective-permute-start(bf16[8,32,512]{2,0,1:T(8,128)(2,1)S(1)} %bitcast.140), channel_id=1, source_target_pairs={{0,16},{4,20},{8,24},{12,28},{16,0},{20,4},{24,8},{28,12},{1,17},{... | collective-permute-start | bytes 786440 | tf_op jit(solution)/shard_map/ppermute | solution.py:138
  68.3 8.1 %collective-permute-done.13 = bf16[8,32,512]{2,0,1:T(8,128)(2,1)S(1)} collective-permute-done((bf16[8,32,512]{2,0,1:T(8,128)(2,1)S(1)}, bf16[8,32,512]{2,0,1:T(8,128)(2,1)S(1)}, u32[]{:S(2)}, u32[]{:S(2)}) %collective-permute-start.13) | collective-permute-done | bytes 262176 | tf_op jit(solution)/shard_map/ppermute | solution.py:138
  76.9 7.1 %collective-permute-done.12 = bf16[8,32,512]{2,0,1:T(8,128)(2,1)S(1)} collective-permute-done((bf16[8,32,512]{2,0,1:T(8,128)(2,1)S(1)}, bf16[8,32,512]{2,0,1:T(8,128)(2,1)S(1)}, u32[]{:S(2)}, u32[]{:S(2)}) %collective-permute-start.12) | collective-permute-done | bytes 262176 | tf_op jit(solution)/shard_map/ppermute | solution.py:138
  84.5 8.9 %collective-permute-done.15 = bf16[8,32,512]{2,0,1:T(8,128)(2,1)S(1)} collective-permute-done((bf16[8,32,512]{2,0,1:T(8,128)(2,1)S(1)}, bf16[8,32,512]{2,0,1:T(8,128)(2,1)S(1)}, u32[]{:S(2)}, u32[]{:S(2)}) %collective-permute-start.15) | collective-permute-done | bytes 262176 | tf_op jit(solution)/shard_map/ppermute | solution.py:138
  93.8 7.4 %collective-permute-done.14 = bf16[8,32,512]{2,0,1:T(8,128)(2,1)S(1)} collective-permute-done((bf16[8,32,512]{2,0,1:T(8,128)(2,1)S(1)}, bf16[8,32,512]{2,0,1:T(8,128)(2,1)S(1)}, u32[]{:S(2)}, u32[]{:S(2)}) %collective-permute-start.14) | collective-permute-done | bytes 262176 | tf_op jit(solution)/shard_map/ppermute | solution.py:138
  102.2 7.4 %collective-permute-done.11 = bf16[8,32,512]{2,0,1:T(8,128)(2,1)S(1)} collective-permute-done((bf16[8,32,512]{2,0,1:T(8,128)(2,1)S(1)}, bf16[8,32,512]{2,0,1:T(8,128)(2,1)S(1)}, u32[]{:S(2)}, u32[]{:S(2)}) %collective-permute-start.11) | collective-permute-done | bytes 262176 | tf_op jit(solution)/shard_map/ppermute | solution.py:138
  117.5 2.7 broadcast_multiply_fusion
  120.2 5.6 %shard_map.145 = (f32[512,256]{1,0:T(8,128)S(1)}, f32[512,256]{1,0:T(8,128)S(1)}, bf16[1024,256]{1,0:T(8,128)(2,1)S(1)}, bf16[1024,256]{1,0:T(8,128)(2,1)S(1)}) custom-call(bf16[512,512]{1,0:T(8,128)(2,1)S(1)} %copy-done.13, bf16[1024,512]{1,0:T(8,128)(2,1)S(1)} %copy-done.1, bf16[1024,512]{1,0:T(8,128)(2,1)S(1)} %copy-done.1, ...), custom_call_target="tpu_custom_call" | custom-call | flops 1610612736 | bytes 3932160 | tf_op jit(solution)/shard_map/pallas_call | solution.py:62
  135.4 5.6 %shard_map.146 = (f32[512,256]{1,0:T(8,128)S(1)}, f32[512,256]{1,0:T(8,128)S(1)}, bf16[1024,256]{1,0:T(8,128)(2,1)S(1)}, bf16[1024,256]{1,0:T(8,128)(2,1)S(1)}) custom-call(bf16[512,512]{1,0:T(8,128)(2,1)S(1)} %copy-done.14, bf16[1024,512]{1,0:T(8,128)(2,1)S(1)} %reshape.253.k_ref.v_ref, bf16[1024,512]{1,0:T(8,128)(2,1)S(1)} %reshape.253.k_ref.v_ref, ...), custom_call_target="tpu_custom_call" | custom-call | flops 1610612736 | bytes 3932160 | tf_op jit(solution)/shard_map/pallas_call | solution.py:62
  146.9 4.8 %collective-permute-start.20 = (bf16[8,32,512]{2,0,1:T(8,128)(2,1)S(1)}, bf16[8,32,512]{2,0,1:T(8,128)(2,1)S(1)}, u32[]{:S(2)}, u32[]{:S(2)}) collective-permute-start(bf16[8,32,512]{2,0,1:T(8,128)(2,1)S(1)} %bitcast.155), channel_id=1, source_target_pairs={{0,28},{4,0},{8,4},{12,8},{16,12},{20,16},{24,20},{28,24},{1,29},{... | collective-permute-start | bytes 786440 | tf_op jit(solution)/shard_map/ppermute | solution.py:138
  155.9 7.3 %shard_map.147 = (f32[512,512]{1,0:T(8,128)S(1)}, f32[512,512]{1,0:T(8,128)S(1)}, bf16[512,512]{1,0:T(8,128)(2,1)}, bf16[512,512]{1,0:T(8,128)(2,1)}) custom-call(bf16[512,512]{1,0:T(8,128)(2,1)S(1)} %copy-done.15, bf16[512,512]{1,0:T(8,128)(2,1)S(1)} %copy-done.16, bf16[512,512]{1,0:T(8,128)(2,1)S(1)} %copy-done.17, f32[512,512]{1,0:T(8,128)S(1)} %copy-done.2), custom_call_target="tpu_custom_call" | custom-call | flops 1610612736 | bytes 5767168 | tf_op jit(solution)/shard_map/pallas_call | solution.py:62
  168.2 14.1 %collective-permute-start.21 = (bf16[8,32,512]{2,0,1:T(8,128)(2,1)S(1)}, bf16[8,32,512]{2,0,1:T(8,128)(2,1)S(1)}, u32[]{:S(2)}, u32[]{:S(2)}) collective-permute-start(bf16[8,32,512]{2,0,1:T(8,128)(2,1)S(1)} %bitcast.148), channel_id=1, source_target_pairs={{0,24},{4,28},{8,0},{12,4},{16,8},{20,12},{24,16},{28,20},{1,25},{... | collective-permute-start | bytes 786440 | tf_op jit(solution)/shard_map/ppermute | solution.py:138
  185.9 11.6 %collective-permute-start.32 = (bf16[8,32,512]{2,0,1:T(8,128)(2,1)S(1)}, bf16[8,32,512]{2,0,1:T(8,128)(2,1)S(1)}, u32[]{:S(2)}, u32[]{:S(2)}) collective-permute-start(bf16[8,32,512]{2,0,1:T(8,128)(2,1)S(1)} %bitcast.146), channel_id=1, source_target_pairs={{0,8},{4,12},{8,16},{12,20},{16,24},{20,28},{24,0},{28,4},{1,9},{5... | collective-permute-start | bytes 786440 | tf_op jit(solution)/shard_map/ppermute | solution.py:138
  198.3 2.5 collective-permute-start.30
  201.4 13.5 %collective-permute-start.29 = (bf16[8,32,512]{2,0,1:T(8,128)(2,1)S(1)}, bf16[8,32,512]{2,0,1:T(8,128)(2,1)S(1)}, u32[]{:S(2)}, u32[]{:S(2)}) collective-permute-start(bf16[8,32,512]{2,0,1:T(8,128)(2,1)S(1)} %bitcast.143), channel_id=1, source_target_pairs={{0,20},{4,24},{8,28},{12,0},{16,4},{20,8},{24,12},{28,16},{1,21},{... | collective-permute-start | bytes 786440 | tf_op jit(solution)/shard_map/ppermute | solution.py:138
  215.2 3.6 %collective-permute-start.28 = (bf16[8,32,512]{2,0,1:T(8,128)(2,1)S(1)}, bf16[8,32,512]{2,0,1:T(8,128)(2,1)S(1)}, u32[]{:S(2)}, u32[]{:S(2)}) collective-permute-start(bf16[8,32,512]{2,0,1:T(8,128)(2,1)S(1)} %bitcast.142), channel_id=1, source_target_pairs={{0,24},{4,28},{8,0},{12,4},{16,8},{20,12},{24,16},{28,20},{1,25},{... | collective-permute-start | bytes 786440 | tf_op jit(solution)/shard_map/ppermute | solution.py:138
  219.2 16.6 %collective-permute-start.17 = (f32[512,512]{1,0:T(8,128)S(1)}, f32[512,512]{1,0:T(8,128)S(1)}, u32[]{:S(2)}, u32[]{:S(2)}) collective-permute-start(f32[512,512]{1,0:T(8,128)S(1)} %fusion.39), channel_id=1, source_target_pairs={{0,1},{1,2},{2,3},{3,0},{4,5},{5,6},{6,7},{7,4},{8,9},{9,10},{10,1... | collective-permute-start | bytes 3145736 | tf_op jit(solution)/shard_map/ppermute | solution.py:219
  241.4 16.2 %collective-permute-done.17 = f32[512,512]{1,0:T(8,128)S(1)} collective-permute-done((f32[512,512]{1,0:T(8,128)S(1)}, f32[512,512]{1,0:T(8,128)S(1)}, u32[]{:S(2)}, u32[]{:S(2)}) %collective-permute-start.17) | collective-permute-done | bytes 1048608 | tf_op jit(solution)/shard_map/ppermute | solution.py:219
  257.7 24.3 %collective-permute-done.18 = f32[512,512]{1,0:T(8,128)S(1)} collective-permute-done((f32[512,512]{1,0:T(8,128)S(1)}, f32[512,512]{1,0:T(8,128)S(1)}, u32[]{:S(2)}, u32[]{:S(2)}) %collective-permute-start.18) | collective-permute-done | bytes 1048608 | tf_op jit(solution)/shard_map/ppermute | solution.py:219
  (210 shorter events, 82.0 us)
Async XLA Ops:
  0.6 115.2 %collective-permute-start.7 = (bf16[512,512]{1,0:T(8,128)(2,1)}, bf16[512,512]{1,0:T(8,128)(2,1)}, u32[]{:S(2)}, u32[]{:S(2)}) collective-permute-start(bf16[512,512]{1,0:T(8,128)(2,1)} %param.19), channel_id=1, source_target_pairs={{0,1},{1,2},{2,3},{3,0},{4,5},{5,6},{6,7},{7,4},{8,9},{9,10},{10,1... | collective-permute-start | bytes 1572872 | tf_op jit(solution)/shard_map/ppermute | solution.py:173
  1.5 112.7 %collective-permute-start.9 = (bf16[512,512]{1,0:T(8,128)(2,1)}, bf16[512,512]{1,0:T(8,128)(2,1)}, u32[]{:S(2)}, u32[]{:S(2)}) collective-permute-start(bf16[512,512]{1,0:T(8,128)(2,1)} %param.19), channel_id=1, source_target_pairs={{0,3},{1,0},{2,1},{3,2},{4,7},{5,4},{6,5},{7,6},{8,11},{9,8},{10,9... | collective-permute-start | bytes 1572872 | tf_op jit(solution)/shard_map/ppermute | solution.py:173
  1.5 116.0 %collective-permute-start.8 = (bf16[512,512]{1,0:T(8,128)(2,1)}, bf16[512,512]{1,0:T(8,128)(2,1)}, u32[]{:S(2)}, u32[]{:S(2)}) collective-permute-start(bf16[512,512]{1,0:T(8,128)(2,1)} %param.19), channel_id=1, source_target_pairs={{0,2},{1,3},{2,0},{3,1},{4,6},{5,7},{6,4},{7,5},{8,10},{9,11},{10,... | collective-permute-start | bytes 1572872 | tf_op jit(solution)/shard_map/ppermute | solution.py:173
  23.1 17.1 %collective-permute-start.3 = (bf16[8,32,512]{2,0,1:T(8,128)(2,1)}, bf16[8,32,512]{2,0,1:T(8,128)(2,1)S(1)}, u32[]{:S(2)}, u32[]{:S(2)}) collective-permute-start(bf16[8,32,512]{2,0,1:T(8,128)(2,1)} %bitcast.134), channel_id=1, source_target_pairs={{0,16},{4,20},{8,24},{12,28},{16,0},{20,4},{24,8},{28,12},{1,17},{... | collective-permute-start | bytes 786440 | tf_op jit(solution)/shard_map/ppermute | solution.py:138
  24.9 20.8 %collective-permute-start.2 = (bf16[8,32,512]{2,0,1:T(8,128)(2,1)S(1)}, bf16[8,32,512]{2,0,1:T(8,128)(2,1)S(1)}, u32[]{:S(2)}, u32[]{:S(2)}) collective-permute-start(bf16[8,32,512]{2,0,1:T(8,128)(2,1)S(1)} %bitcast.133), channel_id=1, source_target_pairs={{0,12},{4,16},{8,20},{12,24},{16,28},{20,0},{24,4},{28,8},{1,13},{... | collective-permute-start | bytes 786440 | tf_op jit(solution)/shard_map/ppermute | solution.py:138
  58.3 18.1 %collective-permute-start.13 = (bf16[8,32,512]{2,0,1:T(8,128)(2,1)S(1)}, bf16[8,32,512]{2,0,1:T(8,128)(2,1)S(1)}, u32[]{:S(2)}, u32[]{:S(2)}) collective-permute-start(bf16[8,32,512]{2,0,1:T(8,128)(2,1)S(1)} %bitcast.140), channel_id=1, source_target_pairs={{0,16},{4,20},{8,24},{12,28},{16,0},{20,4},{24,8},{28,12},{1,17},{... | collective-permute-start | bytes 786440 | tf_op jit(solution)/shard_map/ppermute | solution.py:138
  65.4 18.6 %collective-permute-start.12 = (bf16[8,32,512]{2,0,1:T(8,128)(2,1)S(1)}, bf16[8,32,512]{2,0,1:T(8,128)(2,1)S(1)}, u32[]{:S(2)}, u32[]{:S(2)}) collective-permute-start(bf16[8,32,512]{2,0,1:T(8,128)(2,1)S(1)} %bitcast.139), channel_id=1, source_target_pairs={{0,12},{4,16},{8,20},{12,24},{16,28},{20,0},{24,4},{28,8},{1,13},{... | collective-permute-start | bytes 786440 | tf_op jit(solution)/shard_map/ppermute | solution.py:138
  84.0 17.2 %collective-permute-start.14 = (bf16[8,32,512]{2,0,1:T(8,128)(2,1)S(1)}, bf16[8,32,512]{2,0,1:T(8,128)(2,1)S(1)}, u32[]{:S(2)}, u32[]{:S(2)}) collective-permute-start(bf16[8,32,512]{2,0,1:T(8,128)(2,1)S(1)} %bitcast.137), channel_id=1, source_target_pairs={{0,20},{4,24},{8,28},{12,0},{16,4},{20,8},{24,12},{28,16},{1,21},{... | collective-permute-start | bytes 786440 | tf_op jit(solution)/shard_map/ppermute | solution.py:138
  146.9 19.3 %collective-permute-start.20 = (bf16[8,32,512]{2,0,1:T(8,128)(2,1)S(1)}, bf16[8,32,512]{2,0,1:T(8,128)(2,1)S(1)}, u32[]{:S(2)}, u32[]{:S(2)}) collective-permute-start(bf16[8,32,512]{2,0,1:T(8,128)(2,1)S(1)} %bitcast.155), channel_id=1, source_target_pairs={{0,28},{4,0},{8,4},{12,8},{16,12},{20,16},{24,20},{28,24},{1,29},{... | collective-permute-start | bytes 786440 | tf_op jit(solution)/shard_map/ppermute | solution.py:138
  151.8 30.9 %collective-permute-start.24 = (bf16[8,32,512]{2,0,1:T(8,128)(2,1)S(1)}, bf16[8,32,512]{2,0,1:T(8,128)(2,1)S(1)}, u32[]{:S(2)}, u32[]{:S(2)}) collective-permute-start(bf16[8,32,512]{2,0,1:T(8,128)(2,1)S(1)} %bitcast.153), channel_id=1, source_target_pairs={{0,12},{4,16},{8,20},{12,24},{16,28},{20,0},{24,4},{28,8},{1,13},{... | collective-permute-start | bytes 786440 | tf_op jit(solution)/shard_map/ppermute | solution.py:138
  152.4 32.1 %collective-permute-start.23 = (bf16[8,32,512]{2,0,1:T(8,128)(2,1)S(1)}, bf16[8,32,512]{2,0,1:T(8,128)(2,1)S(1)}, u32[]{:S(2)}, u32[]{:S(2)}) collective-permute-start(bf16[8,32,512]{2,0,1:T(8,128)(2,1)S(1)} %bitcast.152), channel_id=1, source_target_pairs={{0,16},{4,20},{8,24},{12,28},{16,0},{20,4},{24,8},{28,12},{1,17},{... | collective-permute-start | bytes 786440 | tf_op jit(solution)/shard_map/ppermute | solution.py:138
  154.0 31.9 %collective-permute-start.22 = (bf16[8,32,512]{2,0,1:T(8,128)(2,1)S(1)}, bf16[8,32,512]{2,0,1:T(8,128)(2,1)S(1)}, u32[]{:S(2)}, u32[]{:S(2)}) collective-permute-start(bf16[8,32,512]{2,0,1:T(8,128)(2,1)S(1)} %bitcast.151), channel_id=1, source_target_pairs={{0,20},{4,24},{8,28},{12,0},{16,4},{20,8},{24,12},{28,16},{1,21},{... | collective-permute-start | bytes 786440 | tf_op jit(solution)/shard_map/ppermute | solution.py:138
  166.2 31.7 %collective-permute-start.26 = (bf16[8,32,512]{2,0,1:T(8,128)(2,1)S(1)}, bf16[8,32,512]{2,0,1:T(8,128)(2,1)S(1)}, u32[]{:S(2)}, u32[]{:S(2)}) collective-permute-start(bf16[8,32,512]{2,0,1:T(8,128)(2,1)S(1)} %bitcast.150), channel_id=1, source_target_pairs={{0,4},{4,8},{8,12},{12,16},{16,20},{20,24},{24,28},{28,0},{1,5},{5... | collective-permute-start | bytes 786440 | tf_op jit(solution)/shard_map/ppermute | solution.py:138
  168.2 30.1 %collective-permute-start.21 = (bf16[8,32,512]{2,0,1:T(8,128)(2,1)S(1)}, bf16[8,32,512]{2,0,1:T(8,128)(2,1)S(1)}, u32[]{:S(2)}, u32[]{:S(2)}) collective-permute-start(bf16[8,32,512]{2,0,1:T(8,128)(2,1)S(1)} %bitcast.148), channel_id=1, source_target_pairs={{0,24},{4,28},{8,0},{12,4},{16,8},{20,12},{24,16},{28,20},{1,25},{... | collective-permute-start | bytes 786440 | tf_op jit(solution)/shard_map/ppermute | solution.py:138
  182.6 18.7 %collective-permute-start.27 = (bf16[8,32,512]{2,0,1:T(8,128)(2,1)S(1)}, bf16[8,32,512]{2,0,1:T(8,128)(2,1)S(1)}, u32[]{:S(2)}, u32[]{:S(2)}) collective-permute-start(bf16[8,32,512]{2,0,1:T(8,128)(2,1)S(1)} %bitcast.149), channel_id=1, source_target_pairs={{0,28},{4,0},{8,4},{12,8},{16,12},{20,16},{24,20},{28,24},{1,29},{... | collective-permute-start | bytes 786440 | tf_op jit(solution)/shard_map/ppermute | solution.py:138
  184.5 30.7 %collective-permute-start.33 = (bf16[8,32,512]{2,0,1:T(8,128)(2,1)S(1)}, bf16[8,32,512]{2,0,1:T(8,128)(2,1)S(1)}, u32[]{:S(2)}, u32[]{:S(2)}) collective-permute-start(bf16[8,32,512]{2,0,1:T(8,128)(2,1)S(1)} %bitcast.147), channel_id=1, source_target_pairs={{0,4},{4,8},{8,12},{12,16},{16,20},{20,24},{24,28},{28,0},{1,5},{5... | collective-permute-start | bytes 786440 | tf_op jit(solution)/shard_map/ppermute | solution.py:138
  185.9 33.3 %collective-permute-start.32 = (bf16[8,32,512]{2,0,1:T(8,128)(2,1)S(1)}, bf16[8,32,512]{2,0,1:T(8,128)(2,1)S(1)}, u32[]{:S(2)}, u32[]{:S(2)}) collective-permute-start(bf16[8,32,512]{2,0,1:T(8,128)(2,1)S(1)} %bitcast.146), channel_id=1, source_target_pairs={{0,8},{4,12},{8,16},{12,20},{16,24},{20,28},{24,0},{28,4},{1,9},{5... | collective-permute-start | bytes 786440 | tf_op jit(solution)/shard_map/ppermute | solution.py:138
  197.9 38.3 %collective-permute-start.31 = (bf16[8,32,512]{2,0,1:T(8,128)(2,1)S(1)}, bf16[8,32,512]{2,0,1:T(8,128)(2,1)S(1)}, u32[]{:S(2)}, u32[]{:S(2)}) collective-permute-start(bf16[8,32,512]{2,0,1:T(8,128)(2,1)S(1)} %bitcast.145), channel_id=1, source_target_pairs={{0,12},{4,16},{8,20},{12,24},{16,28},{20,0},{24,4},{28,8},{1,13},{... | collective-permute-start | bytes 786440 | tf_op jit(solution)/shard_map/ppermute | solution.py:138
  198.3 39.7 %collective-permute-start.30 = (bf16[8,32,512]{2,0,1:T(8,128)(2,1)S(1)}, bf16[8,32,512]{2,0,1:T(8,128)(2,1)S(1)}, u32[]{:S(2)}, u32[]{:S(2)}) collective-permute-start(bf16[8,32,512]{2,0,1:T(8,128)(2,1)S(1)} %bitcast.144), channel_id=1, source_target_pairs={{0,16},{4,20},{8,24},{12,28},{16,0},{20,4},{24,8},{28,12},{1,17},{... | collective-permute-start | bytes 786440 | tf_op jit(solution)/shard_map/ppermute | solution.py:138
  201.4 37.2 %collective-permute-start.29 = (bf16[8,32,512]{2,0,1:T(8,128)(2,1)S(1)}, bf16[8,32,512]{2,0,1:T(8,128)(2,1)S(1)}, u32[]{:S(2)}, u32[]{:S(2)}) collective-permute-start(bf16[8,32,512]{2,0,1:T(8,128)(2,1)S(1)} %bitcast.143), channel_id=1, source_target_pairs={{0,20},{4,24},{8,28},{12,0},{16,4},{20,8},{24,12},{28,16},{1,21},{... | collective-permute-start | bytes 786440 | tf_op jit(solution)/shard_map/ppermute | solution.py:138
  215.2 23.7 %collective-permute-start.28 = (bf16[8,32,512]{2,0,1:T(8,128)(2,1)S(1)}, bf16[8,32,512]{2,0,1:T(8,128)(2,1)S(1)}, u32[]{:S(2)}, u32[]{:S(2)}) collective-permute-start(bf16[8,32,512]{2,0,1:T(8,128)(2,1)S(1)} %bitcast.142), channel_id=1, source_target_pairs={{0,24},{4,28},{8,0},{12,4},{16,8},{20,12},{24,16},{28,20},{1,25},{... | collective-permute-start | bytes 786440 | tf_op jit(solution)/shard_map/ppermute | solution.py:138
  219.2 38.4 %collective-permute-start.17 = (f32[512,512]{1,0:T(8,128)S(1)}, f32[512,512]{1,0:T(8,128)S(1)}, u32[]{:S(2)}, u32[]{:S(2)}) collective-permute-start(f32[512,512]{1,0:T(8,128)S(1)} %fusion.39), channel_id=1, source_target_pairs={{0,1},{1,2},{2,3},{3,0},{4,5},{5,6},{6,7},{7,4},{8,9},{9,10},{10,1... | collective-permute-start | bytes 3145736 | tf_op jit(solution)/shard_map/ppermute | solution.py:219
  236.2 45.7 %collective-permute-start.18 = (f32[512,512]{1,0:T(8,128)S(1)}, f32[512,512]{1,0:T(8,128)S(1)}, u32[]{:S(2)}, u32[]{:S(2)}) collective-permute-start(f32[512,512]{1,0:T(8,128)S(1)} %fusion.37), channel_id=1, source_target_pairs={{0,2},{1,3},{2,0},{3,1},{4,6},{5,7},{6,4},{7,5},{8,10},{9,11},{10,... | collective-permute-start | bytes 3145736 | tf_op jit(solution)/shard_map/ppermute | solution.py:219
  238.0 45.1 %collective-permute-start.19 = (f32[512,512]{1,0:T(8,128)S(1)}, f32[512,512]{1,0:T(8,128)S(1)}, u32[]{:S(2)}, u32[]{:S(2)}) collective-permute-start(f32[512,512]{1,0:T(8,128)S(1)} %fusion.35), channel_id=1, source_target_pairs={{0,3},{1,0},{2,1},{3,2},{4,7},{5,4},{6,5},{7,6},{8,11},{9,8},{10,9... | collective-permute-start | bytes 3145736 | tf_op jit(solution)/shard_map/ppermute | solution.py:219
  (51 other events, 340.2 us)

commit v7 on v5

--- a/solution.py
+++ b/solution.py
@@ -9,7 +9,7 @@
 
 
 QBLK = 512
-CHUNKS = 2
+CHUNKS = 4
 
 
 keep_scale = 1.0 / 0.9
@@ -77,6 +77,36 @@
             bytes_accessed=rows * cols * 14 + keys * cols * 8,
         ),
     )(q, k, v, g)
+
+
+def _gather_kernel(*refs):
+    table_ref = refs[0]
+    pieces = refs[1:-1]
+    out_ref = refs[-1]
+    capacity = pieces[0].shape[0]
+    total = None
+    for shift, piece in enumerate(pieces):
+        rows = table_ref[shift * capacity:(shift + 1) * capacity, :].astype(jnp.bfloat16)
+        part = lax.dot_general(rows, piece[...], (((0,), (0,)), ((), ())), preferred_element_type=jnp.float32)
+        total = part if total is None else total + part
+    out_ref[...] = total.astype(out_ref.dtype)
+
+
+def gather_pieces(table, pieces):
+    out_rows = table.shape[1]
+    capacity, entries = pieces[0].shape
+    whole = pl.BlockSpec(memory_space=pltpu.VMEM)
+    return pl.pallas_call(
+        _gather_kernel,
+        in_specs=[whole] * (1 + len(pieces)),
+        out_specs=whole,
+        out_shape=jax.ShapeDtypeStruct((out_rows, entries), jnp.bfloat16),
+        compiler_params=pltpu.CompilerParams(vmem_limit_bytes=32 * 1024 * 1024),
+        cost_estimate=pl.CostEstimate(
+            flops=2 * table.shape[0] * out_rows * entries, transcendentals=0,
+            bytes_accessed=len(pieces) * capacity * entries * 2 + out_rows * entries * 2,
+        ),
+    )(table, *pieces)
 
 
 def per_device(
@@ -126,7 +156,7 @@
     gate_cols = jnp.repeat(gate_values, head_dim)[None, :]
     keep_mask = dropout_keep.astype(jnp.float32)
 
-    chunk_heads = heads_here // CHUNKS if heads_here % CHUNKS == 0 else heads_here
+    chunk_heads = max(1, heads_here // CHUNKS)
     chunk_count = heads_here // chunk_heads
     chunk_cols = chunk_heads * head_dim
     entries2 = block_len * 2 * chunk_cols
@@ -139,14 +169,9 @@
         return pieces
 
     def gather_slots(table, pieces):
-        total = None
-        for shift, piece in enumerate(pieces):
-            part = lax.dot_general(
-                table[shift * capacity:(shift + 1) * capacity], piece.reshape(capacity, entries2),
-                (((0,), (0,)), ((), ())), preferred_element_type=jnp.float32,
-            )
-            total = part if total is None else total + part
-        return total.astype(jnp.bfloat16)
+        return gather_pieces(
+            table.astype(jnp.float32), [piece.reshape(capacity, entries2) for piece in pieces]
+        )
 
     def fetch(chunk):
         cols = slice(chunk * chunk_cols, (chunk + 1) * chunk_cols)

time: 288 us -> 284 us (0.986)
  starting transfers between devices: 50.7 us -> 124 us
  waiting for transfers between devices: 141 us -> 75 us
  matrix products: 42.8 us -> 15.3 us
  Pallas kernels: 18.4 us -> 29.9 us
  local copies, waits for them, and re-layouts: 22.1 us -> 27.9 us
    ppermute x28 -> x56, waiting for transfers between devices: 141 us -> 36.3 us  [exchange(): pieces.append(lax.ppermute(buffer[shift], 'mem', pairs))]
    ppermute x28 -> x56, starting transfers between devices: 46.6 us -> 120 us  [exchange(): pieces.append(lax.ppermute(buffer[shift], 'mem', pairs))]
    ppermute x3, waiting for transfers between devices: 0.01 us -> 38.7 us  [per_device(): part = lax.ppermute(part, 'head', pairs)]
    dot_general x32 -> x0, matrix products: 21.9 us -> none  [gather_slots(): lax.dot_general(table[shift * capacity:(shift + 1) * capacity], piece.res...]
    pallas_call x0 -> x8, Pallas kernels: none -> 12.4 us  [gather_pieces(): pl.pallas_call(_gather_kernel, in_specs=[whole] * (1 + len(pieces)), out_...]
    dot_general x4, matrix products: 7.52 us -> 2.57 us  [per_device(): jnp.dot(dropped, weight_cols(target), preferred_element_type=jnp.float32)]
    unnamed x60 -> x118, local copies, waits for them, and re-layouts: 8 us -> 12.3 us
    slice x4 -> x8, local copies, waits for them, and re-layouts: 2.63 us -> 6.59 us  [exchange(): pieces.append(lax.ppermute(buffer[shift], 'mem', pairs))]
  transfers between devices with their start and end apart: 34 -> 62, of which waited for: 20 -> 18; matrix products, arithmetic and copies ran while one was open for 16% -> 12% of each run, Pallas kernels for 2% -> 8%
where the time goes in v7:
time: 284 us; the launch traced here: 281 us
  starting transfers between devices  124 us (44%)
  waiting for transfers between devices  75 us (26%)
  Pallas kernels  29.9 us (11%)
  local copies, waits for them, and re-layouts  27.9 us (10%)
  matrix products  15.3 us (5%)
  other arithmetic  7.7 us (3%)
    ppermute x56, starting transfers between devices, exchange(): pieces.append(lax.ppermute(buffer[shift], 'mem', pairs))  120 us
    ppermute x3, waiting for transfers between devices, per_device(): part = lax.ppermute(part, 'head', pairs)  38.7 us
    ppermute x56, waiting for transfers between devices, exchange(): pieces.append(lax.ppermute(buffer[shift], 'mem', pairs))  36.3 us
    pallas_call x5, Pallas kernels, attention_branch(): pl.pallas_call(kernel, grid=(heads,), in_specs=[spec(rows, q_off), spec(k...  17.6 us
    pallas_call x8, Pallas kernels, gather_pieces(): pl.pallas_call(_gather_kernel, in_specs=[whole] * (1 + len(pieces)), out_...  12.4 us
    unnamed x118, local copies, waits for them, and re-layouts  12.3 us
    dot_general x4, matrix products, per_device(): lax.dot_general(piece, weight_cols(owner), (((1,), (1,)), ((), ())), pref...  7.43 us
    slice x8, local copies, waits for them, and re-layouts, exchange(): pieces.append(lax.ppermute(buffer[shift], 'mem', pairs))  6.59 us
  transfers between devices with their start and end apart: 62, of which 18 were waited for; matrix products, arithmetic and copies ran while one was open for 12% of the time, Pallas kernels for 8%

profile of v7, /device:TPU:0, one launch (start us, length us, event | category | flops | bytes accessed | tf_op | source)
XLA Modules:
  0.0 281.3 jit_solution(2154940896698900412)
XLA Ops:
  8.3 3.3 %collective-permute-start.3 = (bf16[8,32,256]{2,0,1:T(8,128)(2,1)S(1)}, bf16[8,32,256]{2,0,1:T(8,128)(2,1)S(1)}, u32[]{:S(2)}, u32[]{:S(2)}) collective-permute-start(bf16[8,32,256]{2,0,1:T(8,128)(2,1)S(1)} %bitcast.272), channel_id=1, source_target_pairs={{0,16},{4,20},{8,24},{12,28},{16,0},{20,4},{24,8},{28,12},{1,17},{... | collective-permute-start | bytes 393224 | tf_op jit(solution)/shard_map/ppermute | solution.py:168
  12.9 3.6 %collective-permute-start.5 = (bf16[8,32,256]{2,0,1:T(8,128)(2,1)S(1)}, bf16[8,32,256]{2,0,1:T(8,128)(2,1)S(1)}, u32[]{:S(2)}, u32[]{:S(2)}) collective-permute-start(bf16[8,32,256]{2,0,1:T(8,128)(2,1)S(1)} %bitcast.227), channel_id=1, source_target_pairs={{0,24},{4,28},{8,0},{12,4},{16,8},{20,12},{24,16},{28,20},{1,25},{... | collective-permute-start | bytes 393224 | tf_op jit(solution)/shard_map/ppermute | solution.py:168
  21.6 6.5 %collective-permute-start.6 = (bf16[8,32,256]{2,0,1:T(8,128)(2,1)S(1)}, bf16[8,32,256]{2,0,1:T(8,128)(2,1)S(1)}, u32[]{:S(2)}, u32[]{:S(2)}) collective-permute-start(bf16[8,32,256]{2,0,1:T(8,128)(2,1)S(1)} %bitcast.226), channel_id=1, source_target_pairs={{0,28},{4,0},{8,4},{12,8},{16,12},{20,16},{24,20},{28,24},{1,29},{... | collective-permute-start | bytes 393224 | tf_op jit(solution)/shard_map/ppermute | solution.py:168
  28.2 3.8 %collective-permute-done.6 = bf16[8,32,256]{2,0,1:T(8,128)(2,1)S(1)} collective-permute-done((bf16[8,32,256]{2,0,1:T(8,128)(2,1)S(1)}, bf16[8,32,256]{2,0,1:T(8,128)(2,1)S(1)}, u32[]{:S(2)}, u32[]{:S(2)}) %collective-permute-start.6) | collective-permute-done | bytes 131104 | tf_op jit(solution)/shard_map/ppermute | solution.py:168
  32.1 5.2 %collective-permute-done = bf16[8,32,256]{2,0,1:T(8,128)(2,1)S(1)} collective-permute-done((bf16[8,32,256]{2,0,1:T(8,128)(2,1)S(1)}, bf16[8,32,256]{2,0,1:T(8,128)(2,1)S(1)}, u32[]{:S(2)}, u32[]{:S(2)}) %collective-permute-start) | collective-permute-done | bytes 131104 | tf_op jit(solution)/shard_map/ppermute | solution.py:168
  37.8 6.6 %collective-permute-done.2 = bf16[8,32,256]{2,0,1:T(8,128)(2,1)S(1)} collective-permute-done((bf16[8,32,256]{2,0,1:T(8,128)(2,1)S(1)}, bf16[8,32,256]{2,0,1:T(8,128)(2,1)S(1)}, u32[]{:S(2)}, u32[]{:S(2)}) %collective-permute-start.2) | collective-permute-done | bytes 131104 | tf_op jit(solution)/shard_map/ppermute | solution.py:168
  51.8 7.3 %shard_map.146 = (f32[512,512]{1,0:T(8,128)S(1)}, f32[512,512]{1,0:T(8,128)S(1)}, bf16[512,512]{1,0:T(8,128)(2,1)}, bf16[512,512]{1,0:T(8,128)(2,1)}) custom-call(bf16[512,512]{1,0:T(8,128)(2,1)S(1)} %copy-done.29, bf16[512,512]{1,0:T(8,128)(2,1)S(1)} %copy-done.27, bf16[512,512]{1,0:T(8,128)(2,1)S(1)} %copy-done.28, f32[512,512]{1,0:T(8,128)S(1)} %get-tuple-element.173.g_ref), custom_call_target="tpu_custom_call" | custom-call | flops 1610612736 | bytes 5767168 | tf_op jit(solution)/shard_map/pallas_call | solution.py:62
  61.3 2.9 %collective-permute-start.12 = (bf16[8,32,256]{2,0,1:T(8,128)(2,1)}, bf16[8,32,256]{2,0,1:T(8,128)(2,1)S(1)}, u32[]{:S(2)}, u32[]{:S(2)}) collective-permute-start(bf16[8,32,256]{2,0,1:T(8,128)(2,1)} %bitcast.21), channel_id=1, source_target_pairs={{0,12},{4,16},{8,20},{12,24},{16,28},{20,0},{24,4},{28,8},{1,13},{... | collective-permute-start | bytes 393224 | tf_op jit(solution)/shard_map/ppermute | solution.py:168
  85.6 6.4 %collective-permute-start.20 = (bf16[8,32,256]{2,0,1:T(8,128)(2,1)}, bf16[8,32,256]{2,0,1:T(8,128)(2,1)}, u32[]{:S(2)}, u32[]{:S(2)}) collective-permute-start(bf16[8,32,256]{2,0,1:T(8,128)(2,1)} %bitcast.266), channel_id=1, source_target_pairs={{0,16},{4,20},{8,24},{12,28},{16,0},{20,4},{24,8},{28,12},{1,17},{... | collective-permute-start | bytes 393224 | tf_op jit(solution)/shard_map/ppermute | solution.py:168
  91.9 3.0 %collective-permute-start.21 = (bf16[8,32,256]{2,0,1:T(8,128)(2,1)}, bf16[8,32,256]{2,0,1:T(8,128)(2,1)}, u32[]{:S(2)}, u32[]{:S(2)}) collective-permute-start(bf16[8,32,256]{2,0,1:T(8,128)(2,1)} %bitcast.265), channel_id=1, source_target_pairs={{0,20},{4,24},{8,28},{12,0},{16,4},{20,8},{24,12},{28,16},{1,21},{... | collective-permute-start | bytes 393224 | tf_op jit(solution)/shard_map/ppermute | solution.py:168
  106.1 4.4 %collective-permute-start.22 = (bf16[8,32,256]{2,0,1:T(8,128)(2,1)}, bf16[8,32,256]{2,0,1:T(8,128)(2,1)S(1)}, u32[]{:S(2)}, u32[]{:S(2)}) collective-permute-start(bf16[8,32,256]{2,0,1:T(8,128)(2,1)} %bitcast.264), channel_id=1, source_target_pairs={{0,24},{4,28},{8,0},{12,4},{16,8},{20,12},{24,16},{28,20},{1,25},{... | collective-permute-start | bytes 393224 | tf_op jit(solution)/shard_map/ppermute | solution.py:168
  129.7 13.5 %collective-permute-start.29 = (bf16[8,32,256]{2,0,1:T(8,128)(2,1)}, bf16[8,32,256]{2,0,1:T(8,128)(2,1)S(1)}, u32[]{:S(2)}, u32[]{:S(2)}) collective-permute-start(bf16[8,32,256]{2,0,1:T(8,128)(2,1)} %bitcast.240), channel_id=1, source_target_pairs={{0,24},{4,28},{8,0},{12,4},{16,8},{20,12},{24,16},{28,20},{1,25},{... | collective-permute-start | bytes 393224 | tf_op jit(solution)/shard_map/ppermute | solution.py:168
  166.5 3.7 %collective-permute-start.41 = (bf16[8,32,256]{2,0,1:T(8,128)(2,1)S(1)}, bf16[8,32,256]{2,0,1:T(8,128)(2,1)S(1)}, u32[]{:S(2)}, u32[]{:S(2)}) collective-permute-start(bf16[8,32,256]{2,0,1:T(8,128)(2,1)S(1)} %bitcast.256), channel_id=1, source_target_pairs={{0,28},{4,0},{8,4},{12,8},{16,12},{20,16},{24,20},{28,24},{1,29},{... | collective-permute-start | bytes 393224 | tf_op jit(solution)/shard_map/ppermute | solution.py:168
  172.9 3.8 %collective-permute-start.44 = (bf16[8,32,256]{2,0,1:T(8,128)(2,1)S(1)}, bf16[8,32,256]{2,0,1:T(8,128)(2,1)S(1)}, u32[]{:S(2)}, u32[]{:S(2)}) collective-permute-start(bf16[8,32,256]{2,0,1:T(8,128)(2,1)S(1)} %bitcast.247), channel_id=1, source_target_pairs={{0,16},{4,20},{8,24},{12,28},{16,0},{20,4},{24,8},{28,12},{1,17},{... | collective-permute-start | bytes 393224 | tf_op jit(solution)/shard_map/ppermute | solution.py:168
  179.2 6.3 %collective-permute-start.47 = (bf16[8,32,256]{2,0,1:T(8,128)(2,1)S(1)}, bf16[8,32,256]{2,0,1:T(8,128)(2,1)S(1)}, u32[]{:S(2)}, u32[]{:S(2)}) collective-permute-start(bf16[8,32,256]{2,0,1:T(8,128)(2,1)S(1)} %bitcast.235), channel_id=1, source_target_pairs={{0,4},{4,8},{8,12},{12,16},{16,20},{20,24},{24,28},{28,0},{1,5},{5... | collective-permute-start | bytes 393224 | tf_op jit(solution)/shard_map/ppermute | solution.py:168
  185.4 4.8 %collective-permute-start.51 = (bf16[8,32,256]{2,0,1:T(8,128)(2,1)S(1)}, bf16[8,32,256]{2,0,1:T(8,128)(2,1)S(1)}, u32[]{:S(2)}, u32[]{:S(2)}) collective-permute-start(bf16[8,32,256]{2,0,1:T(8,128)(2,1)S(1)} %bitcast.263), channel_id=1, source_target_pairs={{0,16},{4,20},{8,24},{12,28},{16,0},{20,4},{24,8},{28,12},{1,17},{... | collective-permute-start | bytes 393224 | tf_op jit(solution)/shard_map/ppermute | solution.py:168
  192.6 10.5 %collective-permute-done.45 = bf16[8,32,256]{2,0,1:T(8,128)(2,1)S(1)} collective-permute-done((bf16[8,32,256]{2,0,1:T(8,128)(2,1)S(1)}, bf16[8,32,256]{2,0,1:T(8,128)(2,1)S(1)}, u32[]{:S(2)}, u32[]{:S(2)}) %collective-permute-start.45) | collective-permute-done | bytes 131104 | tf_op jit(solution)/shard_map/ppermute | solution.py:168
  203.2 4.7 %collective-permute-start.48 = (bf16[8,32,256]{2,0,1:T(8,128)(2,1)S(1)}, bf16[8,32,256]{2,0,1:T(8,128)(2,1)S(1)}, u32[]{:S(2)}, u32[]{:S(2)}) collective-permute-start(bf16[8,32,256]{2,0,1:T(8,128)(2,1)S(1)} %bitcast.258), channel_id=1, source_target_pairs={{0,28},{4,0},{8,4},{12,8},{16,12},{20,16},{24,20},{28,24},{1,29},{... | collective-permute-start | bytes 393224 | tf_op jit(solution)/shard_map/ppermute | solution.py:168
  211.0 3.4 %collective-permute-start.56 = (bf16[8,32,256]{2,0,1:T(8,128)(2,1)S(1)}, bf16[8,32,256]{2,0,1:T(8,128)(2,1)S(1)}, u32[]{:S(2)}, u32[]{:S(2)}) collective-permute-start(bf16[8,32,256]{2,0,1:T(8,128)(2,1)S(1)} %bitcast.248), channel_id=1, source_target_pairs={{0,24},{4,28},{8,0},{12,4},{16,8},{20,12},{24,16},{28,20},{1,25},{... | collective-permute-start | bytes 393224 | tf_op jit(solution)/shard_map/ppermute | solution.py:168
  216.9 3.7 %collective-permute-start.59 = (bf16[8,32,256]{2,0,1:T(8,128)(2,1)S(1)}, bf16[8,32,256]{2,0,1:T(8,128)(2,1)S(1)}, u32[]{:S(2)}, u32[]{:S(2)}) collective-permute-start(bf16[8,32,256]{2,0,1:T(8,128)(2,1)S(1)} %bitcast.238), channel_id=1, source_target_pairs={{0,12},{4,16},{8,20},{12,24},{16,28},{20,0},{24,4},{28,8},{1,13},{... | collective-permute-start | bytes 393224 | tf_op jit(solution)/shard_map/ppermute | solution.py:168
  225.4 8.7 %collective-permute-start.61 = (bf16[8,32,256]{2,0,1:T(8,128)(2,1)S(1)}, bf16[8,32,256]{2,0,1:T(8,128)(2,1)S(1)}, u32[]{:S(2)}, u32[]{:S(2)}) collective-permute-start(bf16[8,32,256]{2,0,1:T(8,128)(2,1)S(1)} %bitcast.229), channel_id=1, source_target_pairs={{0,4},{4,8},{8,12},{12,16},{16,20},{20,24},{24,28},{28,0},{1,5},{5... | collective-permute-start | bytes 393224 | tf_op jit(solution)/shard_map/ppermute | solution.py:168
  241.4 15.1 %collective-permute-done.31 = f32[512,512]{1,0:T(8,128)S(1)} collective-permute-done((f32[512,512]{1,0:T(8,128)S(1)}, f32[512,512]{1,0:T(8,128)S(1)}, u32[]{:S(2)}, u32[]{:S(2)}) %collective-permute-start.31) | collective-permute-done | bytes 1048608 | tf_op jit(solution)/shard_map/ppermute | solution.py:250
  256.5 6.1 %collective-permute-done.32 = f32[512,512]{1,0:T(8,128)S(1)} collective-permute-done((f32[512,512]{1,0:T(8,128)S(1)}, f32[512,512]{1,0:T(8,128)S(1)}, u32[]{:S(2)}, u32[]{:S(2)}) %collective-permute-start.32) | collective-permute-done | bytes 1048608 | tf_op jit(solution)/shard_map/ppermute | solution.py:250
  262.6 17.5 %collective-permute-done.33 = f32[512,512]{1,0:T(8,128)S(1)} collective-permute-done((f32[512,512]{1,0:T(8,128)S(1)}, f32[512,512]{1,0:T(8,128)S(1)}, u32[]{:S(2)}, u32[]{:S(2)}) %collective-permute-start.33) | collective-permute-done | bytes 1048608 | tf_op jit(solution)/shard_map/ppermute | solution.py:250
  (296 shorter events, 125.0 us)
Async XLA Ops:
  0.6 47.7 %collective-permute-start.7 = (bf16[512,512]{1,0:T(8,128)(2,1)}, bf16[512,512]{1,0:T(8,128)(2,1)}, u32[]{:S(2)}, u32[]{:S(2)}) collective-permute-start(bf16[512,512]{1,0:T(8,128)(2,1)} %param.19), channel_id=1, source_target_pairs={{0,1},{1,2},{2,3},{3,0},{4,5},{5,6},{6,7},{7,4},{8,9},{9,10},{10,1... | collective-permute-start | bytes 1572872 | tf_op jit(solution)/shard_map/ppermute | solution.py:198
  1.2 45.5 %collective-permute-start.9 = (bf16[512,512]{1,0:T(8,128)(2,1)}, bf16[512,512]{1,0:T(8,128)(2,1)}, u32[]{:S(2)}, u32[]{:S(2)}) collective-permute-start(bf16[512,512]{1,0:T(8,128)(2,1)} %param.19), channel_id=1, source_target_pairs={{0,3},{1,0},{2,1},{3,2},{4,7},{5,4},{6,5},{7,6},{8,11},{9,8},{10,9... | collective-permute-start | bytes 1572872 | tf_op jit(solution)/shard_map/ppermute | solution.py:198
  80.7 25.5 %collective-permute-start.17 = (bf16[8,32,256]{2,0,1:T(8,128)(2,1)}, bf16[8,32,256]{2,0,1:T(8,128)(2,1)}, u32[]{:S(2)}, u32[]{:S(2)}) collective-permute-start(bf16[8,32,256]{2,0,1:T(8,128)(2,1)} %bitcast.269), channel_id=1, source_target_pairs={{0,4},{4,8},{8,12},{12,16},{16,20},{20,24},{24,28},{28,0},{1,5},{5... | collective-permute-start | bytes 393224 | tf_op jit(solution)/shard_map/ppermute | solution.py:168
  81.4 29.2 %collective-permute-start.18 = (bf16[8,32,256]{2,0,1:T(8,128)(2,1)}, bf16[8,32,256]{2,0,1:T(8,128)(2,1)}, u32[]{:S(2)}, u32[]{:S(2)}) collective-permute-start(bf16[8,32,256]{2,0,1:T(8,128)(2,1)} %bitcast.268), channel_id=1, source_target_pairs={{0,8},{4,12},{8,16},{12,20},{16,24},{20,28},{24,0},{28,4},{1,9},{5... | collective-permute-start | bytes 393224 | tf_op jit(solution)/shard_map/ppermute | solution.py:168
  83.3 27.9 %collective-permute-start.19 = (bf16[8,32,256]{2,0,1:T(8,128)(2,1)}, bf16[8,32,256]{2,0,1:T(8,128)(2,1)}, u32[]{:S(2)}, u32[]{:S(2)}) collective-permute-start(bf16[8,32,256]{2,0,1:T(8,128)(2,1)} %bitcast.267), channel_id=1, source_target_pairs={{0,12},{4,16},{8,20},{12,24},{16,28},{20,0},{24,4},{28,8},{1,13},{... | collective-permute-start | bytes 393224 | tf_op jit(solution)/shard_map/ppermute | solution.py:168
  85.6 27.7 %collective-permute-start.20 = (bf16[8,32,256]{2,0,1:T(8,128)(2,1)}, bf16[8,32,256]{2,0,1:T(8,128)(2,1)}, u32[]{:S(2)}, u32[]{:S(2)}) collective-permute-start(bf16[8,32,256]{2,0,1:T(8,128)(2,1)} %bitcast.266), channel_id=1, source_target_pairs={{0,16},{4,20},{8,24},{12,28},{16,0},{20,4},{24,8},{28,12},{1,17},{... | collective-permute-start | bytes 393224 | tf_op jit(solution)/shard_map/ppermute | solution.py:168
  91.9 21.3 %collective-permute-start.21 = (bf16[8,32,256]{2,0,1:T(8,128)(2,1)}, bf16[8,32,256]{2,0,1:T(8,128)(2,1)}, u32[]{:S(2)}, u32[]{:S(2)}) collective-permute-start(bf16[8,32,256]{2,0,1:T(8,128)(2,1)} %bitcast.265), channel_id=1, source_target_pairs={{0,20},{4,24},{8,28},{12,0},{16,4},{20,8},{24,12},{28,16},{1,21},{... | collective-permute-start | bytes 393224 | tf_op jit(solution)/shard_map/ppermute | solution.py:168
  113.2 30.0 %collective-permute-start.25 = (bf16[8,32,256]{2,0,1:T(8,128)(2,1)}, bf16[8,32,256]{2,0,1:T(8,128)(2,1)}, u32[]{:S(2)}, u32[]{:S(2)}) collective-permute-start(bf16[8,32,256]{2,0,1:T(8,128)(2,1)} %bitcast.254), channel_id=1, source_target_pairs={{0,8},{4,12},{8,16},{12,20},{16,24},{20,28},{24,0},{28,4},{1,9},{5... | collective-permute-start | bytes 393224 | tf_op jit(solution)/shard_map/ppermute | solution.py:168
  113.2 30.5 %collective-permute-start.26 = (bf16[8,32,256]{2,0,1:T(8,128)(2,1)}, bf16[8,32,256]{2,0,1:T(8,128)(2,1)}, u32[]{:S(2)}, u32[]{:S(2)}) collective-permute-start(bf16[8,32,256]{2,0,1:T(8,128)(2,1)} %bitcast.249), channel_id=1, source_target_pairs={{0,12},{4,16},{8,20},{12,24},{16,28},{20,0},{24,4},{28,8},{1,13},{... | collective-permute-start | bytes 393224 | tf_op jit(solution)/shard_map/ppermute | solution.py:168
  114.8 30.5 %collective-permute-start.27 = (bf16[8,32,256]{2,0,1:T(8,128)(2,1)}, bf16[8,32,256]{2,0,1:T(8,128)(2,1)}, u32[]{:S(2)}, u32[]{:S(2)}) collective-permute-start(bf16[8,32,256]{2,0,1:T(8,128)(2,1)} %bitcast.246), channel_id=1, source_target_pairs={{0,16},{4,20},{8,24},{12,28},{16,0},{20,4},{24,8},{28,12},{1,17},{... | collective-permute-start | bytes 393224 | tf_op jit(solution)/shard_map/ppermute | solution.py:168
  117.6 27.7 %collective-permute-start.28 = (bf16[8,32,256]{2,0,1:T(8,128)(2,1)}, bf16[8,32,256]{2,0,1:T(8,128)(2,1)}, u32[]{:S(2)}, u32[]{:S(2)}) collective-permute-start(bf16[8,32,256]{2,0,1:T(8,128)(2,1)} %bitcast.243), channel_id=1, source_target_pairs={{0,20},{4,24},{8,28},{12,0},{16,4},{20,8},{24,12},{28,16},{1,21},{... | collective-permute-start | bytes 393224 | tf_op jit(solution)/shard_map/ppermute | solution.py:168
  143.8 20.8 %collective-permute-start.34 = (bf16[8,32,256]{2,0,1:T(8,128)(2,1)}, bf16[8,32,256]{2,0,1:T(8,128)(2,1)}, u32[]{:S(2)}, u32[]{:S(2)}) collective-permute-start(bf16[8,32,256]{2,0,1:T(8,128)(2,1)} %bitcast.244), channel_id=1, source_target_pairs={{0,28},{4,0},{8,4},{12,8},{16,12},{20,16},{24,20},{28,24},{1,29},{... | collective-permute-start | bytes 393224 | tf_op jit(solution)/shard_map/ppermute | solution.py:168
  145.4 21.2 %collective-permute-start.36 = (bf16[8,32,256]{2,0,1:T(8,128)(2,1)}, bf16[8,32,256]{2,0,1:T(8,128)(2,1)}, u32[]{:S(2)}, u32[]{:S(2)}) collective-permute-start(bf16[8,32,256]{2,0,1:T(8,128)(2,1)} %bitcast.234), channel_id=1, source_target_pairs={{0,20},{4,24},{8,28},{12,0},{16,4},{20,8},{24,12},{28,16},{1,21},{... | collective-permute-start | bytes 393224 | tf_op jit(solution)/shard_map/ppermute | solution.py:168
  147.0 23.3 %collective-permute-start.37 = (bf16[8,32,256]{2,0,1:T(8,128)(2,1)}, bf16[8,32,256]{2,0,1:T(8,128)(2,1)}, u32[]{:S(2)}, u32[]{:S(2)}) collective-permute-start(bf16[8,32,256]{2,0,1:T(8,128)(2,1)} %bitcast.233), channel_id=1, source_target_pairs={{0,16},{4,20},{8,24},{12,28},{16,0},{20,4},{24,8},{28,12},{1,17},{... | collective-permute-start | bytes 393224 | tf_op jit(solution)/shard_map/ppermute | solution.py:168
  148.8 23.1 %collective-permute-start.38 = (bf16[8,32,256]{2,0,1:T(8,128)(2,1)}, bf16[8,32,256]{2,0,1:T(8,128)(2,1)}, u32[]{:S(2)}, u32[]{:S(2)}) collective-permute-start(bf16[8,32,256]{2,0,1:T(8,128)(2,1)} %bitcast.232), channel_id=1, source_target_pairs={{0,12},{4,16},{8,20},{12,24},{16,28},{20,0},{24,4},{28,8},{1,13},{... | collective-permute-start | bytes 393224 | tf_op jit(solution)/shard_map/ppermute | solution.py:168
  177.2 25.9 %collective-permute-start.45 = (bf16[8,32,256]{2,0,1:T(8,128)(2,1)S(1)}, bf16[8,32,256]{2,0,1:T(8,128)(2,1)S(1)}, u32[]{:S(2)}, u32[]{:S(2)}) collective-permute-start(bf16[8,32,256]{2,0,1:T(8,128)(2,1)S(1)} %bitcast.242), channel_id=1, source_target_pairs={{0,12},{4,16},{8,20},{12,24},{16,28},{20,0},{24,4},{28,8},{1,13},{... | collective-permute-start | bytes 393224 | tf_op jit(solution)/shard_map/ppermute | solution.py:168
  178.4 24.7 %collective-permute-start.46 = (bf16[8,32,256]{2,0,1:T(8,128)(2,1)S(1)}, bf16[8,32,256]{2,0,1:T(8,128)(2,1)S(1)}, u32[]{:S(2)}, u32[]{:S(2)}) collective-permute-start(bf16[8,32,256]{2,0,1:T(8,128)(2,1)S(1)} %bitcast.239), channel_id=1, source_target_pairs={{0,8},{4,12},{8,16},{12,20},{16,24},{20,28},{24,0},{28,4},{1,9},{5... | collective-permute-start | bytes 393224 | tf_op jit(solution)/shard_map/ppermute | solution.py:168
  179.2 24.0 %collective-permute-start.47 = (bf16[8,32,256]{2,0,1:T(8,128)(2,1)S(1)}, bf16[8,32,256]{2,0,1:T(8,128)(2,1)S(1)}, u32[]{:S(2)}, u32[]{:S(2)}) collective-permute-start(bf16[8,32,256]{2,0,1:T(8,128)(2,1)S(1)} %bitcast.235), channel_id=1, source_target_pairs={{0,4},{4,8},{8,12},{12,16},{16,20},{20,24},{24,28},{28,0},{1,5},{5... | collective-permute-start | bytes 393224 | tf_op jit(solution)/shard_map/ppermute | solution.py:168
  185.4 22.5 %collective-permute-start.51 = (bf16[8,32,256]{2,0,1:T(8,128)(2,1)S(1)}, bf16[8,32,256]{2,0,1:T(8,128)(2,1)S(1)}, u32[]{:S(2)}, u32[]{:S(2)}) collective-permute-start(bf16[8,32,256]{2,0,1:T(8,128)(2,1)S(1)} %bitcast.263), channel_id=1, source_target_pairs={{0,16},{4,20},{8,24},{12,28},{16,0},{20,4},{24,8},{28,12},{1,17},{... | collective-permute-start | bytes 393224 | tf_op jit(solution)/shard_map/ppermute | solution.py:168
  214.9 21.7 %collective-permute-start.58 = (bf16[8,32,256]{2,0,1:T(8,128)(2,1)S(1)}, bf16[8,32,256]{2,0,1:T(8,128)(2,1)S(1)}, u32[]{:S(2)}, u32[]{:S(2)}) collective-permute-start(bf16[8,32,256]{2,0,1:T(8,128)(2,1)S(1)} %bitcast.241), channel_id=1, source_target_pairs={{0,16},{4,20},{8,24},{12,28},{16,0},{20,4},{24,8},{28,12},{1,17},{... | collective-permute-start | bytes 393224 | tf_op jit(solution)/shard_map/ppermute | solution.py:168
  216.9 20.2 %collective-permute-start.59 = (bf16[8,32,256]{2,0,1:T(8,128)(2,1)S(1)}, bf16[8,32,256]{2,0,1:T(8,128)(2,1)S(1)}, u32[]{:S(2)}, u32[]{:S(2)}) collective-permute-start(bf16[8,32,256]{2,0,1:T(8,128)(2,1)S(1)} %bitcast.238), channel_id=1, source_target_pairs={{0,12},{4,16},{8,20},{12,24},{16,28},{20,0},{24,4},{28,8},{1,13},{... | collective-permute-start | bytes 393224 | tf_op jit(solution)/shard_map/ppermute | solution.py:168
  234.1 22.4 %collective-permute-start.31 = (f32[512,512]{1,0:T(8,128)S(1)}, f32[512,512]{1,0:T(8,128)S(1)}, u32[]{:S(2)}, u32[]{:S(2)}) collective-permute-start(f32[512,512]{1,0:T(8,128)S(1)} %fusion.15), channel_id=1, source_target_pairs={{0,1},{1,2},{2,3},{3,0},{4,5},{5,6},{6,7},{7,4},{8,9},{9,10},{10,1... | collective-permute-start | bytes 3145736 | tf_op jit(solution)/shard_map/ppermute | solution.py:250
  236.5 26.0 %collective-permute-start.32 = (f32[512,512]{1,0:T(8,128)S(1)}, f32[512,512]{1,0:T(8,128)S(1)}, u32[]{:S(2)}, u32[]{:S(2)}) collective-permute-start(f32[512,512]{1,0:T(8,128)S(1)} %fusion.13), channel_id=1, source_target_pairs={{0,2},{1,3},{2,0},{3,1},{4,6},{5,7},{6,4},{7,5},{8,10},{9,11},{10,... | collective-permute-start | bytes 3145736 | tf_op jit(solution)/shard_map/ppermute | solution.py:250
  237.1 43.0 %collective-permute-start.33 = (f32[512,512]{1,0:T(8,128)S(1)}, f32[512,512]{1,0:T(8,128)S(1)}, u32[]{:S(2)}, u32[]{:S(2)}) collective-permute-start(f32[512,512]{1,0:T(8,128)S(1)} %fusion.11), channel_id=1, source_target_pairs={{0,3},{1,0},{2,1},{3,2},{4,7},{5,4},{6,5},{7,6},{8,11},{9,8},{10,9... | collective-permute-start | bytes 3145736 | tf_op jit(solution)/shard_map/ppermute | solution.py:250
  (93 other events, 1064.3 us)

commit v8 on v7

--- a/solution.py
+++ b/solution.py
@@ -9,7 +9,7 @@
 
 
 QBLK = 512
-CHUNKS = 4
+CHUNKS = 2
 
 
 keep_scale = 1.0 / 0.9
@@ -156,7 +156,7 @@
     gate_cols = jnp.repeat(gate_values, head_dim)[None, :]
     keep_mask = dropout_keep.astype(jnp.float32)
 
-    chunk_heads = max(1, heads_here // CHUNKS)
+    chunk_heads = heads_here // CHUNKS if heads_here % CHUNKS == 0 else heads_here
     chunk_count = heads_here // chunk_heads
     chunk_cols = chunk_heads * head_dim
     entries2 = block_len * 2 * chunk_cols
@@ -209,10 +209,6 @@
         queries, grad_loc, local_keys, local_values, heads_here, head_dim, True
     )
 
-    if chunk_count > 1:
-        memory_keys, memory_values, o_loc, q_loc, k_loc, v_loc, grad_mem = lax.optimization_barrier(
-            (memory_keys, memory_values, o_loc, q_loc, k_loc, v_loc, grad_mem)
-        )
     o_mem_parts, q_mem_parts, summed_parts = [], [], []
     for chunk in range(chunk_count):
         if chunk + 1 < chunk_count:

time: 284 us -> 268 us (0.944)
  starting transfers between devices: 124 us -> 80.2 us
  waiting for transfers between devices: 75 us -> 102 us
    ppermute x56 -> x28, waiting for transfers between devices: 36.3 us -> 87.2 us  [exchange(): pieces.append(lax.ppermute(buffer[shift], 'mem', pairs))]
    ppermute x56 -> x28, starting transfers between devices: 120 us -> 75.7 us  [exchange(): pieces.append(lax.ppermute(buffer[shift], 'mem', pairs))]
    ppermute x3, waiting for transfers between devices: 38.7 us -> 14.9 us  [per_device(): part = lax.ppermute(part, 'head', pairs)]
    unnamed x118 -> x78, local copies, waits for them, and re-layouts: 12.3 us -> 15.4 us
    pallas_call x8 -> x4, Pallas kernels: 12.4 us -> 9.55 us  [gather_pieces(): pl.pallas_call(_gather_kernel, in_specs=[whole] * (1 + len(pieces)), out_...]
    slice x8 -> x4, local copies, waits for them, and re-layouts: 6.59 us -> 4.1 us  [exchange(): pieces.append(lax.ppermute(buffer[shift], 'mem', pairs))]
    pallas_call x5 -> x3, Pallas kernels: 17.6 us -> 18.4 us  [attention_branch(): pl.pallas_call(kernel, grid=(heads,), in_specs=[spec(rows, q_off), spec(k...]
  transfers between devices with their start and end apart: 62 -> 34, of which waited for: 18 -> 11; matrix products, arithmetic and copies ran while one was open for 12% -> 11% of each run, Pallas kernels for 8% -> 11%
where the time goes in v8:
time: 268 us; the launch traced here: 265 us
  waiting for transfers between devices  102 us (38%)
  starting transfers between devices  80.2 us (30%)
  local copies, waits for them, and re-layouts  29.3 us (11%)
  Pallas kernels  27.9 us (10%)
  matrix products  16.5 us (6%)
  other arithmetic  7.97 us (3%)
    ppermute x28, waiting for transfers between devices, exchange(): pieces.append(lax.ppermute(buffer[shift], 'mem', pairs))  87.2 us
    ppermute x28, starting transfers between devices, exchange(): pieces.append(lax.ppermute(buffer[shift], 'mem', pairs))  75.7 us
    pallas_call x3, Pallas kernels, attention_branch(): pl.pallas_call(kernel, grid=(heads,), in_specs=[spec(rows, q_off), spec(k...  18.4 us
    unnamed x78, local copies, waits for them, and re-layouts  15.4 us
    ppermute x3, waiting for transfers between devices, per_device(): part = lax.ppermute(part, 'head', pairs)  14.9 us
    pallas_call x4, Pallas kernels, gather_pieces(): pl.pallas_call(_gather_kernel, in_specs=[whole] * (1 + len(pieces)), out_...  9.55 us
    dot_general x4, matrix products, per_device(): lax.dot_general(piece, weight_cols(owner), (((1,), (1,)), ((), ())), pref...  8.41 us
  transfers between devices with their start and end apart: 34, of which 11 were waited for; matrix products, arithmetic and copies ran while one was open for 11% of the time, Pallas kernels for 11%

profile of v8, /device:TPU:0, one launch (start us, length us, event | category | flops | bytes accessed | tf_op | source)
XLA Modules:
  0.0 265.4 jit_solution(7337514595472476714)
XLA Ops:
  8.1 4.1 %collective-permute-start.3 = (bf16[8,32,512]{2,0,1:T(8,128)(2,1)}, bf16[8,32,512]{2,0,1:T(8,128)(2,1)S(1)}, u32[]{:S(2)}, u32[]{:S(2)}) collective-permute-start(bf16[8,32,512]{2,0,1:T(8,128)(2,1)} %bitcast.9), channel_id=1, source_target_pairs={{0,16},{4,20},{8,24},{12,28},{16,0},{20,4},{24,8},{28,12},{1,17},{... | collective-permute-start | bytes 786440 | tf_op jit(solution)/shard_map/ppermute | solution.py:168
  13.4 3.6 %collective-permute-start.5 = (bf16[8,32,512]{2,0,1:T(8,128)(2,1)}, bf16[8,32,512]{2,0,1:T(8,128)(2,1)S(1)}, u32[]{:S(2)}, u32[]{:S(2)}) collective-permute-start(bf16[8,32,512]{2,0,1:T(8,128)(2,1)} %bitcast.13), channel_id=1, source_target_pairs={{0,24},{4,28},{8,0},{12,4},{16,8},{20,12},{24,16},{28,20},{1,25},{... | collective-permute-start | bytes 786440 | tf_op jit(solution)/shard_map/ppermute | solution.py:168
  21.2 9.7 %collective-permute-done.3 = bf16[8,32,512]{2,0,1:T(8,128)(2,1)S(1)} collective-permute-done((bf16[8,32,512]{2,0,1:T(8,128)(2,1)}, bf16[8,32,512]{2,0,1:T(8,128)(2,1)S(1)}, u32[]{:S(2)}, u32[]{:S(2)}) %collective-permute-start.3) | collective-permute-done | bytes 262176 | tf_op jit(solution)/shard_map/ppermute | solution.py:168
  30.9 7.0 %collective-permute-start = (bf16[8,32,512]{2,0,1:T(8,128)(2,1)}, bf16[8,32,512]{2,0,1:T(8,128)(2,1)S(1)}, u32[]{:S(2)}, u32[]{:S(2)}) collective-permute-start(bf16[8,32,512]{2,0,1:T(8,128)(2,1)} %bitcast.129), channel_id=1, source_target_pairs={{0,4},{4,8},{8,12},{12,16},{16,20},{20,24},{24,28},{28,0},{1,5},{5... | collective-permute-start | bytes 786440 | tf_op jit(solution)/shard_map/ppermute | solution.py:168
  37.9 9.8 %collective-permute-start.1 = (bf16[8,32,512]{2,0,1:T(8,128)(2,1)}, bf16[8,32,512]{2,0,1:T(8,128)(2,1)S(1)}, u32[]{:S(2)}, u32[]{:S(2)}) collective-permute-start(bf16[8,32,512]{2,0,1:T(8,128)(2,1)} %bitcast.128), channel_id=1, source_target_pairs={{0,8},{4,12},{8,16},{12,20},{16,24},{20,28},{24,0},{28,4},{1,9},{5... | collective-permute-start | bytes 786440 | tf_op jit(solution)/shard_map/ppermute | solution.py:168
  50.8 7.9 %collective-permute-done = bf16[8,32,512]{2,0,1:T(8,128)(2,1)S(1)} collective-permute-done((bf16[8,32,512]{2,0,1:T(8,128)(2,1)}, bf16[8,32,512]{2,0,1:T(8,128)(2,1)S(1)}, u32[]{:S(2)}, u32[]{:S(2)}) %collective-permute-start) | collective-permute-done | bytes 262176 | tf_op jit(solution)/shard_map/ppermute | solution.py:168
  60.1 4.7 %collective-permute-start.10 = (bf16[8,32,512]{2,0,1:T(8,128)(2,1)}, bf16[8,32,512]{2,0,1:T(8,128)(2,1)}, u32[]{:S(2)}, u32[]{:S(2)}) collective-permute-start(bf16[8,32,512]{2,0,1:T(8,128)(2,1)} %bitcast.19), channel_id=1, source_target_pairs={{0,4},{4,8},{8,12},{12,16},{16,20},{20,24},{24,28},{28,0},{1,5},{5... | collective-permute-start | bytes 786440 | tf_op jit(solution)/shard_map/ppermute | solution.py:168
  64.8 26.8 %collective-permute-done.2 = bf16[8,32,512]{2,0,1:T(8,128)(2,1)S(1)} collective-permute-done((bf16[8,32,512]{2,0,1:T(8,128)(2,1)}, bf16[8,32,512]{2,0,1:T(8,128)(2,1)S(1)}, u32[]{:S(2)}, u32[]{:S(2)}) %collective-permute-start.2) | collective-permute-done | bytes 262176 | tf_op jit(solution)/shard_map/ppermute | solution.py:168
  103.6 3.6 %collective-permute-start.14 = (bf16[8,32,512]{2,0,1:T(8,128)(2,1)}, bf16[8,32,512]{2,0,1:T(8,128)(2,1)}, u32[]{:S(2)}, u32[]{:S(2)}) collective-permute-start(bf16[8,32,512]{2,0,1:T(8,128)(2,1)} %bitcast.23), channel_id=1, source_target_pairs={{0,20},{4,24},{8,28},{12,0},{16,4},{20,8},{24,12},{28,16},{1,21},{... | collective-permute-start | bytes 786440 | tf_op jit(solution)/shard_map/ppermute | solution.py:168
  109.9 5.6 %shard_map.146 = (f32[512,256]{1,0:T(8,128)S(1)}, f32[512,256]{1,0:T(8,128)S(1)}, bf16[1024,256]{1,0:T(8,128)(2,1)S(1)}, bf16[1024,256]{1,0:T(8,128)(2,1)S(1)}) custom-call(bf16[512,512]{1,0:T(8,128)(2,1)S(1)} %copy-done.24, bf16[1024,512]{1,0:T(8,128)(2,1)S(1)} %copy-done.2, bf16[1024,512]{1,0:T(8,128)(2,1)S(1)} %copy-done.2, ...), custom_call_target="tpu_custom_call" | custom-call | flops 1610612736 | bytes 3932160 | tf_op jit(solution)/shard_map/pallas_call | solution.py:62
  120.5 3.8 %collective-permute-start.15 = (bf16[8,32,512]{2,0,1:T(8,128)(2,1)S(1)}, bf16[8,32,512]{2,0,1:T(8,128)(2,1)S(1)}, u32[]{:S(2)}, u32[]{:S(2)}) collective-permute-start(bf16[8,32,512]{2,0,1:T(8,128)(2,1)S(1)} %bitcast.125), channel_id=1, source_target_pairs={{0,24},{4,28},{8,0},{12,4},{16,8},{20,12},{24,16},{28,20},{1,25},{... | collective-permute-start | bytes 786440 | tf_op jit(solution)/shard_map/ppermute | solution.py:168
  127.3 11.1 %collective-permute-done.15 = bf16[8,32,512]{2,0,1:T(8,128)(2,1)S(1)} collective-permute-done((bf16[8,32,512]{2,0,1:T(8,128)(2,1)S(1)}, bf16[8,32,512]{2,0,1:T(8,128)(2,1)S(1)}, u32[]{:S(2)}, u32[]{:S(2)}) %collective-permute-start.15) | collective-permute-done | bytes 262176 | tf_op jit(solution)/shard_map/ppermute | solution.py:168
  139.9 5.3 %collective-permute-start.20 = (bf16[8,32,512]{2,0,1:T(8,128)(2,1)}, bf16[8,32,512]{2,0,1:T(8,128)(2,1)}, u32[]{:S(2)}, u32[]{:S(2)}) collective-permute-start(bf16[8,32,512]{2,0,1:T(8,128)(2,1)} %bitcast.34), channel_id=1, source_target_pairs={{0,28},{4,0},{8,4},{12,8},{16,12},{20,16},{24,20},{28,24},{1,29},{... | collective-permute-start | bytes 786440 | tf_op jit(solution)/shard_map/ppermute | solution.py:168
  154.6 3.4 %shard_map.147 = bf16[32,16384]{1,0:T(8,128)(2,1)S(1)} custom-call(f32[64,32]{1,0:T(8,128)S(1)} %fusion.27.refs_0_, bf16[8,16384]{1,0:T(8,128)(2,1)S(1)} %get-tuple-element.73, bf16[8,16384]{1,0:T(8,128)(2,1)} %bitcast.27.refs_2_, bf16[8,16384]{1,0:T(8,128)(2,1)} %bitcast.28.refs_3_, bf16[8,16384]{1,0:T(8,128)(2,1)S(1)} %bitcast.102, ...), custom_call_target="tpu_custom_call" | custom-call | flops 67108864 | bytes 3145728 | tf_op jit(solution)/shard_map/pallas_call | solution.py:99
  162.9 5.5 %shard_map.148 = (f32[512,256]{1,0:T(8,128)S(1)}, f32[512,256]{1,0:T(8,128)S(1)}, bf16[1024,256]{1,0:T(8,128)(2,1)S(1)}, bf16[1024,256]{1,0:T(8,128)(2,1)S(1)}) custom-call(bf16[512,512]{1,0:T(8,128)(2,1)S(1)} %copy-done.25, bf16[1024,512]{1,0:T(8,128)(2,1)S(1)} %copy-done.3, bf16[1024,512]{1,0:T(8,128)(2,1)S(1)} %copy-done.3, f32[512,512]{1,0:T(8,128)S(1)} %copy-done.6), custom_call_target="tpu_custom_call" | custom-call | flops 1610612736 | bytes 3932160 | tf_op jit(solution)/shard_map/pallas_call | solution.py:62
  175.6 7.3 %shard_map.149 = (f32[512,512]{1,0:T(8,128)S(1)}, f32[512,512]{1,0:T(8,128)S(1)}, bf16[512,512]{1,0:T(8,128)(2,1)}, bf16[512,512]{1,0:T(8,128)(2,1)}) custom-call(bf16[512,512]{1,0:T(8,128)(2,1)S(1)} %copy-done.26, bf16[512,512]{1,0:T(8,128)(2,1)S(1)} %copy-done.27, bf16[512,512]{1,0:T(8,128)(2,1)S(1)} %copy-done.28, f32[512,512]{1,0:T(8,128)S(1)} %copy-done.4), custom_call_target="tpu_custom_call" | custom-call | flops 1610612736 | bytes 5767168 | tf_op jit(solution)/shard_map/pallas_call | solution.py:62
  185.9 4.8 %collective-permute-start.27 = (bf16[8,32,512]{2,0,1:T(8,128)(2,1)S(1)}, bf16[8,32,512]{2,0,1:T(8,128)(2,1)S(1)}, u32[]{:S(2)}, u32[]{:S(2)}) collective-permute-start(bf16[8,32,512]{2,0,1:T(8,128)(2,1)S(1)} %bitcast.138), channel_id=1, source_target_pairs={{0,28},{4,0},{8,4},{12,8},{16,12},{20,16},{24,20},{28,24},{1,29},{... | collective-permute-start | bytes 786440 | tf_op jit(solution)/shard_map/ppermute | solution.py:168
  190.6 4.6 %collective-permute-done.23 = bf16[8,32,512]{2,0,1:T(8,128)(2,1)} collective-permute-done((bf16[8,32,512]{2,0,1:T(8,128)(2,1)}, bf16[8,32,512]{2,0,1:T(8,128)(2,1)}, u32[]{:S(2)}, u32[]{:S(2)}) %collective-permute-start.23) | collective-permute-done | bytes 262176 | tf_op jit(solution)/shard_map/ppermute | solution.py:168
  195.3 4.7 %collective-permute-done.26 = bf16[8,32,512]{2,0,1:T(8,128)(2,1)S(1)} collective-permute-done((bf16[8,32,512]{2,0,1:T(8,128)(2,1)S(1)}, bf16[8,32,512]{2,0,1:T(8,128)(2,1)S(1)}, u32[]{:S(2)}, u32[]{:S(2)}) %collective-permute-start.26) | collective-permute-done | bytes 262176 | tf_op jit(solution)/shard_map/ppermute | solution.py:168
  200.0 16.7 %collective-permute-start.31 = (bf16[8,32,512]{2,0,1:T(8,128)(2,1)S(1)}, bf16[8,32,512]{2,0,1:T(8,128)(2,1)S(1)}, u32[]{:S(2)}, u32[]{:S(2)}) collective-permute-start(bf16[8,32,512]{2,0,1:T(8,128)(2,1)S(1)} %bitcast.134), channel_id=1, source_target_pairs={{0,12},{4,16},{8,20},{12,24},{16,28},{20,0},{24,4},{28,8},{1,13},{... | collective-permute-start | bytes 786440 | tf_op jit(solution)/shard_map/ppermute | solution.py:168
  220.2 13.2 %collective-permute-done.30 = bf16[8,32,512]{2,0,1:T(8,128)(2,1)S(1)} collective-permute-done((bf16[8,32,512]{2,0,1:T(8,128)(2,1)S(1)}, bf16[8,32,512]{2,0,1:T(8,128)(2,1)S(1)}, u32[]{:S(2)}, u32[]{:S(2)}) %collective-permute-start.30) | collective-permute-done | bytes 262176 | tf_op jit(solution)/shard_map/ppermute | solution.py:168
  237.1 5.5 %collective-permute-done.32 = bf16[8,32,512]{2,0,1:T(8,128)(2,1)S(1)} collective-permute-done((bf16[8,32,512]{2,0,1:T(8,128)(2,1)S(1)}, bf16[8,32,512]{2,0,1:T(8,128)(2,1)S(1)}, u32[]{:S(2)}, u32[]{:S(2)}) %collective-permute-start.32) | collective-permute-done | bytes 262176 | tf_op jit(solution)/shard_map/ppermute | solution.py:168
  242.6 3.3 %collective-permute-done.33 = bf16[8,32,512]{2,0,1:T(8,128)(2,1)S(1)} collective-permute-done((bf16[8,32,512]{2,0,1:T(8,128)(2,1)S(1)}, bf16[8,32,512]{2,0,1:T(8,128)(2,1)S(1)}, u32[]{:S(2)}, u32[]{:S(2)}) %collective-permute-start.33) | collective-permute-done | bytes 262176 | tf_op jit(solution)/shard_map/ppermute | solution.py:168
  249.2 14.9 %collective-permute-done.19 = f32[512,512]{1,0:T(8,128)S(1)} collective-permute-done((f32[512,512]{1,0:T(8,128)S(1)}, f32[512,512]{1,0:T(8,128)S(1)}, u32[]{:S(2)}, u32[]{:S(2)}) %collective-permute-start.19) | collective-permute-done | bytes 1048608 | tf_op jit(solution)/shard_map/ppermute | solution.py:246
  (174 shorter events, 77.2 us)
Async XLA Ops:
  13.4 24.4 %collective-permute-start.5 = (bf16[8,32,512]{2,0,1:T(8,128)(2,1)}, bf16[8,32,512]{2,0,1:T(8,128)(2,1)S(1)}, u32[]{:S(2)}, u32[]{:S(2)}) collective-permute-start(bf16[8,32,512]{2,0,1:T(8,128)(2,1)} %bitcast.13), channel_id=1, source_target_pairs={{0,24},{4,28},{8,0},{12,4},{16,8},{20,12},{24,16},{28,20},{1,25},{... | collective-permute-start | bytes 786440 | tf_op jit(solution)/shard_map/ppermute | solution.py:168
  17.0 30.6 %collective-permute-start.6 = (bf16[8,32,512]{2,0,1:T(8,128)(2,1)}, bf16[8,32,512]{2,0,1:T(8,128)(2,1)S(1)}, u32[]{:S(2)}, u32[]{:S(2)}) collective-permute-start(bf16[8,32,512]{2,0,1:T(8,128)(2,1)} %bitcast.15), channel_id=1, source_target_pairs={{0,28},{4,0},{8,4},{12,8},{16,12},{20,16},{24,20},{28,24},{1,29},{... | collective-permute-start | bytes 786440 | tf_op jit(solution)/shard_map/ppermute | solution.py:168
  17.5 82.5 %collective-permute-start.9 = (bf16[512,512]{1,0:T(8,128)(2,1)}, bf16[512,512]{1,0:T(8,128)(2,1)}, u32[]{:S(2)}, u32[]{:S(2)}) collective-permute-start(bf16[512,512]{1,0:T(8,128)(2,1)} %param.19), channel_id=1, source_target_pairs={{0,3},{1,0},{2,1},{3,2},{4,7},{5,4},{6,5},{7,6},{8,11},{9,8},{10,9... | collective-permute-start | bytes 1572872 | tf_op jit(solution)/shard_map/ppermute | solution.py:198
  30.8 71.0 %collective-permute-start.7 = (bf16[512,512]{1,0:T(8,128)(2,1)}, bf16[512,512]{1,0:T(8,128)(2,1)}, u32[]{:S(2)}, u32[]{:S(2)}) collective-permute-start(bf16[512,512]{1,0:T(8,128)(2,1)} %param.19), channel_id=1, source_target_pairs={{0,1},{1,2},{2,3},{3,0},{4,5},{5,6},{6,7},{7,4},{8,9},{9,10},{10,1... | collective-permute-start | bytes 1572872 | tf_op jit(solution)/shard_map/ppermute | solution.py:198
  30.9 27.8 %collective-permute-start = (bf16[8,32,512]{2,0,1:T(8,128)(2,1)}, bf16[8,32,512]{2,0,1:T(8,128)(2,1)S(1)}, u32[]{:S(2)}, u32[]{:S(2)}) collective-permute-start(bf16[8,32,512]{2,0,1:T(8,128)(2,1)} %bitcast.129), channel_id=1, source_target_pairs={{0,4},{4,8},{8,12},{12,16},{16,20},{20,24},{24,28},{28,0},{1,5},{5... | collective-permute-start | bytes 786440 | tf_op jit(solution)/shard_map/ppermute | solution.py:168
  47.6 43.9 %collective-permute-start.2 = (bf16[8,32,512]{2,0,1:T(8,128)(2,1)}, bf16[8,32,512]{2,0,1:T(8,128)(2,1)S(1)}, u32[]{:S(2)}, u32[]{:S(2)}) collective-permute-start(bf16[8,32,512]{2,0,1:T(8,128)(2,1)} %bitcast.127), channel_id=1, source_target_pairs={{0,12},{4,16},{8,20},{12,24},{16,28},{20,0},{24,4},{28,8},{1,13},{... | collective-permute-start | bytes 786440 | tf_op jit(solution)/shard_map/ppermute | solution.py:168
  58.6 44.9 %collective-permute-start.8 = (bf16[512,512]{1,0:T(8,128)(2,1)}, bf16[512,512]{1,0:T(8,128)(2,1)}, u32[]{:S(2)}, u32[]{:S(2)}) collective-permute-start(bf16[512,512]{1,0:T(8,128)(2,1)} %param.19), channel_id=1, source_target_pairs={{0,2},{1,3},{2,0},{3,1},{4,6},{5,7},{6,4},{7,5},{8,10},{9,11},{10,... | collective-permute-start | bytes 1572872 | tf_op jit(solution)/shard_map/ppermute | solution.py:198
  60.1 60.4 %collective-permute-start.10 = (bf16[8,32,512]{2,0,1:T(8,128)(2,1)}, bf16[8,32,512]{2,0,1:T(8,128)(2,1)}, u32[]{:S(2)}, u32[]{:S(2)}) collective-permute-start(bf16[8,32,512]{2,0,1:T(8,128)(2,1)} %bitcast.19), channel_id=1, source_target_pairs={{0,4},{4,8},{8,12},{12,16},{16,20},{20,24},{24,28},{28,0},{1,5},{5... | collective-permute-start | bytes 786440 | tf_op jit(solution)/shard_map/ppermute | solution.py:168
  91.6 32.8 %collective-permute-start.11 = (bf16[8,32,512]{2,0,1:T(8,128)(2,1)}, bf16[8,32,512]{2,0,1:T(8,128)(2,1)}, u32[]{:S(2)}, u32[]{:S(2)}) collective-permute-start(bf16[8,32,512]{2,0,1:T(8,128)(2,1)} %bitcast.20), channel_id=1, source_target_pairs={{0,8},{4,12},{8,16},{12,20},{16,24},{20,28},{24,0},{28,4},{1,9},{5... | collective-permute-start | bytes 786440 | tf_op jit(solution)/shard_map/ppermute | solution.py:168
  100.0 26.9 %collective-permute-start.12 = (bf16[8,32,512]{2,0,1:T(8,128)(2,1)}, bf16[8,32,512]{2,0,1:T(8,128)(2,1)S(1)}, u32[]{:S(2)}, u32[]{:S(2)}) collective-permute-start(bf16[8,32,512]{2,0,1:T(8,128)(2,1)} %bitcast.126), channel_id=1, source_target_pairs={{0,12},{4,16},{8,20},{12,24},{16,28},{20,0},{24,4},{28,8},{1,13},{... | collective-permute-start | bytes 786440 | tf_op jit(solution)/shard_map/ppermute | solution.py:168
  101.9 25.4 %collective-permute-start.13 = (bf16[8,32,512]{2,0,1:T(8,128)(2,1)}, bf16[8,32,512]{2,0,1:T(8,128)(2,1)S(1)}, u32[]{:S(2)}, u32[]{:S(2)}) collective-permute-start(bf16[8,32,512]{2,0,1:T(8,128)(2,1)} %bitcast.22), channel_id=1, source_target_pairs={{0,16},{4,20},{8,24},{12,28},{16,0},{20,4},{24,8},{28,12},{1,17},{... | collective-permute-start | bytes 786440 | tf_op jit(solution)/shard_map/ppermute | solution.py:168
  103.6 23.7 %collective-permute-start.14 = (bf16[8,32,512]{2,0,1:T(8,128)(2,1)}, bf16[8,32,512]{2,0,1:T(8,128)(2,1)}, u32[]{:S(2)}, u32[]{:S(2)}) collective-permute-start(bf16[8,32,512]{2,0,1:T(8,128)(2,1)} %bitcast.23), channel_id=1, source_target_pairs={{0,20},{4,24},{8,28},{12,0},{16,4},{20,8},{24,12},{28,16},{1,21},{... | collective-permute-start | bytes 786440 | tf_op jit(solution)/shard_map/ppermute | solution.py:168
  139.9 43.8 %collective-permute-start.20 = (bf16[8,32,512]{2,0,1:T(8,128)(2,1)}, bf16[8,32,512]{2,0,1:T(8,128)(2,1)}, u32[]{:S(2)}, u32[]{:S(2)}) collective-permute-start(bf16[8,32,512]{2,0,1:T(8,128)(2,1)} %bitcast.34), channel_id=1, source_target_pairs={{0,28},{4,0},{8,4},{12,8},{16,12},{20,16},{24,20},{28,24},{1,29},{... | collective-permute-start | bytes 786440 | tf_op jit(solution)/shard_map/ppermute | solution.py:168
  145.2 40.1 %collective-permute-start.21 = (bf16[8,32,512]{2,0,1:T(8,128)(2,1)}, bf16[8,32,512]{2,0,1:T(8,128)(2,1)}, u32[]{:S(2)}, u32[]{:S(2)}) collective-permute-start(bf16[8,32,512]{2,0,1:T(8,128)(2,1)} %bitcast.36), channel_id=1, source_target_pairs={{0,24},{4,28},{8,0},{12,4},{16,8},{20,12},{24,16},{28,20},{1,25},{... | collective-permute-start | bytes 786440 | tf_op jit(solution)/shard_map/ppermute | solution.py:168
  145.2 40.7 %collective-permute-start.22 = (bf16[8,32,512]{2,0,1:T(8,128)(2,1)}, bf16[8,32,512]{2,0,1:T(8,128)(2,1)}, u32[]{:S(2)}, u32[]{:S(2)}) collective-permute-start(bf16[8,32,512]{2,0,1:T(8,128)(2,1)} %bitcast.38), channel_id=1, source_target_pairs={{0,20},{4,24},{8,28},{12,0},{16,4},{20,8},{24,12},{28,16},{1,21},{... | collective-permute-start | bytes 786440 | tf_op jit(solution)/shard_map/ppermute | solution.py:168
  148.4 46.8 %collective-permute-start.23 = (bf16[8,32,512]{2,0,1:T(8,128)(2,1)}, bf16[8,32,512]{2,0,1:T(8,128)(2,1)}, u32[]{:S(2)}, u32[]{:S(2)}) collective-permute-start(bf16[8,32,512]{2,0,1:T(8,128)(2,1)} %bitcast.40), channel_id=1, source_target_pairs={{0,16},{4,20},{8,24},{12,28},{16,0},{20,4},{24,8},{28,12},{1,17},{... | collective-permute-start | bytes 786440 | tf_op jit(solution)/shard_map/ppermute | solution.py:168
  149.8 45.4 %collective-permute-start.24 = (bf16[8,32,512]{2,0,1:T(8,128)(2,1)}, bf16[8,32,512]{2,0,1:T(8,128)(2,1)}, u32[]{:S(2)}, u32[]{:S(2)}) collective-permute-start(bf16[8,32,512]{2,0,1:T(8,128)(2,1)} %bitcast.42), channel_id=1, source_target_pairs={{0,12},{4,16},{8,20},{12,24},{16,28},{20,0},{24,4},{28,8},{1,13},{... | collective-permute-start | bytes 786440 | tf_op jit(solution)/shard_map/ppermute | solution.py:168
  185.9 31.3 %collective-permute-start.27 = (bf16[8,32,512]{2,0,1:T(8,128)(2,1)S(1)}, bf16[8,32,512]{2,0,1:T(8,128)(2,1)S(1)}, u32[]{:S(2)}, u32[]{:S(2)}) collective-permute-start(bf16[8,32,512]{2,0,1:T(8,128)(2,1)S(1)} %bitcast.138), channel_id=1, source_target_pairs={{0,28},{4,0},{8,4},{12,8},{16,12},{20,16},{24,20},{28,24},{1,29},{... | collective-permute-start | bytes 786440 | tf_op jit(solution)/shard_map/ppermute | solution.py:168
  195.2 23.6 %collective-permute-start.29 = (bf16[8,32,512]{2,0,1:T(8,128)(2,1)S(1)}, bf16[8,32,512]{2,0,1:T(8,128)(2,1)S(1)}, u32[]{:S(2)}, u32[]{:S(2)}) collective-permute-start(bf16[8,32,512]{2,0,1:T(8,128)(2,1)S(1)} %bitcast.136), channel_id=1, source_target_pairs={{0,20},{4,24},{8,28},{12,0},{16,4},{20,8},{24,12},{28,16},{1,21},{... | collective-permute-start | bytes 786440 | tf_op jit(solution)/shard_map/ppermute | solution.py:168
  195.2 38.2 %collective-permute-start.30 = (bf16[8,32,512]{2,0,1:T(8,128)(2,1)S(1)}, bf16[8,32,512]{2,0,1:T(8,128)(2,1)S(1)}, u32[]{:S(2)}, u32[]{:S(2)}) collective-permute-start(bf16[8,32,512]{2,0,1:T(8,128)(2,1)S(1)} %bitcast.135), channel_id=1, source_target_pairs={{0,16},{4,20},{8,24},{12,28},{16,0},{20,4},{24,8},{28,12},{1,17},{... | collective-permute-start | bytes 786440 | tf_op jit(solution)/shard_map/ppermute | solution.py:168
  200.0 33.5 %collective-permute-start.31 = (bf16[8,32,512]{2,0,1:T(8,128)(2,1)S(1)}, bf16[8,32,512]{2,0,1:T(8,128)(2,1)S(1)}, u32[]{:S(2)}, u32[]{:S(2)}) collective-permute-start(bf16[8,32,512]{2,0,1:T(8,128)(2,1)S(1)} %bitcast.134), channel_id=1, source_target_pairs={{0,12},{4,16},{8,20},{12,24},{16,28},{20,0},{24,4},{28,8},{1,13},{... | collective-permute-start | bytes 786440 | tf_op jit(solution)/shard_map/ppermute | solution.py:168
  217.2 32.1 %collective-permute-start.17 = (f32[512,512]{1,0:T(8,128)S(1)}, f32[512,512]{1,0:T(8,128)S(1)}, u32[]{:S(2)}, u32[]{:S(2)}) collective-permute-start(f32[512,512]{1,0:T(8,128)S(1)} %fusion.15), channel_id=1, source_target_pairs={{0,1},{1,2},{2,3},{3,0},{4,5},{5,6},{6,7},{7,4},{8,9},{9,10},{10,1... | collective-permute-start | bytes 3145736 | tf_op jit(solution)/shard_map/ppermute | solution.py:246
  217.2 32.0 %collective-permute-start.18 = (f32[512,512]{1,0:T(8,128)S(1)}, f32[512,512]{1,0:T(8,128)S(1)}, u32[]{:S(2)}, u32[]{:S(2)}) collective-permute-start(f32[512,512]{1,0:T(8,128)S(1)} %fusion.13), channel_id=1, source_target_pairs={{0,2},{1,3},{2,0},{3,1},{4,6},{5,7},{6,4},{7,5},{8,10},{9,11},{10,... | collective-permute-start | bytes 3145736 | tf_op jit(solution)/shard_map/ppermute | solution.py:246
  218.8 45.4 %collective-permute-start.19 = (f32[512,512]{1,0:T(8,128)S(1)}, f32[512,512]{1,0:T(8,128)S(1)}, u32[]{:S(2)}, u32[]{:S(2)}) collective-permute-start(f32[512,512]{1,0:T(8,128)S(1)} %fusion.11), channel_id=1, source_target_pairs={{0,3},{1,0},{2,1},{3,2},{4,7},{5,4},{6,5},{7,6},{8,11},{9,8},{10,9... | collective-permute-start | bytes 3145736 | tf_op jit(solution)/shard_map/ppermute | solution.py:246
  (47 other events, 613.5 us)
